TPU v7x, 32 devices: a whole 2x2x4 slice. The times are simulated.
32 devices in a mesh: parts: 2 (over x), chan: 16 (over z, y, core).
Axes of the slice: x: 2, y: 2, z: 4, core: 2. Of those that a mesh axis runs over, the one named last changes fastest.
Arguments:
- spectra: bfloat16 [1024, 8, 1024], P(('parts', 'chan')), parts along dimension 0, may hold values from -8 to 8
- source_blocks: int32 [4, 2], P('parts'), parts along dimension 0, may hold values from 0 to 15
- window_valid: int32 [16], P('parts'), parts along dimension 0, may hold values 0 or 1
Outputs:
- correlations: bfloat16 [2, 2, 32, 1024, 512], P(None, None, None, ('parts', 'chan')), parts along dimension 3
There are 2 independent parts, one for each index of `parts`. A program takes and returns all parts, laid end to end along the dimension named above; each array names one. Nothing has to cross between parts.
All inputs are finite; a program needn't handle non-finite values. Where the computation divides by a largest or mean magnitude, that divisor is 1e-20 or more.
Results may differ from a plain program's by a relative error of at most 0.0045.
Values may be sent and summed in bfloat16 or wider, within the bound.
No kernel may reach another device: no remote copies, remote signals or barrier semaphores. Data moves between devices by JAX's collectives and lax.ppermute only.
A program may use at most 192 MiB of HBM per device.

v0:
```python
import math

import jax
import jax.numpy as jnp
from jax import lax
from jax.sharding import PartitionSpec as P

SOURCE = 32
LAGS = 512


def from_root(block, axis, source):
    block = jnp.where(lax.axis_index(axis) == source, block, jnp.zeros_like(block))
    return lax.psum(block, axis)


def build_table(bins, lags):
    freq = jnp.arange(bins, dtype=jnp.int32)[:, None]
    shifted = jnp.arange(lags, dtype=jnp.int32)[None, :] - lags // 2
    phase = jnp.remainder(freq * shifted, 2 * bins).astype(jnp.float32)
    theta = phase * (2.0 * math.pi / (2 * bins))
    weight = jnp.where(freq == 0, 1.0, 2.0).astype(jnp.float32) / (2 * bins)
    return jnp.concatenate([weight * jnp.cos(theta), -weight * jnp.sin(theta)], axis=0).astype(
        jnp.bfloat16
    )


def shards(spectra, source_blocks, window_valid):
    receivers, windows, width = spectra.shape
    bins = width // 2
    per_device = receivers // SOURCE
    lag_table = build_table(bins, LAGS)
    window_mask = window_valid.astype(jnp.bfloat16)[None, :, None]
    real_rcv = spectra[..., :bins]
    imag_rcv = spectra[..., bins:]
    num_steps = source_blocks.shape[0]
    traces_all = []
    for step in range(num_steps):
        for slot in range(2):
            block_index = source_blocks[step, slot]
            source = from_root(spectra, "chan", block_index // per_device)
            masked = source * window_mask
            stacked_src = jnp.concatenate([masked[..., :bins], masked[..., bins:]], axis=0)
            with_real = jnp.einsum(
                "swf,rwf->srf", stacked_src, real_rcv, preferred_element_type=jnp.float32
            )
            with_imag = jnp.einsum(
                "swf,rwf->srf", stacked_src, imag_rcv, preferred_element_type=jnp.float32
            )
            real_part = with_real[:SOURCE] + with_imag[SOURCE:]
            imag_part = with_imag[:SOURCE] - with_real[SOURCE:]
            cross = jnp.concatenate([real_part, imag_part], axis=2).astype(jnp.bfloat16)
            flat = cross.reshape(SOURCE * receivers, width)
            traces = jnp.dot(flat, lag_table, preferred_element_type=jnp.float32).reshape(
                SOURCE, receivers, LAGS
            )
            traces, local_peak = (traces, jnp.max(jnp.abs(traces), axis=(1, 2)))
            global_peak = lax.pmax(local_peak, "chan")
            traces_all.append((traces / (global_peak[:, None, None] + 1e-06)).astype(jnp.bfloat16))
    stacked = jnp.stack(traces_all, axis=0)
    return stacked.reshape(num_steps, 2, SOURCE, receivers, LAGS)


def solution(mesh):
    placed = (P(("parts", "chan"), None, None), P("parts", None), P("parts"))
    return jax.shard_map(
        shards,
        mesh=mesh,
        in_specs=placed,
        out_specs=P(None, None, None, ("parts", "chan"), None),
        check_vma=False,
    )
```

profile of v0, /device:TPU:0, one launch (start us, length us, event | category | flops | bytes accessed | tf_op | source)
XLA Modules:
  0.0 358.3 jit_solution(7590580880067634399)
XLA Ops:
  6.5 0.0 all-reduce.4.cloned.1.call-start
  6.5 1.4 fusion.67
  10.5 2.7 copy.28
  13.2 3.5 broadcast_select_fusion.3
  16.7 0.0 copy-start.8
  16.7 0.0 all-reduce.4.cloned.1.call-update
  16.7 0.6 copy-done.8
  17.3 4.4 %multiply_convert_fusion.1 = (bf16[512,512]{1,0:T(8,128)(2,1)S(1)}, bf16[512,512]{1,0:T(8,128)(2,1)S(1)}) fusion(s32[512]{0:T(512)S(1)} %iota_add_fusion, f32[512]{0:T(512)S(1)} %get-tuple-element.51, f32[512]{0:T(512)S(1)} %get-tuple-element.52), kind=kLoop, calls=%fused_computation.57 | loop fusion | flops 4718592 | bytes 1054720 | tf_op jit(solution)/shard_map/convert.6
  21.8 167.9 %all-reduce.4.cloned.1.call-done = (bf16[32,8,1024]{0,1,2:T(8,128)(2,1)}, bf16[32,8,1024]{0,1,2:T(8,128)(2,1)}, bf16[32,8,1024]{0,1,2:T(8,128)(2,1)}, bf16[32,8,1024]{0,1,2:T(8,128)(2,1)}) async-done(((bf16[32,8,1024]{0,1,2:T(8,128)(2,1)}, bf16[32,8,1024]{0,1,2:T(8,128)(2,1)}, bf16[32,8,1024]{0,1,2:T(8,128)(2,1)}, bf16[32,8,1024]{0,1,2:T(8,128)(2,1)}), (bf16[32,8,1024]{0,1,2:T(8,128)(2,1)}, ...) | async-done | bytes 2097168 | tf_op jit(solution)/shard_map/psum | solution.py:14
  189.7 4.1 %broadcast_multiply_fusion.3 = (bf16[32,8,1024]{0,1,2:T(8,128)(2,1)S(1)}, bf16[32,8,1024]{0,1,2:T(8,128)(2,1)S(1)}, bf16[32,8,1024]{0,1,2:T(8,128)(2,1)S(1)}, bf16[32,8,1024]{0,1,2:T(8,128)(2,1)S(1)}) fusion(bf16[32,8,1024]{0,1,2:T(8,128)(2,1)} %get-tuple-element.12, bf16[8]{0:T(256)(128)(2,1)S(1)} %convert_element_type.33, ...), kind=kLoop, calls=%fused_computation.63 | loop fusion | flops 1048576 | bytes 4194320 | tf_op jit(solution)/shard_map/mul | solution.py:42
  193.8 0.3 fusion.65
  194.1 4.3 %fusion.36 = f32[512,64,32]{1,2,0:T(8,128)} fusion(bf16[32,8,1024]{0,1,2:T(8,128)(2,1)S(1)} %copy.28, bf16[32,8,512]{0,1,2:T(8,128)(2,1)S(1)} %get-tuple-element.26, bf16[32,8,512]{0,1,2:T(8,128)(2,1)S(1)} %get-tuple-element.25), kind=kOutput, calls=%fused_computation.71 | convolution fusion | flops 17825792 | bytes 7340032 | tf_op jit(solution)/shard_map/swf,rwf->srf/dot_general | solution.py:47
  198.4 4.3 %fusion.44 = f32[512,64,32]{1,2,0:T(8,128)} fusion(bf16[32,8,1024]{0,1,2:T(8,128)(2,1)S(1)} %copy.28, bf16[32,8,512]{0,1,2:T(8,128)(2,1)S(1)} %get-tuple-element.26, bf16[32,8,512]{0,1,2:T(8,128)(2,1)S(1)} %get-tuple-element.25), kind=kOutput, calls=%fused_computation.79 | convolution fusion | flops 17825792 | bytes 7340032 | tf_op jit(solution)/shard_map/swf,rwf->srf/dot_general | solution.py:44
  202.6 4.3 %fusion.34 = f32[512,64,32]{1,2,0:T(8,128)} fusion(bf16[32,8,1024]{0,1,2:T(8,128)(2,1)S(1)} %copy.28, bf16[32,8,512]{0,1,2:T(8,128)(2,1)S(1)} %get-tuple-element.55, bf16[32,8,512]{0,1,2:T(8,128)(2,1)S(1)} %get-tuple-element.56), kind=kOutput, calls=%fused_computation.69 | convolution fusion | flops 17825792 | bytes 7340032 | tf_op jit(solution)/shard_map/swf,rwf->srf/dot_general | solution.py:47
  206.9 4.3 %fusion.42 = f32[512,64,32]{1,2,0:T(8,128)} fusion(bf16[32,8,1024]{0,1,2:T(8,128)(2,1)S(1)} %copy.28, bf16[32,8,512]{0,1,2:T(8,128)(2,1)S(1)} %get-tuple-element.55, bf16[32,8,512]{0,1,2:T(8,128)(2,1)S(1)} %get-tuple-element.56), kind=kOutput, calls=%fused_computation.77 | convolution fusion | flops 17825792 | bytes 7340032 | tf_op jit(solution)/shard_map/swf,rwf->srf/dot_general | solution.py:44
  211.2 0.3 fusion.63
  211.4 4.3 %fusion.40 = f32[512,64,32]{1,2,0:T(8,128)} fusion(bf16[32,8,1024]{0,1,2:T(8,128)(2,1)S(1)} %copy.28, bf16[32,8,512]{0,1,2:T(8,128)(2,1)S(1)} %get-tuple-element.22, bf16[32,8,512]{0,1,2:T(8,128)(2,1)S(1)} %get-tuple-element.21), kind=kOutput, calls=%fused_computation.75 | convolution fusion | flops 17825792 | bytes 7340032 | tf_op jit(solution)/shard_map/swf,rwf->srf/dot_general | solution.py:47
  215.8 4.3 %fusion.48 = f32[512,64,32]{1,2,0:T(8,128)} fusion(bf16[32,8,1024]{0,1,2:T(8,128)(2,1)S(1)} %copy.28, bf16[32,8,512]{0,1,2:T(8,128)(2,1)S(1)} %get-tuple-element.22, bf16[32,8,512]{0,1,2:T(8,128)(2,1)S(1)} %get-tuple-element.21), kind=kOutput, calls=%fused_computation.83 | convolution fusion | flops 17825792 | bytes 7340032 | tf_op jit(solution)/shard_map/swf,rwf->srf/dot_general | solution.py:44
  220.0 4.3 %fusion.38 = f32[512,64,32]{1,2,0:T(8,128)} fusion(bf16[32,8,1024]{0,1,2:T(8,128)(2,1)S(1)} %copy.28, bf16[32,8,512]{0,1,2:T(8,128)(2,1)S(1)} %get-tuple-element.53, bf16[32,8,512]{0,1,2:T(8,128)(2,1)S(1)} %get-tuple-element.54), kind=kOutput, calls=%fused_computation.73 | convolution fusion | flops 17825792 | bytes 7340032 | tf_op jit(solution)/shard_map/swf,rwf->srf/dot_general | solution.py:47
  224.3 4.3 %fusion.46 = f32[512,64,32]{1,2,0:T(8,128)} fusion(bf16[32,8,1024]{0,1,2:T(8,128)(2,1)S(1)} %copy.28, bf16[32,8,512]{0,1,2:T(8,128)(2,1)S(1)} %get-tuple-element.53, bf16[32,8,512]{0,1,2:T(8,128)(2,1)S(1)} %get-tuple-element.54), kind=kOutput, calls=%fused_computation.81 | convolution fusion | flops 17825792 | bytes 7340032 | tf_op jit(solution)/shard_map/swf,rwf->srf/dot_general | solution.py:44
  228.6 7.7 %copy.38 = f32[512,64,32]{0,2,1:T(8,128)} copy(f32[512,64,32]{1,2,0:T(8,128)} %fusion.36) | data formatting | bytes 8388608 | tf_op jit(solution)/shard_map/swf,rwf->srf/dot_general | solution.py:47
  236.3 7.7 %copy.37 = f32[512,64,32]{0,2,1:T(8,128)} copy(f32[512,64,32]{1,2,0:T(8,128)} %fusion.44) | data formatting | bytes 8388608 | tf_op jit(solution)/shard_map/swf,rwf->srf/dot_general | solution.py:44
  244.1 7.6 %copy.41 = f32[512,64,32]{0,2,1:T(8,128)} copy(f32[512,64,32]{1,2,0:T(8,128)} %fusion.34) | data formatting | bytes 8388608 | tf_op jit(solution)/shard_map/swf,rwf->srf/dot_general | solution.py:47
  251.7 7.8 %copy.40 = f32[512,64,32]{0,2,1:T(8,128)} copy(f32[512,64,32]{1,2,0:T(8,128)} %fusion.42) | data formatting | bytes 8388608 | tf_op jit(solution)/shard_map/swf,rwf->srf/dot_general | solution.py:44
  259.5 7.8 %copy.32 = f32[512,64,32]{0,2,1:T(8,128)} copy(f32[512,64,32]{1,2,0:T(8,128)} %fusion.40) | data formatting | bytes 8388608 | tf_op jit(solution)/shard_map/swf,rwf->srf/dot_general | solution.py:47
  267.2 7.7 %copy.30 = f32[512,64,32]{0,2,1:T(8,128)} copy(f32[512,64,32]{1,2,0:T(8,128)} %fusion.48) | data formatting | bytes 8388608 | tf_op jit(solution)/shard_map/swf,rwf->srf/dot_general | solution.py:44
  275.0 7.7 %copy.35 = f32[512,64,32]{0,2,1:T(8,128)} copy(f32[512,64,32]{1,2,0:T(8,128)} %fusion.38) | data formatting | bytes 8388608 | tf_op jit(solution)/shard_map/swf,rwf->srf/dot_general | solution.py:47
  282.7 7.8 %copy.34 = f32[512,64,32]{0,2,1:T(8,128)} copy(f32[512,64,32]{1,2,0:T(8,128)} %fusion.46) | data formatting | bytes 8388608 | tf_op jit(solution)/shard_map/swf,rwf->srf/dot_general | solution.py:44
  290.4 0.0 copy-start.4
  290.4 0.0 copy-start.5
  290.4 4.4 %fusion.3 = (bf16[32,32,512]{2,1,0:T(8,128)(2,1)S(1)}, bf16[32,32,512]{2,1,0:T(8,128)(2,1)S(1)}) fusion(f32[64,32,512]{2,1,0:T(8,128)} %bitcast.40, f32[64,32,512]{2,1,0:T(8,128)} %bitcast.42), kind=kLoop, calls=%fused_computation.8 | loop fusion | flops 2097152 | bytes 10485760 | tf_op jit(solution)/shard_map/convert.2
  294.9 0.2 copy-done.4
  295.1 1.3 copy-done.5
  296.4 1.3 fusion.1
  297.6 1.4 abs_reduce_fusion.1
  299.0 0.0 copy-start.2
  299.0 0.0 copy-start.3
  299.0 2.6 abs_reduce_fusion
  301.6 0.0 copy-done.2
  301.6 1.6 copy-done.3
  303.2 1.3 fusion.7
  304.5 0.0 copy-start
  304.5 0.0 copy-start.1
  304.5 2.6 abs_reduce_fusion.3
  307.1 0.0 copy-done
  307.1 1.6 copy-done.1
  308.7 1.3 fusion.5
  310.0 2.6 abs_reduce_fusion.2
  312.6 32.0 %all-reduce = (f32[32]{0:T(128)S(1)}, f32[32]{0:T(128)S(1)}, f32[32]{0:T(128)S(1)}, f32[32]{0:T(128)S(1)}) all-reduce(f32[32]{0:T(128)S(1)} %get-tuple-element.43, f32[32]{0:T(128)S(1)} %get-tuple-element.45, f32[32]{0:T(128)S(1)} %get-tuple-element.47, f32[32]{0:T(128)S(1)} %get-tuple-element.49), channel_id=1, replica_groups=mesh['parts'=2,'chan'=16] {'chan'}, use_global_device_ids=true, to_apply=%region_11.12 | all-reduce | flops 128 | bytes 1024 | tf_op jit(solution)/shard_map/pmax | solution.py:58
  344.6 1.9 fusion.33
  346.5 0.0 copy-start.7
  346.5 0.3 fusion.32
  346.9 0.0 copy-start.6
  346.9 1.2 copy-done.7
  348.1 0.3 fusion.31
  348.5 0.4 copy-done.6
  348.8 0.3 fusion.30
  349.2 2.3 pad_maximum_fusion
  (7 shorter events, 0.0 us)
Async XLA Ops:
  6.5 183.2 %all-reduce.4.cloned.1.call-start = ((), (), s32[]{:S(2)}) async-start(), calls=%async_computation | async-start | bytes 16777216 | tf_op jit(solution)/shard_map/psum | solution.py:14
  16.7 0.7 copy-start.8
  290.4 4.7 %copy-start.4 = (f32[512,64,32]{0,2,1:T(8,128)S(1)}, f32[512,64,32]{0,2,1:T(8,128)}, u32[]{:S(2)}) copy-start(f32[512,64,32]{0,2,1:T(8,128)} %copy.41) | copy-start | bytes 12582916
  290.4 5.9 %copy-start.5 = (f32[512,64,32]{0,2,1:T(8,128)S(1)}, f32[512,64,32]{0,2,1:T(8,128)}, u32[]{:S(2)}) copy-start(f32[512,64,32]{0,2,1:T(8,128)} %copy.40) | copy-start | bytes 12582916
  299.0 2.6 copy-start.2
  299.0 4.2 %copy-start.3 = (f32[512,64,32]{0,2,1:T(8,128)S(1)}, f32[512,64,32]{0,2,1:T(8,128)}, u32[]{:S(2)}) copy-start(f32[512,64,32]{0,2,1:T(8,128)} %copy.30) | copy-start | bytes 12582916
  304.5 2.6 copy-start
  304.5 4.2 %copy-start.1 = (f32[512,64,32]{0,2,1:T(8,128)S(1)}, f32[512,64,32]{0,2,1:T(8,128)}, u32[]{:S(2)}) copy-start(f32[512,64,32]{0,2,1:T(8,128)} %copy.34) | copy-start | bytes 12582916
  346.5 1.6 copy-start.7
  346.9 2.0 copy-start.6
Sparse Core Ops, SparseCore 0:
  16.8 172.8 all-reduce.3
where the time goes:
time: 359 us; the launch traced here: 358 us
  waiting for transfers between devices  168 us (47%)
  local copies, waits for them, and re-layouts  73.5 us (20%)
  matrix products  43.4 us (12%)
  blocking collectives  32 us (9%)
  other arithmetic  25.4 us (7%)
  between operations  16 us (4%)
    psum x1, waiting for transfers between devices, from_root(): return lax.psum(block, axis)  168 us
    pmax x1, blocking collectives, shards(): global_peak = lax.pmax(local_peak, 'chan')  32 us
    dot_general x4, local copies, waits for them, and re-layouts, shards(): jnp.einsum('swf,rwf->srf', stacked_src, real_rcv, preferred_element_type=...  31 us
    dot_general x4, local copies, waits for them, and re-layouts, shards(): jnp.einsum('swf,rwf->srf', stacked_src, imag_rcv, preferred_element_type=...  30.8 us
    dot_general x4, matrix products, shards(): jnp.einsum('swf,rwf->srf', stacked_src, imag_rcv, preferred_element_type=...  17.2 us
    dot_general x4, matrix products, shards(): jnp.einsum('swf,rwf->srf', stacked_src, real_rcv, preferred_element_type=...  17 us
    another operation x5, other arithmetic  12.6 us
    unnamed x19, local copies, waits for them, and re-layouts  9.71 us
  transfers between devices with their start and end apart: 1, of which 1 were waited for; matrix products, arithmetic and copies ran while one was open for 1% of the time, Pallas kernels for 0%

commit v1 on v0

v1 whole, which is shorter than its diff:
```python
import math

import jax
import jax.numpy as jnp
from jax import lax
from jax.sharding import PartitionSpec as P

SOURCE = 32
LAGS = 512


def build_table(bins, lags):
    freq = jnp.arange(bins, dtype=jnp.int32)[:, None]
    shifted = jnp.arange(lags, dtype=jnp.int32)[None, :] - lags // 2
    phase = jnp.remainder(freq * shifted, 2 * bins).astype(jnp.float32)
    theta = phase * (2.0 * math.pi / (2 * bins))
    weight = jnp.where(freq == 0, 1.0, 2.0).astype(jnp.float32) / (2 * bins)
    return jnp.concatenate([weight * jnp.cos(theta), -weight * jnp.sin(theta)], axis=0).astype(
        jnp.bfloat16
    )


def plane_size(mesh):
    devs = list(mesh.devices[0])
    n = len(devs)
    best = 1
    for axis in range(3):
        first = next((i for i, d in enumerate(devs) if d.coords[axis] != devs[0].coords[axis]), None)
        if first is not None and first > best:
            best = first
    if best >= n or n % best:
        best = 1
    return best


def pairs_of(n, fn):
    out = []
    for i in range(n):
        j = fn(i)
        if j is not None:
            out.append((i, j))
    return out


def make_shards(n, qc):
    zc = n // qc
    plane_bits = [1 << b for b in reversed(range(qc.bit_length() - 1))]

    def shards(spectra, source_blocks, window_valid):
        receivers, windows, width = spectra.shape
        bins = width // 2
        me = lax.axis_index("chan")
        z = me // qc
        q = me % qc
        blocks = source_blocks.reshape(-1)
        nb = blocks.shape[0]
        zk = blocks // qc
        qk = blocks % qc
        piece = SOURCE // qc

        own = spectra.reshape(qc, piece, windows, width)
        by_off = [lax.dynamic_index_in_dim(own, q, 0, keepdims=False)]
        for d in range(1, qc):
            send = lax.dynamic_index_in_dim(own, q ^ d, 0, keepdims=False)
            by_off.append(
                lax.ppermute(send, "chan", pairs_of(n, lambda i, d=d: (i // qc) * qc + ((i % qc) ^ d)))
            )
        by_off = jnp.stack(by_off)

        here = zk == z
        sel = jnp.take(by_off, qk ^ q, axis=0)
        payload = jnp.where(here[:, None, None, None], sel, jnp.zeros_like(sel))

        up_pairs = pairs_of(n, lambda i: i + qc if i // qc < zc - 1 else None)
        down_pairs = pairs_of(n, lambda i: i - qc if i // qc > 0 else None)
        mask = here[:, None, None, None]
        cur_up, cur_down = payload, payload
        rec_up, rec_down = payload, payload
        for r in range(zc - 1):
            rec_up = lax.ppermute(cur_up, "chan", up_pairs)
            rec_down = lax.ppermute(cur_down, "chan", down_pairs)
            if r < zc - 2:
                cur_up = jnp.where(mask, payload, rec_up)
                cur_down = jnp.where(mask, payload, rec_down)
        below = (z > zk)[:, None, None, None]
        mine = jnp.where(mask, payload, jnp.where(below, rec_up, rec_down))

        offs = [0]
        held = [mine]
        for b in plane_bits:
            got = lax.ppermute(
                jnp.stack(held), "chan", pairs_of(n, lambda i, b=b: (i // qc) * qc + ((i % qc) ^ b))
            )
            offs = offs + [o ^ b for o in offs]
            held = held + [got[i] for i in range(got.shape[0])]
        stack = jnp.stack(held)
        inv = [0] * qc
        for e, o in enumerate(offs):
            inv[o] = e
        inv = jnp.array(inv, jnp.int32)
        order = jnp.take(inv, jnp.arange(qc, dtype=jnp.int32) ^ q)
        full = jnp.take(stack, order, axis=0)
        src_all = jnp.transpose(full, (1, 0, 2, 3, 4)).reshape(nb, SOURCE, windows, width)

        lag_table = build_table(bins, LAGS)
        window_mask = window_valid.astype(jnp.bfloat16)[None, None, :, None]
        src_all = src_all * window_mask
        rr = spectra[..., :bins].astype(jnp.float32)[None, None]
        ri = spectra[..., bins:].astype(jnp.float32)[None, None]
        traces_all = []
        peaks = []
        for k in range(nb):
            src = src_all[k]
            sr = src[..., :bins].astype(jnp.float32)[:, None]
            si = src[..., bins:].astype(jnp.float32)[:, None]
            real_part = jnp.sum(sr * rr[0] + si * ri[0], axis=2)
            imag_part = jnp.sum(sr * ri[0] - si * rr[0], axis=2)
            cross = jnp.concatenate([real_part, imag_part], axis=2).astype(jnp.bfloat16)
            flat = cross.reshape(SOURCE * receivers, width)
            traces = jnp.dot(flat, lag_table, preferred_element_type=jnp.float32).reshape(
                SOURCE, receivers, LAGS
            )
            traces_all.append(traces)
            peaks.append(jnp.max(jnp.abs(traces), axis=(1, 2)))
        peak = jnp.stack(peaks)
        d = 1
        while d < n:
            peak = jnp.maximum(peak, lax.ppermute(peak, "chan", pairs_of(n, lambda i, d=d: i ^ d)))
            d *= 2
        out = [
            (traces_all[k] / (peak[k][:, None, None] + 1e-06)).astype(jnp.bfloat16) for k in range(nb)
        ]
        stacked = jnp.stack(out, axis=0)
        return stacked.reshape(source_blocks.shape[0], source_blocks.shape[1], SOURCE, receivers, LAGS)

    return shards


def solution(mesh):
    n = mesh.shape["chan"]
    qc = plane_size(mesh)
    placed = (P(("parts", "chan"), None, None), P("parts", None), P("parts"))
    return jax.shard_map(
        make_shards(n, qc),
        mesh=mesh,
        in_specs=placed,
        out_specs=P(None, None, None, ("parts", "chan"), None),
        check_vma=False,
    )
```

time: 359 us -> 163 us (0.45)
  waiting for transfers between devices: 168 us -> 63 us
  local copies, waits for them, and re-layouts: 73.5 us -> 7.22 us
  other arithmetic: 25.4 us -> 63.6 us
  matrix products: 43.4 us -> 5.51 us
  blocking collectives: 32 us -> 0 us
  starting transfers between devices: 0.01 us -> 23 us
  between operations: 16 us -> 0.34 us
    psum x1 -> x0, waiting for transfers between devices: 168 us -> none  [from_root(): return lax.psum(block, axis)]
    ppermute x0 -> x15, waiting for transfers between devices: none -> 63 us  [the longest x3 27.6 us: shards(): rec_up = lax.ppermute(cur_up, 'chan', up_pairs)]
    dot_general x8 -> x0, local copies, waits for them, and re-layouts: 61.8 us -> none  [the longest x4 31 us: shards(): jnp.einsum('swf,rwf->srf', stacked_src, real_rcv, preferred_element_type=...]
    reduce_sum x0 -> x1, other arithmetic: none -> 49.7 us  [shards(): real_part = jnp.sum(sr * rr[0] + si * ri[0], axis=2)]
    dot_general x8 -> x0, matrix products: 34.2 us -> none  [the longest x4 17.2 us: shards(): jnp.einsum('swf,rwf->srf', stacked_src, imag_rcv, preferred_element_type=...]
    pmax x1 -> x0, blocking collectives: 32 us -> none  [shards(): global_peak = lax.pmax(local_peak, 'chan')]
    ppermute x0 -> x15, starting transfers between devices: none -> 23 us  [the longest x3 10.4 us: shards(): rec_up = lax.ppermute(cur_up, 'chan', up_pairs)]
    unnamed x19 -> x14, local copies, waits for them, and re-layouts: 9.71 us -> 0.94 us
  transfers between devices with their start and end apart: 1 -> 15, of which waited for: 1 -> 13; matrix products, arithmetic and copies ran while one was open for 1% -> 5% of each run, Pallas kernels for 0% -> 0%
where the time goes in v1:
time: 163 us
  other arithmetic  63.6 us (39%)
  waiting for transfers between devices  63 us (39%)
  starting transfers between devices  23 us (14%)
  local copies, waits for them, and re-layouts  7.22 us (4%)
  matrix products  5.51 us (3%)
    reduce_sum x1, other arithmetic, shards(): real_part = jnp.sum(sr * rr[0] + si * ri[0], axis=2)  49.7 us
    ppermute x3, waiting for transfers between devices, shards(): rec_up = lax.ppermute(cur_up, 'chan', up_pairs)  27.6 us
    ppermute x3, waiting for transfers between devices, shards(): rec_down = lax.ppermute(cur_down, 'chan', down_pairs)  12.5 us
    ppermute x3, starting transfers between devices, shards(): rec_up = lax.ppermute(cur_up, 'chan', up_pairs)  10.4 us
    ppermute x4, waiting for transfers between devices, shards(): lax.ppermute(peak, 'chan', pairs_of(n, lambda i, d=d: i ^ d))  9.3 us
    ppermute x2, waiting for transfers between devices, shards(): lax.ppermute(jnp.stack(held), 'chan', pairs_of(n, lambda i, b=b: i // qc...  8.58 us
    dot_general x4, matrix products, shards(): jnp.dot(flat, lag_table, preferred_element_type=jnp.float32)  5.51 us
    another operation x1, other arithmetic  5.38 us
  transfers between devices with their start and end apart: 15, of which 13 were waited for; matrix products, arithmetic and copies ran while one was open for 5% of the time, Pallas kernels for 0%

profile of v1, /device:TPU:0, one launch (start us, length us, event | category | flops | bytes accessed | tf_op | source)
XLA Modules:
  0.0 162.6 jit_solution(15383809230326634347)
XLA Ops:
  0.0 1.1 constant_dynamic-slice_fusion
  1.1 0.6 collective-permute-start
  1.7 2.6 %collective-permute-start.1 = (bf16[8,8,1024]{2,1,0:T(8,128)(2,1)S(1)}, bf16[8,8,1024]{2,1,0:T(8,128)(2,1)S(1)}, u32[]{:S(2)}, u32[]{:S(2)}) collective-permute-start(bf16[8,8,1024]{2,1,0:T(8,128)(2,1)S(1)} %get-tuple-element.41), channel_id=1, source_target_pairs={{0,2},{1,3},{2,0},{3,1},{4,6},{5,7},{6,4},{7,5},{8,10},{9,11},{10,... | collective-permute-start | bytes 393224 | tf_op jit(solution)/shard_map/ppermute | solution.py:66
  4.3 0.0 collective-permute-start.2
  4.3 0.8 reshape.278
  5.1 0.8 reshape.276
  5.9 2.7 %collective-permute-done.1 = bf16[8,8,1024]{2,1,0:T(8,128)(2,1)S(1)} collective-permute-done((bf16[8,8,1024]{2,1,0:T(8,128)(2,1)S(1)}, bf16[8,8,1024]{2,1,0:T(8,128)(2,1)S(1)}, u32[]{:S(2)}, u32[]{:S(2)}) %collective-permute-start.1) | collective-permute-done | bytes 131104 | tf_op jit(solution)/shard_map/ppermute | solution.py:66
  8.6 2.3 %collective-permute-done.2 = bf16[8,8,1024]{2,1,0:T(8,128)(2,1)S(1)} collective-permute-done((bf16[8,8,1024]{2,1,0:T(8,128)(2,1)S(1)}, bf16[8,8,1024]{2,1,0:T(8,128)(2,1)S(1)}, u32[]{:S(2)}, u32[]{:S(2)}) %collective-permute-start.2) | collective-permute-done | bytes 131104 | tf_op jit(solution)/shard_map/ppermute | solution.py:66
  10.9 0.1 pad_maximum_fusion.3
  11.0 0.6 gather_fusion.1
  11.6 0.1 select_select_fusion
  11.7 3.5 %collective-permute-start.3 = (bf16[4,8,8,1024]{3,2,1,0:T(8,128)(2,1)S(1)}, bf16[4,8,8,1024]{3,2,1,0:T(8,128)(2,1)S(1)}, u32[]{:S(2)}, u32[]{:S(2)}) collective-permute-start(bf16[4,8,8,1024]{3,2,1,0:T(8,128)(2,1)S(1)} %select_select_fusion), channel_id=1, source_target_pairs={{0,4},{1,5},{2,6},{3,7},{4,8},{5,9},{6,10},{7,11},{8,12},{9,13},{1... | collective-permute-start | bytes 1572872 | tf_op jit(solution)/shard_map/ppermute | solution.py:80
  15.2 1.3 collective-permute-start.6
  16.5 10.4 %collective-permute-done.3 = bf16[4,8,8,1024]{3,2,1,0:T(8,128)(2,1)S(1)} collective-permute-done((bf16[4,8,8,1024]{3,2,1,0:T(8,128)(2,1)S(1)}, bf16[4,8,8,1024]{3,2,1,0:T(8,128)(2,1)S(1)}, u32[]{:S(2)}, u32[]{:S(2)}) %collective-permute-start.3) | collective-permute-done | bytes 524320 | tf_op jit(solution)/shard_map/ppermute | solution.py:80
  26.8 4.1 %collective-permute-done.6 = bf16[4,8,8,1024]{3,2,1,0:T(8,128)(2,1)S(1)} collective-permute-done((bf16[4,8,8,1024]{3,2,1,0:T(8,128)(2,1)S(1)}, bf16[4,8,8,1024]{3,2,1,0:T(8,128)(2,1)S(1)}, u32[]{:S(2)}, u32[]{:S(2)}) %collective-permute-start.6) | collective-permute-done | bytes 524320 | tf_op jit(solution)/shard_map/ppermute | solution.py:81
  31.0 0.2 broadcast_select_fusion.1
  31.1 3.5 %collective-permute-start.4 = (bf16[4,8,8,1024]{3,2,1,0:T(8,128)(2,1)S(1)}, bf16[4,8,8,1024]{3,2,1,0:T(8,128)(2,1)S(1)}, u32[]{:S(2)}, u32[]{:S(2)}) collective-permute-start(bf16[4,8,8,1024]{3,2,1,0:T(8,128)(2,1)S(1)} %get-tuple-element.28), channel_id=1, source_target_pairs={{0,4},{1,5},{2,6},{3,7},{4,8},{5,9},{6,10},{7,11},{8,12},{9,13},{1... | collective-permute-start | bytes 1572872 | tf_op jit(solution)/shard_map/ppermute | solution.py:80
  34.6 0.0 copy-start.6
  34.6 0.0 copy-start
  34.7 1.3 collective-permute-start.7
  36.0 9.2 %collective-permute-done.4 = bf16[4,8,8,1024]{3,2,1,0:T(8,128)(2,1)S(1)} collective-permute-done((bf16[4,8,8,1024]{3,2,1,0:T(8,128)(2,1)S(1)}, bf16[4,8,8,1024]{3,2,1,0:T(8,128)(2,1)S(1)}, u32[]{:S(2)}, u32[]{:S(2)}) %collective-permute-start.4) | collective-permute-done | bytes 524320 | tf_op jit(solution)/shard_map/ppermute | solution.py:80
  45.2 4.2 %collective-permute-done.7 = bf16[4,8,8,1024]{3,2,1,0:T(8,128)(2,1)S(1)} collective-permute-done((bf16[4,8,8,1024]{3,2,1,0:T(8,128)(2,1)S(1)}, bf16[4,8,8,1024]{3,2,1,0:T(8,128)(2,1)S(1)}, u32[]{:S(2)}, u32[]{:S(2)}) %collective-permute-start.7) | collective-permute-done | bytes 524320 | tf_op jit(solution)/shard_map/ppermute | solution.py:81
  49.3 0.2 broadcast_select_fusion
  49.5 3.5 %collective-permute-start.5 = (bf16[4,8,8,1024]{3,2,1,0:T(8,128)(2,1)S(1)}, bf16[4,8,8,1024]{3,2,1,0:T(8,128)(2,1)S(1)}, u32[]{:S(2)}, u32[]{:S(2)}) collective-permute-start(bf16[4,8,8,1024]{3,2,1,0:T(8,128)(2,1)S(1)} %get-tuple-element.26), channel_id=1, source_target_pairs={{0,4},{1,5},{2,6},{3,7},{4,8},{5,9},{6,10},{7,11},{8,12},{9,13},{1... | collective-permute-start | bytes 1572872 | tf_op jit(solution)/shard_map/ppermute | solution.py:80
  53.0 1.3 collective-permute-start.8
  54.3 8.1 %collective-permute-done.5 = bf16[4,8,8,1024]{3,2,1,0:T(8,128)(2,1)S(1)} collective-permute-done((bf16[4,8,8,1024]{3,2,1,0:T(8,128)(2,1)S(1)}, bf16[4,8,8,1024]{3,2,1,0:T(8,128)(2,1)S(1)}, u32[]{:S(2)}, u32[]{:S(2)}) %collective-permute-start.5) | collective-permute-done | bytes 524320 | tf_op jit(solution)/shard_map/ppermute | solution.py:80
  62.4 4.1 %collective-permute-done.8 = bf16[4,8,8,1024]{3,2,1,0:T(8,128)(2,1)S(1)} collective-permute-done((bf16[4,8,8,1024]{3,2,1,0:T(8,128)(2,1)S(1)}, bf16[4,8,8,1024]{3,2,1,0:T(8,128)(2,1)S(1)}, u32[]{:S(2)}, u32[]{:S(2)}) %collective-permute-start.8) | collective-permute-done | bytes 524320 | tf_op jit(solution)/shard_map/ppermute | solution.py:81
  66.5 0.2 select_bitcast_fusion.1
  66.7 0.0 copy-start.1
  66.7 1.6 collective-permute-start.9
  68.4 0.6 gather_fusion
  69.0 8.6 %collective-permute-done.9 = bf16[1,4,8,8,1024]{4,3,2,1,0:T(8,128)(2,1)S(1)} collective-permute-done((bf16[1,4,8,8,1024]{4,3,2,1,0:T(8,128)(2,1)S(1)}, bf16[1,4,8,8,1024]{4,3,2,1,0:T(8,128)(2,1)S(1)}, u32[]{:S(2)}, u32[]{:S(2)}) %collective-permute-start.9) | collective-permute-done | bytes 524320 | tf_op jit(solution)/shard_map/ppermute | solution.py:91
  77.6 0.1 pad_maximum_fusion.2
  77.7 0.1 collective-permute-start.10
  77.8 5.4 %multiply_convert_fusion.1 = (bf16[512,512]{1,0:T(8,128)(2,1)}, bf16[512,512]{1,0:T(8,128)(2,1)}) fusion(s32[512]{0:T(512)S(1)} %iota_add_fusion, f32[512]{0:T(512)S(1)} %get-tuple-element.58, f32[512]{0:T(512)S(1)} %get-tuple-element.59), kind=kLoop, calls=%fused_computation.47 | loop fusion | flops 4718592 | bytes 1054720 | tf_op jit(solution)/shard_map/convert.6
  83.2 1.2 slice_convert_fusion.9
  84.3 0.2 pad_maximum_fusion.1
  84.5 2.0 %gather_fusion.2 = bf16[4,4,8,8,1024]{4,3,2,1,0:T(8,128)(2,1)} fusion(bf16[4,4,8,8,1024]{4,3,2,1,0:T(8,128)(2,1)S(1)} %pad_maximum_fusion.1, s32[1024]{0:T(1024)S(1)} %pad_clamp_fusion), kind=kCustom, calls=%fused_computation.2 | custom fusion | bytes 4194320 | tf_op jit(solution)/shard_map/jit(_take)/gather | solution.py:102
  86.5 1.9 %select_bitcast_fusion = bf16[4,4,8,8,1024]{4,3,2,0,1:T(8,128)(2,1)S(1)} fusion(bf16[4,4,8,8,1024]{4,3,2,1,0:T(8,128)(2,1)} %gather_fusion.2, pred[4]{0:T(512)(128)(4,1)S(1)} %compare_and_fusion.1), kind=kLoop, calls=%fused_computation.37 | loop fusion | flops 1048576 | bytes 4194308 | tf_op jit(solution)/shard_map/jit(_take)/select_n | solution.py:102
  88.4 0.2 copy.6
  88.6 0.2 broadcast_multiply_fusion
  88.8 0.2 slice_bitcast_fusion
  89.0 0.3 slice_convert_fusion.1
  89.3 0.3 slice_convert_fusion.5
  89.6 0.8 copy-done.2
  90.4 0.2 copy-done.3
  90.5 49.7 %add_reduce_fusion.3 = (bf16[32,32,512]{2,1,0:T(8,128)(2,1)S(1)}, bf16[32,32,512]{2,1,0:T(8,128)(2,1)S(1)}, bf16[32,32,512]{2,1,0:T(8,128)(2,1)S(1)}, bf16[32,32...) fusion(f32[32,8,512]{2,1,0:T(8,128)S(1)} %copy-done.3, ...), kind=kLoop, calls=%fused_computation.10 | loop fusion | flops 130023424 | bytes 13631488 | tf_op jit(solution)/shard_map/reduce_sum | solution.py:116
  140.2 1.4 abs_reduce_fusion.3
  141.6 1.4 abs_reduce_fusion.2
  143.0 1.4 abs_reduce_fusion.1
  144.4 1.4 abs_reduce_fusion
  145.8 0.5 collective-permute-start.11
  146.3 0.8 collective-permute-done.11
  147.1 1.6 collective-permute-start.12
  148.7 2.1 %collective-permute-done.12 = f32[4,32]{1,0:T(4,128)S(1)} collective-permute-done((f32[4,32]{1,0:T(4,128)S(1)}, f32[4,32]{1,0:T(4,128)S(1)}, u32[]{:S(2)}, u32[]{:S(2)}) %collective-permute-start.12) | collective-permute-done | bytes 544 | tf_op jit(solution)/shard_map/ppermute | solution.py:128
  150.8 0.9 collective-permute-start.13
  151.7 2.8 %collective-permute-done.13 = f32[4,32]{1,0:T(4,128)S(1)} collective-permute-done((f32[4,32]{1,0:T(4,128)S(1)}, f32[4,32]{1,0:T(4,128)S(1)}, u32[]{:S(2)}, u32[]{:S(2)}) %collective-permute-start.13) | collective-permute-done | bytes 544 | tf_op jit(solution)/shard_map/ppermute | solution.py:128
  154.5 0.8 collective-permute-start.14
  155.3 3.7 %collective-permute-done.14 = f32[4,32]{1,0:T(4,128)S(1)} collective-permute-done((f32[4,32]{1,0:T(4,128)S(1)}, f32[4,32]{1,0:T(4,128)S(1)}, u32[]{:S(2)}, u32[]{:S(2)}) %collective-permute-start.14) | collective-permute-done | bytes 544 | tf_op jit(solution)/shard_map/ppermute | solution.py:128
  159.0 0.3 fusion.22
  159.3 0.3 fusion.23
  159.6 0.3 fusion.24
  160.0 0.3 fusion.25
  160.3 2.3 %pad_maximum_fusion = bf16[4,32,32,512]{3,2,1,0:T(8,128)(2,1)} fusion(bf16[1,32,32,512]{3,2,1,0:T(8,128)(2,1)S(1)} %fusion.25, bf16[1,32,32,512]{3,2,1,0:T(8,128)(2,1)S(1)} %fusion.24, bf16[1,32,32,512]{3,2,1,0:T(8,128)(2,1)S(1)} %fusion.23, bf16[1,32,32,512]{3,2,1,0:T(8,128)(2,1)S(1)} %fusion.22), kind=kLoop, calls=%fused_computation.11 | loop fusion | flops 6291456 | bytes 8388608 | tf_op jit(solution)/shard_map/stack | solution.py:133
  (29 shorter events, 0.2 us)
Async XLA Ops:
  1.1 4.8 %collective-permute-start = (bf16[8,8,1024]{2,1,0:T(8,128)(2,1)S(1)}, bf16[8,8,1024]{2,1,0:T(8,128)(2,1)S(1)}, u32[]{:S(2)}, u32[]{:S(2)}) collective-permute-start(bf16[8,8,1024]{2,1,0:T(8,128)(2,1)S(1)} %get-tuple-element.42), channel_id=1, source_target_pairs={{0,1},{1,0},{2,3},{3,2},{4,5},{5,4},{6,7},{7,6},{8,9},{9,8},{10,11... | collective-permute-start | bytes 393224 | tf_op jit(solution)/shard_map/ppermute | solution.py:66
  1.7 6.9 %collective-permute-start.1 = (bf16[8,8,1024]{2,1,0:T(8,128)(2,1)S(1)}, bf16[8,8,1024]{2,1,0:T(8,128)(2,1)S(1)}, u32[]{:S(2)}, u32[]{:S(2)}) collective-permute-start(bf16[8,8,1024]{2,1,0:T(8,128)(2,1)S(1)} %get-tuple-element.41), channel_id=1, source_target_pairs={{0,2},{1,3},{2,0},{3,1},{4,6},{5,7},{6,4},{7,5},{8,10},{9,11},{10,... | collective-permute-start | bytes 393224 | tf_op jit(solution)/shard_map/ppermute | solution.py:66
  4.3 6.6 %collective-permute-start.2 = (bf16[8,8,1024]{2,1,0:T(8,128)(2,1)S(1)}, bf16[8,8,1024]{2,1,0:T(8,128)(2,1)S(1)}, u32[]{:S(2)}, u32[]{:S(2)}) collective-permute-start(bf16[8,8,1024]{2,1,0:T(8,128)(2,1)S(1)} %get-tuple-element.40), channel_id=1, source_target_pairs={{0,3},{1,2},{2,1},{3,0},{4,7},{5,6},{6,5},{7,4},{8,11},{9,10},{10,... | collective-permute-start | bytes 393224 | tf_op jit(solution)/shard_map/ppermute | solution.py:66
  11.7 15.1 %collective-permute-start.3 = (bf16[4,8,8,1024]{3,2,1,0:T(8,128)(2,1)S(1)}, bf16[4,8,8,1024]{3,2,1,0:T(8,128)(2,1)S(1)}, u32[]{:S(2)}, u32[]{:S(2)}) collective-permute-start(bf16[4,8,8,1024]{3,2,1,0:T(8,128)(2,1)S(1)} %select_select_fusion), channel_id=1, source_target_pairs={{0,4},{1,5},{2,6},{3,7},{4,8},{5,9},{6,10},{7,11},{8,12},{9,13},{1... | collective-permute-start | bytes 1572872 | tf_op jit(solution)/shard_map/ppermute | solution.py:80
  15.2 15.8 %collective-permute-start.6 = (bf16[4,8,8,1024]{3,2,1,0:T(8,128)(2,1)S(1)}, bf16[4,8,8,1024]{3,2,1,0:T(8,128)(2,1)S(1)}, u32[]{:S(2)}, u32[]{:S(2)}) collective-permute-start(bf16[4,8,8,1024]{3,2,1,0:T(8,128)(2,1)S(1)} %select_select_fusion), channel_id=1, source_target_pairs={{4,0},{5,1},{6,2},{7,3},{8,4},{9,5},{10,6},{11,7},{12,8},{13,9},{1... | collective-permute-start | bytes 1572872 | tf_op jit(solution)/shard_map/ppermute | solution.py:81
  31.1 14.0 %collective-permute-start.4 = (bf16[4,8,8,1024]{3,2,1,0:T(8,128)(2,1)S(1)}, bf16[4,8,8,1024]{3,2,1,0:T(8,128)(2,1)S(1)}, u32[]{:S(2)}, u32[]{:S(2)}) collective-permute-start(bf16[4,8,8,1024]{3,2,1,0:T(8,128)(2,1)S(1)} %get-tuple-element.28), channel_id=1, source_target_pairs={{0,4},{1,5},{2,6},{3,7},{4,8},{5,9},{6,10},{7,11},{8,12},{9,13},{1... | collective-permute-start | bytes 1572872 | tf_op jit(solution)/shard_map/ppermute | solution.py:80
  34.6 33.7 %copy-start.6 = (s32[8]{0:T(128)S(1)}, s32[8]{0:T(128)}, u32[]{:S(2)}) copy-start(s32[8]{0:T(128)} %param.6) | copy-start | bytes 100
  34.6 33.7 %copy-start = (s32[4]{0:T(128)S(1)}, s32[4]{0:T(128)}, u32[]{:S(2)}) copy-start(s32[4]{0:T(128)} %constant.137.clone) | copy-start | bytes 52
  34.7 14.7 %collective-permute-start.7 = (bf16[4,8,8,1024]{3,2,1,0:T(8,128)(2,1)S(1)}, bf16[4,8,8,1024]{3,2,1,0:T(8,128)(2,1)S(1)}, u32[]{:S(2)}, u32[]{:S(2)}) collective-permute-start(bf16[4,8,8,1024]{3,2,1,0:T(8,128)(2,1)S(1)} %get-tuple-element.27), channel_id=1, source_target_pairs={{4,0},{5,1},{6,2},{7,3},{8,4},{9,5},{10,6},{11,7},{12,8},{13,9},{1... | collective-permute-start | bytes 1572872 | tf_op jit(solution)/shard_map/ppermute | solution.py:81
  49.5 12.9 %collective-permute-start.5 = (bf16[4,8,8,1024]{3,2,1,0:T(8,128)(2,1)S(1)}, bf16[4,8,8,1024]{3,2,1,0:T(8,128)(2,1)S(1)}, u32[]{:S(2)}, u32[]{:S(2)}) collective-permute-start(bf16[4,8,8,1024]{3,2,1,0:T(8,128)(2,1)S(1)} %get-tuple-element.26), channel_id=1, source_target_pairs={{0,4},{1,5},{2,6},{3,7},{4,8},{5,9},{6,10},{7,11},{8,12},{9,13},{1... | collective-permute-start | bytes 1572872 | tf_op jit(solution)/shard_map/ppermute | solution.py:80
  53.0 13.5 %collective-permute-start.8 = (bf16[4,8,8,1024]{3,2,1,0:T(8,128)(2,1)S(1)}, bf16[4,8,8,1024]{3,2,1,0:T(8,128)(2,1)S(1)}, u32[]{:S(2)}, u32[]{:S(2)}) collective-permute-start(bf16[4,8,8,1024]{3,2,1,0:T(8,128)(2,1)S(1)} %get-tuple-element.25), channel_id=1, source_target_pairs={{4,0},{5,1},{6,2},{7,3},{8,4},{9,5},{10,6},{11,7},{12,8},{13,9},{1... | collective-permute-start | bytes 1572872 | tf_op jit(solution)/shard_map/ppermute | solution.py:81
  66.7 16.5 %copy-start.1 = (bf16[32,8,1024]{2,1,0:T(8,128)(2,1)S(1)}, bf16[32,8,1024]{2,1,0:T(8,128)(2,1)}, u32[]{:S(2)}) copy-start(bf16[32,8,1024]{2,1,0:T(8,128)(2,1)} %param.4) | copy-start | bytes 1572868
  66.7 10.8 %collective-permute-start.9 = (bf16[1,4,8,8,1024]{4,3,2,1,0:T(8,128)(2,1)S(1)}, bf16[1,4,8,8,1024]{4,3,2,1,0:T(8,128)(2,1)S(1)}, u32[]{:S(2)}, u32[]{:S(2)}) collective-permute-start(bf16[1,4,8,8,1024]{4,3,2,1,0:T(8,128)(2,1)S(1)} %select_bitcast_fusion.1), channel_id=1, source_target_pairs={{0,2},{1,3},{2,0},{3,1},{4,6},{5,7},{6,4},{7,5},{8,10},{9,11},{10,... | collective-permute-start | bytes 1572872 | tf_op jit(solution)/shard_map/ppermute | solution.py:91
  77.7 6.7 %collective-permute-start.10 = (bf16[2,4,8,8,1024]{4,3,2,1,0:T(8,128)(2,1)S(1)}, bf16[2,4,8,8,1024]{4,3,2,1,0:T(8,128)(2,1)S(1)}, u32[]{:S(2)}, u32[]{:S(2)}) collective-permute-start(bf16[2,4,8,8,1024]{4,3,2,1,0:T(8,128)(2,1)S(1)} %pad_maximum_fusion.2), channel_id=1, source_target_pairs={{0,1},{1,0},{2,3},{3,2},{4,5},{5,4},{6,7},{7,6},{8,9},{9,8},{10,11... | collective-permute-start | bytes 3145736 | tf_op jit(solution)/shard_map/ppermute | solution.py:91
  89.3 1.0 copy-start.2
  89.3 1.2 copy-start.3
  90.5 49.7 %copy-start.4 = (bf16[512,512]{1,0:T(8,128)(2,1)S(1)}, bf16[512,512]{1,0:T(8,128)(2,1)}, u32[]{:S(2)}) copy-start(bf16[512,512]{1,0:T(8,128)(2,1)} %get-tuple-element.47) | copy-start | bytes 1572868
  90.5 49.7 %copy-start.5 = (bf16[512,512]{1,0:T(8,128)(2,1)S(1)}, bf16[512,512]{1,0:T(8,128)(2,1)}, u32[]{:S(2)}) copy-start(bf16[512,512]{1,0:T(8,128)(2,1)} %get-tuple-element.48) | copy-start | bytes 1572868
  145.8 1.4 collective-permute-start.11
  147.1 3.7 %collective-permute-start.12 = (f32[4,32]{1,0:T(4,128)S(1)}, f32[4,32]{1,0:T(4,128)S(1)}, u32[]{:S(2)}, u32[]{:S(2)}) collective-permute-start(f32[4,32]{1,0:T(4,128)S(1)} %fusion.37), channel_id=1, source_target_pairs={{0,2},{1,3},{2,0},{3,1},{4,6},{5,7},{6,4},{7,5},{8,10},{9,11},{10,... | collective-permute-start | bytes 1544 | tf_op jit(solution)/shard_map/ppermute | solution.py:128
  150.8 3.7 %collective-permute-start.13 = (f32[4,32]{1,0:T(4,128)S(1)}, f32[4,32]{1,0:T(4,128)S(1)}, u32[]{:S(2)}, u32[]{:S(2)}) collective-permute-start(f32[4,32]{1,0:T(4,128)S(1)} %fusion.38), channel_id=1, source_target_pairs={{0,4},{1,5},{2,6},{3,7},{4,0},{5,1},{6,2},{7,3},{8,12},{9,13},{10,... | collective-permute-start | bytes 1544 | tf_op jit(solution)/shard_map/ppermute | solution.py:128
  154.5 4.5 %collective-permute-start.14 = (f32[4,32]{1,0:T(4,128)S(1)}, f32[4,32]{1,0:T(4,128)S(1)}, u32[]{:S(2)}, u32[]{:S(2)}) collective-permute-start(f32[4,32]{1,0:T(4,128)S(1)} %max.14), channel_id=1, source_target_pairs={{0,8},{1,9},{2,10},{3,11},{4,12},{5,13},{6,14},{7,15},{8,0},{9,1},... | collective-permute-start | bytes 1544 | tf_op jit(solution)/shard_map/ppermute | solution.py:128

commit v2 on v1

--- a/solution.py
+++ b/solution.py
@@ -67,69 +67,62 @@
             )
         by_off = jnp.stack(by_off)
 
-        here = zk == z
-        sel = jnp.take(by_off, qk ^ q, axis=0)
-        payload = jnp.where(here[:, None, None, None], sel, jnp.zeros_like(sel))
-
         up_pairs = pairs_of(n, lambda i: i + qc if i // qc < zc - 1 else None)
         down_pairs = pairs_of(n, lambda i: i - qc if i // qc > 0 else None)
-        mask = here[:, None, None, None]
-        cur_up, cur_down = payload, payload
-        rec_up, rec_down = payload, payload
-        for r in range(zc - 1):
-            rec_up = lax.ppermute(cur_up, "chan", up_pairs)
-            rec_down = lax.ppermute(cur_down, "chan", down_pairs)
-            if r < zc - 2:
-                cur_up = jnp.where(mask, payload, rec_up)
-                cur_down = jnp.where(mask, payload, rec_down)
-        below = (z > zk)[:, None, None, None]
-        mine = jnp.where(mask, payload, jnp.where(below, rec_up, rec_down))
-
+        inv = [0] * qc
         offs = [0]
-        held = [mine]
         for b in plane_bits:
-            got = lax.ppermute(
-                jnp.stack(held), "chan", pairs_of(n, lambda i, b=b: (i // qc) * qc + ((i % qc) ^ b))
-            )
             offs = offs + [o ^ b for o in offs]
-            held = held + [got[i] for i in range(got.shape[0])]
-        stack = jnp.stack(held)
-        inv = [0] * qc
         for e, o in enumerate(offs):
             inv[o] = e
-        inv = jnp.array(inv, jnp.int32)
-        order = jnp.take(inv, jnp.arange(qc, dtype=jnp.int32) ^ q)
-        full = jnp.take(stack, order, axis=0)
-        src_all = jnp.transpose(full, (1, 0, 2, 3, 4)).reshape(nb, SOURCE, windows, width)
+        order = jnp.take(jnp.array(inv, jnp.int32), jnp.arange(qc, dtype=jnp.int32) ^ q)
 
         lag_table = build_table(bins, LAGS)
-        window_mask = window_valid.astype(jnp.bfloat16)[None, None, :, None]
-        src_all = src_all * window_mask
-        rr = spectra[..., :bins].astype(jnp.float32)[None, None]
-        ri = spectra[..., bins:].astype(jnp.float32)[None, None]
-        traces_all = []
-        peaks = []
+        window_mask = window_valid.astype(jnp.bfloat16)[None, :, None]
+        rr = spectra[..., :bins].astype(jnp.float32)
+        ri = spectra[..., bins:].astype(jnp.float32)
+
+        out = []
         for k in range(nb):
-            src = src_all[k]
+            here = zk[k] == z
+            sel = lax.dynamic_index_in_dim(by_off, qk[k] ^ q, 0, keepdims=False)
+            payload = jnp.where(here, sel, jnp.zeros_like(sel))
+
+            cur_up, cur_down = payload, payload
+            rec_up, rec_down = payload, payload
+            for r in range(zc - 1):
+                rec_up = lax.ppermute(cur_up, "chan", up_pairs)
+                rec_down = lax.ppermute(cur_down, "chan", down_pairs)
+                if r < zc - 2:
+                    cur_up = jnp.where(here, payload, rec_up)
+                    cur_down = jnp.where(here, payload, rec_down)
+            mine = jnp.where(here, payload, jnp.where(z > zk[k], rec_up, rec_down))
+
+            held = [mine]
+            for b in plane_bits:
+                got = lax.ppermute(
+                    jnp.stack(held), "chan", pairs_of(n, lambda i, b=b: (i // qc) * qc + ((i % qc) ^ b))
+                )
+                held = held + [got[i] for i in range(got.shape[0])]
+            stack = jnp.stack(held)
+            full = jnp.take(stack, order, axis=0)
+            src = full.reshape(SOURCE, windows, width) * window_mask
+
             sr = src[..., :bins].astype(jnp.float32)[:, None]
             si = src[..., bins:].astype(jnp.float32)[:, None]
-            real_part = jnp.sum(sr * rr[0] + si * ri[0], axis=2)
-            imag_part = jnp.sum(sr * ri[0] - si * rr[0], axis=2)
+            real_part = jnp.sum(sr * rr + si * ri, axis=2)
+            imag_part = jnp.sum(sr * ri - si * rr, axis=2)
             cross = jnp.concatenate([real_part, imag_part], axis=2).astype(jnp.bfloat16)
             flat = cross.reshape(SOURCE * receivers, width)
             traces = jnp.dot(flat, lag_table, preferred_element_type=jnp.float32).reshape(
                 SOURCE, receivers, LAGS
             )
-            traces_all.append(traces)
-            peaks.append(jnp.max(jnp.abs(traces), axis=(1, 2)))
-        peak = jnp.stack(peaks)
-        d = 1
-        while d < n:
-            peak = jnp.maximum(peak, lax.ppermute(peak, "chan", pairs_of(n, lambda i, d=d: i ^ d)))
-            d *= 2
-        out = [
-            (traces_all[k] / (peak[k][:, None, None] + 1e-06)).astype(jnp.bfloat16) for k in range(nb)
-        ]
+            peak = jnp.max(jnp.abs(traces), axis=(1, 2))
+            d = 1
+            while d < n:
+                peak = jnp.maximum(peak, lax.ppermute(peak, "chan", pairs_of(n, lambda i, d=d: i ^ d)))
+                d *= 2
+            out.append((traces / (peak[:, None, None] + 1e-06)).astype(jnp.bfloat16))
         stacked = jnp.stack(out, axis=0)
         return stacked.reshape(source_blocks.shape[0], source_blocks.shape[1], SOURCE, receivers, LAGS)
 

time: 163 us -> 189 us (1.16)
  starting transfers between devices: 23 us -> 94.8 us
  waiting for transfers between devices: 63 us -> 7 us
  between operations: 0.34 us -> 8.25 us
    ppermute x3 -> x12, starting transfers between devices: 10.4 us -> 53.8 us  [shards(): rec_up = lax.ppermute(cur_up, 'chan', up_pairs)]
    ppermute x3 -> x12, waiting for transfers between devices: 27.6 us -> 0.03 us  [shards(): rec_up = lax.ppermute(cur_up, 'chan', up_pairs)]
    ppermute x4 -> x16, starting transfers between devices: 3.85 us -> 16.1 us  [shards(): lax.ppermute(peak, 'chan', pairs_of(n, lambda i, d=d: i ^ d))]
    ppermute x3 -> x12, starting transfers between devices: 3.88 us -> 15.7 us  [shards(): rec_down = lax.ppermute(cur_down, 'chan', down_pairs)]
    ppermute x3 -> x12, waiting for transfers between devices: 12.5 us -> 1.59 us  [shards(): rec_down = lax.ppermute(cur_down, 'chan', down_pairs)]
    ppermute x4 -> x16, waiting for transfers between devices: 9.3 us -> 2.72 us  [shards(): lax.ppermute(peak, 'chan', pairs_of(n, lambda i, d=d: i ^ d))]
    ppermute x2 -> x8, waiting for transfers between devices: 8.58 us -> 2.65 us  [shards(): lax.ppermute(jnp.stack(held), 'chan', pairs_of(n, lambda i, b=b: i // qc...]
    ppermute x3, waiting for transfers between devices: 5 us -> 0.01 us  [shards(): lax.ppermute(send, 'chan', pairs_of(n, lambda i, d=d: i // qc * qc + (i %...]
  transfers between devices with their start and end apart: 15 -> 51, of which waited for: 13 -> 6; matrix products, arithmetic and copies ran while one was open for 5% -> 10% of each run, Pallas kernels for 0% -> 0%
where the time goes in v2:
time: 189 us; the launch traced here: 188 us
  starting transfers between devices  94.8 us (50%)
  other arithmetic  65.4 us (35%)
  between operations  8.25 us (4%)
  waiting for transfers between devices  7 us (4%)
  local copies, waits for them, and re-layouts  6.74 us (4%)
  matrix products  5.5 us (3%)
    ppermute x12, starting transfers between devices, shards(): rec_up = lax.ppermute(cur_up, 'chan', up_pairs)  53.8 us
    reduce_sum x1, other arithmetic, shards(): real_part = jnp.sum(sr * rr + si * ri, axis=2)  49.7 us
    ppermute x16, starting transfers between devices, shards(): lax.ppermute(peak, 'chan', pairs_of(n, lambda i, d=d: i ^ d))  16.1 us
    ppermute x12, starting transfers between devices, shards(): rec_down = lax.ppermute(cur_down, 'chan', down_pairs)  15.7 us
    ppermute x8, starting transfers between devices, shards(): lax.ppermute(jnp.stack(held), 'chan', pairs_of(n, lambda i, b=b: i // qc...  6.09 us
    dot_general x4, matrix products, shards(): jnp.dot(flat, lag_table, preferred_element_type=jnp.float32)  5.5 us
    another operation x1, other arithmetic  5.34 us
  transfers between devices with their start and end apart: 51, of which 6 were waited for; matrix products, arithmetic and copies ran while one was open for 10% of the time, Pallas kernels for 0%

profile of v2, /device:TPU:0, one launch (start us, length us, event | category | flops | bytes accessed | tf_op | source)
XLA Modules:
  0.0 187.7 jit_solution(17769325104971848733)
XLA Ops:
  0.0 1.1 constant_dynamic-slice_fusion
  1.1 0.6 collective-permute-start
  1.7 2.6 %collective-permute-start.1 = (bf16[8,8,1024]{2,1,0:T(8,128)(2,1)S(1)}, bf16[8,8,1024]{2,1,0:T(8,128)(2,1)S(1)}, u32[]{:S(2)}, u32[]{:S(2)}) collective-permute-start(bf16[8,8,1024]{2,1,0:T(8,128)(2,1)S(1)} %get-tuple-element.38), channel_id=1, source_target_pairs={{0,2},{1,3},{2,0},{3,1},{4,6},{5,7},{6,4},{7,5},{8,10},{9,11},{10,... | collective-permute-start | bytes 393224 | tf_op jit(solution)/shard_map/ppermute | solution.py:66
  4.3 0.8 reshape.131
  5.1 0.7 fusion.32
  8.2 2.0 %slice_convert_fusion.9 = (f32[32,8,512]{2,1,0:T(8,128)S(1)}, f32[32,8,512]{2,1,0:T(8,128)}) fusion(bf16[32,8,1024]{2,1,0:T(8,128)(2,1)} %param.6), kind=kLoop, calls=%fused_computation.80 | loop fusion | flops 262144 | bytes 1572864 | tf_op jit(solution)/shard_map/convert_element_type | solution.py:82
  12.8 1.3 gather_fusion
  14.1 5.3 %multiply_convert_fusion.1 = (bf16[512,512]{1,0:T(8,128)(2,1)}, bf16[512,512]{1,0:T(8,128)(2,1)}) fusion(s32[512]{0:T(512)S(1)} %iota_add_fusion, f32[512]{0:T(512)S(1)} %get-tuple-element.84, f32[512]{0:T(512)S(1)} %get-tuple-element.85), kind=kLoop, calls=%fused_computation.46 | loop fusion | flops 4718592 | bytes 1054720 | tf_op jit(solution)/shard_map/convert.6
  19.5 3.7 %collective-permute-start.3 = (bf16[8,8,1024]{2,1,0:T(8,128)(2,1)S(1)}, bf16[8,8,1024]{2,1,0:T(8,128)(2,1)S(1)}, u32[]{:S(2)}, u32[]{:S(2)}) collective-permute-start(bf16[8,8,1024]{2,1,0:T(8,128)(2,1)S(1)} %get-tuple-element.27), channel_id=1, source_target_pairs={{0,4},{1,5},{2,6},{3,7},{4,8},{5,9},{6,10},{7,11},{8,12},{9,13},{1... | collective-permute-start | bytes 393224 | tf_op jit(solution)/shard_map/ppermute | solution.py:94
  23.3 1.3 collective-permute-start.6
  27.1 4.6 %collective-permute-start.27 = (bf16[8,8,1024]{2,1,0:T(8,128)(2,1)S(1)}, bf16[8,8,1024]{2,1,0:T(8,128)(2,1)S(1)}, u32[]{:S(2)}, u32[]{:S(2)}) collective-permute-start(bf16[8,8,1024]{2,1,0:T(8,128)(2,1)S(1)} %get-tuple-element.25), channel_id=1, source_target_pairs={{0,4},{1,5},{2,6},{3,7},{4,8},{5,9},{6,10},{7,11},{8,12},{9,13},{1... | collective-permute-start | bytes 393224 | tf_op jit(solution)/shard_map/ppermute | solution.py:94
  31.7 1.3 collective-permute-start.30
  33.0 4.6 %collective-permute-start.15 = (bf16[8,8,1024]{2,1,0:T(8,128)(2,1)S(1)}, bf16[8,8,1024]{2,1,0:T(8,128)(2,1)S(1)}, u32[]{:S(2)}, u32[]{:S(2)}) collective-permute-start(bf16[8,8,1024]{2,1,0:T(8,128)(2,1)S(1)} %get-tuple-element.26), channel_id=1, source_target_pairs={{0,4},{1,5},{2,6},{3,7},{4,8},{5,9},{6,10},{7,11},{8,12},{9,13},{1... | collective-permute-start | bytes 393224 | tf_op jit(solution)/shard_map/ppermute | solution.py:94
  37.6 1.3 collective-permute-start.18
  38.9 4.6 %collective-permute-start.39 = (bf16[8,8,1024]{2,1,0:T(8,128)(2,1)S(1)}, bf16[8,8,1024]{2,1,0:T(8,128)(2,1)S(1)}, u32[]{:S(2)}, u32[]{:S(2)}) collective-permute-start(bf16[8,8,1024]{2,1,0:T(8,128)(2,1)S(1)} %get-tuple-element.24), channel_id=1, source_target_pairs={{0,4},{1,5},{2,6},{3,7},{4,8},{5,9},{6,10},{7,11},{8,12},{9,13},{1... | collective-permute-start | bytes 393224 | tf_op jit(solution)/shard_map/ppermute | solution.py:94
  43.5 1.3 collective-permute-start.42
  44.8 4.6 %collective-permute-start.4 = (bf16[8,8,1024]{2,1,0:T(8,128)(2,1)S(1)}, bf16[8,8,1024]{2,1,0:T(8,128)(2,1)S(1)}, u32[]{:S(2)}, u32[]{:S(2)}) collective-permute-start(bf16[8,8,1024]{2,1,0:T(8,128)(2,1)S(1)} %get-tuple-element.55), channel_id=1, source_target_pairs={{0,4},{1,5},{2,6},{3,7},{4,8},{5,9},{6,10},{7,11},{8,12},{9,13},{1... | collective-permute-start | bytes 393224 | tf_op jit(solution)/shard_map/ppermute | solution.py:94
  49.4 1.3 collective-permute-start.7
  50.7 4.6 %collective-permute-start.28 = (bf16[8,8,1024]{2,1,0:T(8,128)(2,1)S(1)}, bf16[8,8,1024]{2,1,0:T(8,128)(2,1)S(1)}, u32[]{:S(2)}, u32[]{:S(2)}) collective-permute-start(bf16[8,8,1024]{2,1,0:T(8,128)(2,1)S(1)} %get-tuple-element.47), channel_id=1, source_target_pairs={{0,4},{1,5},{2,6},{3,7},{4,8},{5,9},{6,10},{7,11},{8,12},{9,13},{1... | collective-permute-start | bytes 393224 | tf_op jit(solution)/shard_map/ppermute | solution.py:94
  55.3 1.3 collective-permute-start.31
  56.6 4.6 %collective-permute-start.16 = (bf16[8,8,1024]{2,1,0:T(8,128)(2,1)S(1)}, bf16[8,8,1024]{2,1,0:T(8,128)(2,1)S(1)}, u32[]{:S(2)}, u32[]{:S(2)}) collective-permute-start(bf16[8,8,1024]{2,1,0:T(8,128)(2,1)S(1)} %get-tuple-element.51), channel_id=1, source_target_pairs={{0,4},{1,5},{2,6},{3,7},{4,8},{5,9},{6,10},{7,11},{8,12},{9,13},{1... | collective-permute-start | bytes 393224 | tf_op jit(solution)/shard_map/ppermute | solution.py:94
  61.2 1.3 collective-permute-start.19
  62.5 4.6 %collective-permute-start.40 = (bf16[8,8,1024]{2,1,0:T(8,128)(2,1)S(1)}, bf16[8,8,1024]{2,1,0:T(8,128)(2,1)S(1)}, u32[]{:S(2)}, u32[]{:S(2)}) collective-permute-start(bf16[8,8,1024]{2,1,0:T(8,128)(2,1)S(1)} %get-tuple-element.43), channel_id=1, source_target_pairs={{0,4},{1,5},{2,6},{3,7},{4,8},{5,9},{6,10},{7,11},{8,12},{9,13},{1... | collective-permute-start | bytes 393224 | tf_op jit(solution)/shard_map/ppermute | solution.py:94
  67.2 1.3 collective-permute-start.43
  68.5 4.6 %collective-permute-start.5 = (bf16[8,8,1024]{2,1,0:T(8,128)(2,1)S(1)}, bf16[8,8,1024]{2,1,0:T(8,128)(2,1)S(1)}, u32[]{:S(2)}, u32[]{:S(2)}) collective-permute-start(bf16[8,8,1024]{2,1,0:T(8,128)(2,1)S(1)} %get-tuple-element.53), channel_id=1, source_target_pairs={{0,4},{1,5},{2,6},{3,7},{4,8},{5,9},{6,10},{7,11},{8,12},{9,13},{1... | collective-permute-start | bytes 393224 | tf_op jit(solution)/shard_map/ppermute | solution.py:94
  73.1 1.3 collective-permute-start.8
  74.4 4.6 %collective-permute-start.29 = (bf16[8,8,1024]{2,1,0:T(8,128)(2,1)S(1)}, bf16[8,8,1024]{2,1,0:T(8,128)(2,1)S(1)}, u32[]{:S(2)}, u32[]{:S(2)}) collective-permute-start(bf16[8,8,1024]{2,1,0:T(8,128)(2,1)S(1)} %get-tuple-element.45), channel_id=1, source_target_pairs={{0,4},{1,5},{2,6},{3,7},{4,8},{5,9},{6,10},{7,11},{8,12},{9,13},{1... | collective-permute-start | bytes 393224 | tf_op jit(solution)/shard_map/ppermute | solution.py:94
  79.0 1.3 collective-permute-start.32
  80.3 4.6 %collective-permute-start.17 = (bf16[8,8,1024]{2,1,0:T(8,128)(2,1)S(1)}, bf16[8,8,1024]{2,1,0:T(8,128)(2,1)S(1)}, u32[]{:S(2)}, u32[]{:S(2)}) collective-permute-start(bf16[8,8,1024]{2,1,0:T(8,128)(2,1)S(1)} %get-tuple-element.49), channel_id=1, source_target_pairs={{0,4},{1,5},{2,6},{3,7},{4,8},{5,9},{6,10},{7,11},{8,12},{9,13},{1... | collective-permute-start | bytes 393224 | tf_op jit(solution)/shard_map/ppermute | solution.py:94
  84.9 1.3 collective-permute-start.20
  86.2 4.6 %collective-permute-start.41 = (bf16[8,8,1024]{2,1,0:T(8,128)(2,1)S(1)}, bf16[8,8,1024]{2,1,0:T(8,128)(2,1)S(1)}, u32[]{:S(2)}, u32[]{:S(2)}) collective-permute-start(bf16[8,8,1024]{2,1,0:T(8,128)(2,1)S(1)} %get-tuple-element.41), channel_id=1, source_target_pairs={{0,4},{1,5},{2,6},{3,7},{4,8},{5,9},{6,10},{7,11},{8,12},{9,13},{1... | collective-permute-start | bytes 393224 | tf_op jit(solution)/shard_map/ppermute | solution.py:94
  90.8 1.5 collective-permute-start.44
  92.3 1.6 collective-permute-start.9
  93.9 0.6 collective-permute-start.33
  94.5 1.6 collective-permute-start.21
  96.1 1.6 collective-permute-done.44
  97.7 1.6 collective-permute-start.45
  99.4 0.5 collective-permute-start.34
  100.5 2.3 %collective-permute-done.45 = bf16[1,8,8,1024]{3,2,1,0:T(8,128)(2,1)S(1)} collective-permute-done((bf16[1,8,8,1024]{3,2,1,0:T(8,128)(2,1)S(1)}, bf16[1,8,8,1024]{3,2,1,0:T(8,128)(2,1)S(1)}, u32[]{:S(2)}, u32[]{:S(2)}) %collective-permute-start.45) | collective-permute-done | bytes 131104 | tf_op jit(solution)/shard_map/ppermute | solution.py:103
  102.9 0.6 gather_fusion.1
  103.5 1.0 pad_maximum_fusion.4
  104.5 0.6 gather_fusion.3
  105.1 1.0 pad_maximum_fusion.3
  106.1 0.6 gather_fusion.2
  106.7 1.0 pad_maximum_fusion.5
  107.7 0.6 gather_fusion.4
  109.4 0.5 copy-done
  110.0 49.7 %add_reduce_fusion.3 = (bf16[32,32,512]{2,1,0:T(8,128)(2,1)S(1)}, bf16[32,32,512]{2,1,0:T(8,128)(2,1)S(1)}, bf16[32,32,512]{2,1,0:T(8,128)(2,1)S(1)}, bf16[32,32...) fusion(f32[32,8,512]{2,1,0:T(8,128)S(1)} %copy-done, ...), kind=kLoop, calls=%fused_computation.12 | loop fusion | flops 130023424 | bytes 13631488 | tf_op jit(solution)/shard_map/reduce_sum | solution.py:113
  159.7 1.4 abs_reduce_fusion.3
  161.6 1.4 abs_reduce_fusion.2
  163.0 1.4 abs_reduce_fusion.1
  164.9 1.4 abs_reduce_fusion
  166.4 1.6 collective-permute-start.12
  168.5 1.5 collective-permute-start.36
  170.5 1.7 collective-permute-start.13
  172.2 0.9 collective-permute-start.25
  173.1 1.2 collective-permute-start.37
  174.2 0.9 collective-permute-start.49
  175.1 2.5 %collective-permute-start.14 = (f32[32]{0:T(128)S(1)}, f32[32]{0:T(128)S(1)}, u32[]{:S(2)}, u32[]{:S(2)}) collective-permute-start(f32[32]{0:T(128)S(1)} %max.50), channel_id=1, source_target_pairs={{0,8},{1,9},{2,10},{3,11},{4,12},{5,13},{6,14},{7,15},{8,0},{9,1},... | collective-permute-start | bytes 392 | tf_op jit(solution)/shard_map/ppermute | solution.py:123
  177.6 0.7 collective-permute-start.26
  178.4 2.2 %collective-permute-start.38 = (f32[32]{0:T(128)S(1)}, f32[32]{0:T(128)S(1)}, u32[]{:S(2)}, u32[]{:S(2)}) collective-permute-start(f32[32]{0:T(128)S(1)} %max.58), channel_id=1, source_target_pairs={{0,8},{1,9},{2,10},{3,11},{4,12},{5,13},{6,14},{7,15},{8,0},{9,1},... | collective-permute-start | bytes 392 | tf_op jit(solution)/shard_map/ppermute | solution.py:123
  180.6 0.7 collective-permute-start.50
  183.2 1.9 collective-permute-done.50
  185.4 2.3 %pad_maximum_fusion = bf16[4,32,32,512]{3,2,1,0:T(8,128)(2,1)} fusion(bf16[1,32,32,512]{3,2,1,0:T(8,128)(2,1)S(1)} %fusion.25, bf16[1,32,32,512]{3,2,1,0:T(8,128)(2,1)S(1)} %fusion.24, bf16[1,32,32,512]{3,2,1,0:T(8,128)(2,1)S(1)} %fusion.23, bf16[1,32,32,512]{3,2,1,0:T(8,128)(2,1)S(1)} %fusion.22), kind=kLoop, calls=%fused_computation.13 | loop fusion | flops 6291456 | bytes 8388608 | tf_op jit(solution)/shard_map/stack | solution.py:126
  (118 shorter events, 6.9 us)
Async XLA Ops:
  0.0 27.1 %copy-start.3 = (s32[8]{0:T(128)S(1)}, s32[8]{0:T(128)}, u32[]{:S(2)}) copy-start(s32[8]{0:T(128)} %param.8) | copy-start | bytes 100
  1.1 18.2 %collective-permute-start = (bf16[8,8,1024]{2,1,0:T(8,128)(2,1)S(1)}, bf16[8,8,1024]{2,1,0:T(8,128)(2,1)S(1)}, u32[]{:S(2)}, u32[]{:S(2)}) collective-permute-start(bf16[8,8,1024]{2,1,0:T(8,128)(2,1)S(1)} %get-tuple-element.39), channel_id=1, source_target_pairs={{0,1},{1,0},{2,3},{3,2},{4,5},{5,4},{6,7},{7,6},{8,9},{9,8},{10,11... | collective-permute-start | bytes 393224 | tf_op jit(solution)/shard_map/ppermute | solution.py:66
  1.7 17.7 %collective-permute-start.1 = (bf16[8,8,1024]{2,1,0:T(8,128)(2,1)S(1)}, bf16[8,8,1024]{2,1,0:T(8,128)(2,1)S(1)}, u32[]{:S(2)}, u32[]{:S(2)}) collective-permute-start(bf16[8,8,1024]{2,1,0:T(8,128)(2,1)S(1)} %get-tuple-element.38), channel_id=1, source_target_pairs={{0,2},{1,3},{2,0},{3,1},{4,6},{5,7},{6,4},{7,5},{8,10},{9,11},{10,... | collective-permute-start | bytes 393224 | tf_op jit(solution)/shard_map/ppermute | solution.py:66
  4.3 15.1 %collective-permute-start.2 = (bf16[8,8,1024]{2,1,0:T(8,128)(2,1)S(1)}, bf16[8,8,1024]{2,1,0:T(8,128)(2,1)S(1)}, u32[]{:S(2)}, u32[]{:S(2)}) collective-permute-start(bf16[8,8,1024]{2,1,0:T(8,128)(2,1)S(1)} %get-tuple-element.37), channel_id=1, source_target_pairs={{0,3},{1,2},{2,1},{3,0},{4,7},{5,6},{6,5},{7,4},{8,11},{9,10},{10,... | collective-permute-start | bytes 393224 | tf_op jit(solution)/shard_map/ppermute | solution.py:66
  19.5 18.0 %collective-permute-start.3 = (bf16[8,8,1024]{2,1,0:T(8,128)(2,1)S(1)}, bf16[8,8,1024]{2,1,0:T(8,128)(2,1)S(1)}, u32[]{:S(2)}, u32[]{:S(2)}) collective-permute-start(bf16[8,8,1024]{2,1,0:T(8,128)(2,1)S(1)} %get-tuple-element.27), channel_id=1, source_target_pairs={{0,4},{1,5},{2,6},{3,7},{4,8},{5,9},{6,10},{7,11},{8,12},{9,13},{1... | collective-permute-start | bytes 393224 | tf_op jit(solution)/shard_map/ppermute | solution.py:94
  23.3 15.6 %collective-permute-start.6 = (bf16[8,8,1024]{2,1,0:T(8,128)(2,1)S(1)}, bf16[8,8,1024]{2,1,0:T(8,128)(2,1)S(1)}, u32[]{:S(2)}, u32[]{:S(2)}) collective-permute-start(bf16[8,8,1024]{2,1,0:T(8,128)(2,1)S(1)} %get-tuple-element.27), channel_id=1, source_target_pairs={{4,0},{5,1},{6,2},{7,3},{8,4},{9,5},{10,6},{11,7},{12,8},{13,9},{1... | collective-permute-start | bytes 393224 | tf_op jit(solution)/shard_map/ppermute | solution.py:95
  27.1 16.3 %collective-permute-start.27 = (bf16[8,8,1024]{2,1,0:T(8,128)(2,1)S(1)}, bf16[8,8,1024]{2,1,0:T(8,128)(2,1)S(1)}, u32[]{:S(2)}, u32[]{:S(2)}) collective-permute-start(bf16[8,8,1024]{2,1,0:T(8,128)(2,1)S(1)} %get-tuple-element.25), channel_id=1, source_target_pairs={{0,4},{1,5},{2,6},{3,7},{4,8},{5,9},{6,10},{7,11},{8,12},{9,13},{1... | collective-permute-start | bytes 393224 | tf_op jit(solution)/shard_map/ppermute | solution.py:94
  31.7 13.1 %collective-permute-start.30 = (bf16[8,8,1024]{2,1,0:T(8,128)(2,1)S(1)}, bf16[8,8,1024]{2,1,0:T(8,128)(2,1)S(1)}, u32[]{:S(2)}, u32[]{:S(2)}) collective-permute-start(bf16[8,8,1024]{2,1,0:T(8,128)(2,1)S(1)} %get-tuple-element.25), channel_id=1, source_target_pairs={{4,0},{5,1},{6,2},{7,3},{8,4},{9,5},{10,6},{11,7},{12,8},{13,9},{1... | collective-permute-start | bytes 393224 | tf_op jit(solution)/shard_map/ppermute | solution.py:95
  33.0 16.4 %collective-permute-start.15 = (bf16[8,8,1024]{2,1,0:T(8,128)(2,1)S(1)}, bf16[8,8,1024]{2,1,0:T(8,128)(2,1)S(1)}, u32[]{:S(2)}, u32[]{:S(2)}) collective-permute-start(bf16[8,8,1024]{2,1,0:T(8,128)(2,1)S(1)} %get-tuple-element.26), channel_id=1, source_target_pairs={{0,4},{1,5},{2,6},{3,7},{4,8},{5,9},{6,10},{7,11},{8,12},{9,13},{1... | collective-permute-start | bytes 393224 | tf_op jit(solution)/shard_map/ppermute | solution.py:94
  37.6 13.1 %collective-permute-start.18 = (bf16[8,8,1024]{2,1,0:T(8,128)(2,1)S(1)}, bf16[8,8,1024]{2,1,0:T(8,128)(2,1)S(1)}, u32[]{:S(2)}, u32[]{:S(2)}) collective-permute-start(bf16[8,8,1024]{2,1,0:T(8,128)(2,1)S(1)} %get-tuple-element.26), channel_id=1, source_target_pairs={{4,0},{5,1},{6,2},{7,3},{8,4},{9,5},{10,6},{11,7},{12,8},{13,9},{1... | collective-permute-start | bytes 393224 | tf_op jit(solution)/shard_map/ppermute | solution.py:95
  38.9 16.4 %collective-permute-start.39 = (bf16[8,8,1024]{2,1,0:T(8,128)(2,1)S(1)}, bf16[8,8,1024]{2,1,0:T(8,128)(2,1)S(1)}, u32[]{:S(2)}, u32[]{:S(2)}) collective-permute-start(bf16[8,8,1024]{2,1,0:T(8,128)(2,1)S(1)} %get-tuple-element.24), channel_id=1, source_target_pairs={{0,4},{1,5},{2,6},{3,7},{4,8},{5,9},{6,10},{7,11},{8,12},{9,13},{1... | collective-permute-start | bytes 393224 | tf_op jit(solution)/shard_map/ppermute | solution.py:94
  43.5 13.1 %collective-permute-start.42 = (bf16[8,8,1024]{2,1,0:T(8,128)(2,1)S(1)}, bf16[8,8,1024]{2,1,0:T(8,128)(2,1)S(1)}, u32[]{:S(2)}, u32[]{:S(2)}) collective-permute-start(bf16[8,8,1024]{2,1,0:T(8,128)(2,1)S(1)} %get-tuple-element.24), channel_id=1, source_target_pairs={{4,0},{5,1},{6,2},{7,3},{8,4},{9,5},{10,6},{11,7},{12,8},{13,9},{1... | collective-permute-start | bytes 393224 | tf_op jit(solution)/shard_map/ppermute | solution.py:95
  44.8 16.4 %collective-permute-start.4 = (bf16[8,8,1024]{2,1,0:T(8,128)(2,1)S(1)}, bf16[8,8,1024]{2,1,0:T(8,128)(2,1)S(1)}, u32[]{:S(2)}, u32[]{:S(2)}) collective-permute-start(bf16[8,8,1024]{2,1,0:T(8,128)(2,1)S(1)} %get-tuple-element.55), channel_id=1, source_target_pairs={{0,4},{1,5},{2,6},{3,7},{4,8},{5,9},{6,10},{7,11},{8,12},{9,13},{1... | collective-permute-start | bytes 393224 | tf_op jit(solution)/shard_map/ppermute | solution.py:94
  49.4 13.1 %collective-permute-start.7 = (bf16[8,8,1024]{2,1,0:T(8,128)(2,1)S(1)}, bf16[8,8,1024]{2,1,0:T(8,128)(2,1)S(1)}, u32[]{:S(2)}, u32[]{:S(2)}) collective-permute-start(bf16[8,8,1024]{2,1,0:T(8,128)(2,1)S(1)} %get-tuple-element.54), channel_id=1, source_target_pairs={{4,0},{5,1},{6,2},{7,3},{8,4},{9,5},{10,6},{11,7},{12,8},{13,9},{1... | collective-permute-start | bytes 393224 | tf_op jit(solution)/shard_map/ppermute | solution.py:95
  50.7 16.4 %collective-permute-start.28 = (bf16[8,8,1024]{2,1,0:T(8,128)(2,1)S(1)}, bf16[8,8,1024]{2,1,0:T(8,128)(2,1)S(1)}, u32[]{:S(2)}, u32[]{:S(2)}) collective-permute-start(bf16[8,8,1024]{2,1,0:T(8,128)(2,1)S(1)} %get-tuple-element.47), channel_id=1, source_target_pairs={{0,4},{1,5},{2,6},{3,7},{4,8},{5,9},{6,10},{7,11},{8,12},{9,13},{1... | collective-permute-start | bytes 393224 | tf_op jit(solution)/shard_map/ppermute | solution.py:94
  55.3 13.1 %collective-permute-start.31 = (bf16[8,8,1024]{2,1,0:T(8,128)(2,1)S(1)}, bf16[8,8,1024]{2,1,0:T(8,128)(2,1)S(1)}, u32[]{:S(2)}, u32[]{:S(2)}) collective-permute-start(bf16[8,8,1024]{2,1,0:T(8,128)(2,1)S(1)} %get-tuple-element.46), channel_id=1, source_target_pairs={{4,0},{5,1},{6,2},{7,3},{8,4},{9,5},{10,6},{11,7},{12,8},{13,9},{1... | collective-permute-start | bytes 393224 | tf_op jit(solution)/shard_map/ppermute | solution.py:95
  56.6 16.4 %collective-permute-start.16 = (bf16[8,8,1024]{2,1,0:T(8,128)(2,1)S(1)}, bf16[8,8,1024]{2,1,0:T(8,128)(2,1)S(1)}, u32[]{:S(2)}, u32[]{:S(2)}) collective-permute-start(bf16[8,8,1024]{2,1,0:T(8,128)(2,1)S(1)} %get-tuple-element.51), channel_id=1, source_target_pairs={{0,4},{1,5},{2,6},{3,7},{4,8},{5,9},{6,10},{7,11},{8,12},{9,13},{1... | collective-permute-start | bytes 393224 | tf_op jit(solution)/shard_map/ppermute | solution.py:94
  61.2 13.1 %collective-permute-start.19 = (bf16[8,8,1024]{2,1,0:T(8,128)(2,1)S(1)}, bf16[8,8,1024]{2,1,0:T(8,128)(2,1)S(1)}, u32[]{:S(2)}, u32[]{:S(2)}) collective-permute-start(bf16[8,8,1024]{2,1,0:T(8,128)(2,1)S(1)} %get-tuple-element.50), channel_id=1, source_target_pairs={{4,0},{5,1},{6,2},{7,3},{8,4},{9,5},{10,6},{11,7},{12,8},{13,9},{1... | collective-permute-start | bytes 393224 | tf_op jit(solution)/shard_map/ppermute | solution.py:95
  62.5 16.4 %collective-permute-start.40 = (bf16[8,8,1024]{2,1,0:T(8,128)(2,1)S(1)}, bf16[8,8,1024]{2,1,0:T(8,128)(2,1)S(1)}, u32[]{:S(2)}, u32[]{:S(2)}) collective-permute-start(bf16[8,8,1024]{2,1,0:T(8,128)(2,1)S(1)} %get-tuple-element.43), channel_id=1, source_target_pairs={{0,4},{1,5},{2,6},{3,7},{4,8},{5,9},{6,10},{7,11},{8,12},{9,13},{1... | collective-permute-start | bytes 393224 | tf_op jit(solution)/shard_map/ppermute | solution.py:94
  67.2 13.1 %collective-permute-start.43 = (bf16[8,8,1024]{2,1,0:T(8,128)(2,1)S(1)}, bf16[8,8,1024]{2,1,0:T(8,128)(2,1)S(1)}, u32[]{:S(2)}, u32[]{:S(2)}) collective-permute-start(bf16[8,8,1024]{2,1,0:T(8,128)(2,1)S(1)} %get-tuple-element.42), channel_id=1, source_target_pairs={{4,0},{5,1},{6,2},{7,3},{8,4},{9,5},{10,6},{11,7},{12,8},{13,9},{1... | collective-permute-start | bytes 393224 | tf_op jit(solution)/shard_map/ppermute | solution.py:95
  68.5 16.4 %collective-permute-start.5 = (bf16[8,8,1024]{2,1,0:T(8,128)(2,1)S(1)}, bf16[8,8,1024]{2,1,0:T(8,128)(2,1)S(1)}, u32[]{:S(2)}, u32[]{:S(2)}) collective-permute-start(bf16[8,8,1024]{2,1,0:T(8,128)(2,1)S(1)} %get-tuple-element.53), channel_id=1, source_target_pairs={{0,4},{1,5},{2,6},{3,7},{4,8},{5,9},{6,10},{7,11},{8,12},{9,13},{1... | collective-permute-start | bytes 393224 | tf_op jit(solution)/shard_map/ppermute | solution.py:94
  73.1 13.1 %collective-permute-start.8 = (bf16[8,8,1024]{2,1,0:T(8,128)(2,1)S(1)}, bf16[8,8,1024]{2,1,0:T(8,128)(2,1)S(1)}, u32[]{:S(2)}, u32[]{:S(2)}) collective-permute-start(bf16[8,8,1024]{2,1,0:T(8,128)(2,1)S(1)} %get-tuple-element.52), channel_id=1, source_target_pairs={{4,0},{5,1},{6,2},{7,3},{8,4},{9,5},{10,6},{11,7},{12,8},{13,9},{1... | collective-permute-start | bytes 393224 | tf_op jit(solution)/shard_map/ppermute | solution.py:95
  74.4 16.4 %collective-permute-start.29 = (bf16[8,8,1024]{2,1,0:T(8,128)(2,1)S(1)}, bf16[8,8,1024]{2,1,0:T(8,128)(2,1)S(1)}, u32[]{:S(2)}, u32[]{:S(2)}) collective-permute-start(bf16[8,8,1024]{2,1,0:T(8,128)(2,1)S(1)} %get-tuple-element.45), channel_id=1, source_target_pairs={{0,4},{1,5},{2,6},{3,7},{4,8},{5,9},{6,10},{7,11},{8,12},{9,13},{1... | collective-permute-start | bytes 393224 | tf_op jit(solution)/shard_map/ppermute | solution.py:94
  79.0 13.3 %collective-permute-start.32 = (bf16[8,8,1024]{2,1,0:T(8,128)(2,1)S(1)}, bf16[8,8,1024]{2,1,0:T(8,128)(2,1)S(1)}, u32[]{:S(2)}, u32[]{:S(2)}) collective-permute-start(bf16[8,8,1024]{2,1,0:T(8,128)(2,1)S(1)} %get-tuple-element.44), channel_id=1, source_target_pairs={{4,0},{5,1},{6,2},{7,3},{8,4},{9,5},{10,6},{11,7},{12,8},{13,9},{1... | collective-permute-start | bytes 393224 | tf_op jit(solution)/shard_map/ppermute | solution.py:95
  80.3 13.6 %collective-permute-start.17 = (bf16[8,8,1024]{2,1,0:T(8,128)(2,1)S(1)}, bf16[8,8,1024]{2,1,0:T(8,128)(2,1)S(1)}, u32[]{:S(2)}, u32[]{:S(2)}) collective-permute-start(bf16[8,8,1024]{2,1,0:T(8,128)(2,1)S(1)} %get-tuple-element.49), channel_id=1, source_target_pairs={{0,4},{1,5},{2,6},{3,7},{4,8},{5,9},{6,10},{7,11},{8,12},{9,13},{1... | collective-permute-start | bytes 393224 | tf_op jit(solution)/shard_map/ppermute | solution.py:94
  84.9 9.6 %collective-permute-start.20 = (bf16[8,8,1024]{2,1,0:T(8,128)(2,1)S(1)}, bf16[8,8,1024]{2,1,0:T(8,128)(2,1)S(1)}, u32[]{:S(2)}, u32[]{:S(2)}) collective-permute-start(bf16[8,8,1024]{2,1,0:T(8,128)(2,1)S(1)} %get-tuple-element.48), channel_id=1, source_target_pairs={{4,0},{5,1},{6,2},{7,3},{8,4},{9,5},{10,6},{11,7},{12,8},{13,9},{1... | collective-permute-start | bytes 393224 | tf_op jit(solution)/shard_map/ppermute | solution.py:95
  86.2 9.9 %collective-permute-start.41 = (bf16[8,8,1024]{2,1,0:T(8,128)(2,1)S(1)}, bf16[8,8,1024]{2,1,0:T(8,128)(2,1)S(1)}, u32[]{:S(2)}, u32[]{:S(2)}) collective-permute-start(bf16[8,8,1024]{2,1,0:T(8,128)(2,1)S(1)} %get-tuple-element.41), channel_id=1, source_target_pairs={{0,4},{1,5},{2,6},{3,7},{4,8},{5,9},{6,10},{7,11},{8,12},{9,13},{1... | collective-permute-start | bytes 393224 | tf_op jit(solution)/shard_map/ppermute | solution.py:94
  90.8 6.9 %collective-permute-start.44 = (bf16[8,8,1024]{2,1,0:T(8,128)(2,1)S(1)}, bf16[8,8,1024]{2,1,0:T(8,128)(2,1)S(1)}, u32[]{:S(2)}, u32[]{:S(2)}) collective-permute-start(bf16[8,8,1024]{2,1,0:T(8,128)(2,1)S(1)} %get-tuple-element.40), channel_id=1, source_target_pairs={{4,0},{5,1},{6,2},{7,3},{8,4},{9,5},{10,6},{11,7},{12,8},{13,9},{1... | collective-permute-start | bytes 393224 | tf_op jit(solution)/shard_map/ppermute | solution.py:95
  92.3 7.0 %collective-permute-start.9 = (bf16[1,8,8,1024]{3,2,1,0:T(8,128)(2,1)S(1)}, bf16[1,8,8,1024]{3,2,1,0:T(8,128)(2,1)S(1)}, u32[]{:S(2)}, u32[]{:S(2)}) collective-permute-start(bf16[1,8,8,1024]{3,2,1,0:T(8,128)(2,1)S(1)} %select_bitcast_fusion.6), channel_id=1, source_target_pairs={{0,2},{1,3},{2,0},{3,1},{4,6},{5,7},{6,4},{7,5},{8,10},{9,11},{10,... | collective-permute-start | bytes 393224 | tf_op jit(solution)/shard_map/ppermute | solution.py:103
  93.9 5.5 %collective-permute-start.33 = (bf16[1,8,8,1024]{3,2,1,0:T(8,128)(2,1)S(1)}, bf16[1,8,8,1024]{3,2,1,0:T(8,128)(2,1)S(1)}, u32[]{:S(2)}, u32[]{:S(2)}) collective-permute-start(bf16[1,8,8,1024]{3,2,1,0:T(8,128)(2,1)S(1)} %select_bitcast_fusion.2), channel_id=1, source_target_pairs={{0,2},{1,3},{2,0},{3,1},{4,6},{5,7},{6,4},{7,5},{8,10},{9,11},{10,... | collective-permute-start | bytes 393224 | tf_op jit(solution)/shard_map/ppermute | solution.py:103
  94.5 5.8 %collective-permute-start.21 = (bf16[1,8,8,1024]{3,2,1,0:T(8,128)(2,1)S(1)}, bf16[1,8,8,1024]{3,2,1,0:T(8,128)(2,1)S(1)}, u32[]{:S(2)}, u32[]{:S(2)}) collective-permute-start(bf16[1,8,8,1024]{3,2,1,0:T(8,128)(2,1)S(1)} %select_bitcast_fusion.4), channel_id=1, source_target_pairs={{0,2},{1,3},{2,0},{3,1},{4,6},{5,7},{6,4},{7,5},{8,10},{9,11},{10,... | collective-permute-start | bytes 393224 | tf_op jit(solution)/shard_map/ppermute | solution.py:103
  97.7 5.0 %collective-permute-start.45 = (bf16[1,8,8,1024]{3,2,1,0:T(8,128)(2,1)S(1)}, bf16[1,8,8,1024]{3,2,1,0:T(8,128)(2,1)S(1)}, u32[]{:S(2)}, u32[]{:S(2)}) collective-permute-start(bf16[1,8,8,1024]{3,2,1,0:T(8,128)(2,1)S(1)} %select_bitcast_fusion), channel_id=1, source_target_pairs={{0,2},{1,3},{2,0},{3,1},{4,6},{5,7},{6,4},{7,5},{8,10},{9,11},{10,... | collective-permute-start | bytes 393224 | tf_op jit(solution)/shard_map/ppermute | solution.py:103
  99.3 3.5 %collective-permute-start.10 = (bf16[2,8,8,1024]{3,2,1,0:T(8,128)(2,1)S(1)}, bf16[2,8,8,1024]{3,2,1,0:T(8,128)(2,1)S(1)}, u32[]{:S(2)}, u32[]{:S(2)}) collective-permute-start(bf16[2,8,8,1024]{3,2,1,0:T(8,128)(2,1)S(1)} %pad_maximum_fusion.6), channel_id=1, source_target_pairs={{0,1},{1,0},{2,3},{3,2},{4,5},{5,4},{6,7},{7,6},{8,9},{9,8},{10,11... | collective-permute-start | bytes 786440 | tf_op jit(solution)/shard_map/ppermute | solution.py:103
  99.4 4.1 %collective-permute-start.34 = (bf16[2,8,8,1024]{3,2,1,0:T(8,128)(2,1)S(1)}, bf16[2,8,8,1024]{3,2,1,0:T(8,128)(2,1)}, u32[]{:S(2)}, u32[]{:S(2)}) collective-permute-start(bf16[2,8,8,1024]{3,2,1,0:T(8,128)(2,1)S(1)} %pad_maximum_fusion.8), channel_id=1, source_target_pairs={{0,1},{1,0},{2,3},{3,2},{4,5},{5,4},{6,7},{7,6},{8,9},{9,8},{10,11... | collective-permute-start | bytes 786440 | tf_op jit(solution)/shard_map/ppermute | solution.py:103
  100.4 4.7 %collective-permute-start.22 = (bf16[2,8,8,1024]{3,2,1,0:T(8,128)(2,1)S(1)}, bf16[2,8,8,1024]{3,2,1,0:T(8,128)(2,1)}, u32[]{:S(2)}, u32[]{:S(2)}) collective-permute-start(bf16[2,8,8,1024]{3,2,1,0:T(8,128)(2,1)S(1)} %pad_maximum_fusion.7), channel_id=1, source_target_pairs={{0,1},{1,0},{2,3},{3,2},{4,5},{5,4},{6,7},{7,6},{8,9},{9,8},{10,11... | collective-permute-start | bytes 786440 | tf_op jit(solution)/shard_map/ppermute | solution.py:103
  102.8 4.0 %collective-permute-start.46 = (bf16[2,8,8,1024]{3,2,1,0:T(8,128)(2,1)S(1)}, bf16[2,8,8,1024]{3,2,1,0:T(8,128)(2,1)}, u32[]{:S(2)}, u32[]{:S(2)}) collective-permute-start(bf16[2,8,8,1024]{3,2,1,0:T(8,128)(2,1)S(1)} %pad_maximum_fusion.9), channel_id=1, source_target_pairs={{0,1},{1,0},{2,3},{3,2},{4,5},{5,4},{6,7},{7,6},{8,9},{9,8},{10,11... | collective-permute-start | bytes 786440 | tf_op jit(solution)/shard_map/ppermute | solution.py:103
  108.9 1.0 copy-start
  110.0 49.7 %copy-start.1 = (bf16[512,512]{1,0:T(8,128)(2,1)S(1)}, bf16[512,512]{1,0:T(8,128)(2,1)}, u32[]{:S(2)}) copy-start(bf16[512,512]{1,0:T(8,128)(2,1)} %get-tuple-element.56) | copy-start | bytes 1572868
  110.0 49.7 %copy-start.2 = (bf16[512,512]{1,0:T(8,128)(2,1)S(1)}, bf16[512,512]{1,0:T(8,128)(2,1)}, u32[]{:S(2)}) copy-start(bf16[512,512]{1,0:T(8,128)(2,1)} %get-tuple-element.57) | copy-start | bytes 1572868
  161.0 5.3 %collective-permute-start.11 = (f32[32]{0:T(128)S(1)}, f32[32]{0:T(128)S(1)}, u32[]{:S(2)}, u32[]{:S(2)}) collective-permute-start(f32[32]{0:T(128)S(1)} %get-tuple-element.82), channel_id=1, source_target_pairs={{0,1},{1,0},{2,3},{3,2},{4,5},{5,4},{6,7},{7,6},{8,9},{9,8},{10,11... | collective-permute-start | bytes 392 | tf_op jit(solution)/shard_map/ppermute | solution.py:123
  162.9 5.0 %collective-permute-start.23 = (f32[32]{0:T(128)S(1)}, f32[32]{0:T(128)S(1)}, u32[]{:S(2)}, u32[]{:S(2)}) collective-permute-start(f32[32]{0:T(128)S(1)} %get-tuple-element.80), channel_id=1, source_target_pairs={{0,1},{1,0},{2,3},{3,2},{4,5},{5,4},{6,7},{7,6},{8,9},{9,8},{10,11... | collective-permute-start | bytes 392 | tf_op jit(solution)/shard_map/ppermute | solution.py:123
  164.4 4.1 %collective-permute-start.35 = (f32[32]{0:T(128)S(1)}, f32[32]{0:T(128)S(1)}, u32[]{:S(2)}, u32[]{:S(2)}) collective-permute-start(f32[32]{0:T(128)S(1)} %get-tuple-element.78), channel_id=1, source_target_pairs={{0,1},{1,0},{2,3},{3,2},{4,5},{5,4},{6,7},{7,6},{8,9},{9,8},{10,11... | collective-permute-start | bytes 392 | tf_op jit(solution)/shard_map/ppermute | solution.py:123
  166.3 3.7 %collective-permute-start.47 = (f32[32]{0:T(128)S(1)}, f32[32]{0:T(128)S(1)}, u32[]{:S(2)}, u32[]{:S(2)}) collective-permute-start(f32[32]{0:T(128)S(1)} %get-tuple-element.76), channel_id=1, source_target_pairs={{0,1},{1,0},{2,3},{3,2},{4,5},{5,4},{6,7},{7,6},{8,9},{9,8},{10,11... | collective-permute-start | bytes 392 | tf_op jit(solution)/shard_map/ppermute | solution.py:123
  166.4 4.1 %collective-permute-start.12 = (f32[32]{0:T(128)S(1)}, f32[32]{0:T(128)S(1)}, u32[]{:S(2)}, u32[]{:S(2)}) collective-permute-start(f32[32]{0:T(128)S(1)} %max.48), channel_id=1, source_target_pairs={{0,2},{1,3},{2,0},{3,1},{4,6},{5,7},{6,4},{7,5},{8,10},{9,11},{10,... | collective-permute-start | bytes 392 | tf_op jit(solution)/shard_map/ppermute | solution.py:123
  168.0 4.2 %collective-permute-start.24 = (f32[32]{0:T(128)S(1)}, f32[32]{0:T(128)S(1)}, u32[]{:S(2)}, u32[]{:S(2)}) collective-permute-start(f32[32]{0:T(128)S(1)} %max.52), channel_id=1, source_target_pairs={{0,2},{1,3},{2,0},{3,1},{4,6},{5,7},{6,4},{7,5},{8,10},{9,11},{10,... | collective-permute-start | bytes 392 | tf_op jit(solution)/shard_map/ppermute | solution.py:123
  168.5 4.6 %collective-permute-start.36 = (f32[32]{0:T(128)S(1)}, f32[32]{0:T(128)S(1)}, u32[]{:S(2)}, u32[]{:S(2)}) collective-permute-start(f32[32]{0:T(128)S(1)} %max.56), channel_id=1, source_target_pairs={{0,2},{1,3},{2,0},{3,1},{4,6},{5,7},{6,4},{7,5},{8,10},{9,11},{10,... | collective-permute-start | bytes 392 | tf_op jit(solution)/shard_map/ppermute | solution.py:123
  170.0 4.2 %collective-permute-start.48 = (f32[32]{0:T(128)S(1)}, f32[32]{0:T(128)S(1)}, u32[]{:S(2)}, u32[]{:S(2)}) collective-permute-start(f32[32]{0:T(128)S(1)} %max.60), channel_id=1, source_target_pairs={{0,2},{1,3},{2,0},{3,1},{4,6},{5,7},{6,4},{7,5},{8,10},{9,11},{10,... | collective-permute-start | bytes 392 | tf_op jit(solution)/shard_map/ppermute | solution.py:123
  170.5 4.6 %collective-permute-start.13 = (f32[32]{0:T(128)S(1)}, f32[32]{0:T(128)S(1)}, u32[]{:S(2)}, u32[]{:S(2)}) collective-permute-start(f32[32]{0:T(128)S(1)} %max.49), channel_id=1, source_target_pairs={{0,4},{1,5},{2,6},{3,7},{4,0},{5,1},{6,2},{7,3},{8,12},{9,13},{10,... | collective-permute-start | bytes 392 | tf_op jit(solution)/shard_map/ppermute | solution.py:123
  172.2 5.4 %collective-permute-start.25 = (f32[32]{0:T(128)S(1)}, f32[32]{0:T(128)S(1)}, u32[]{:S(2)}, u32[]{:S(2)}) collective-permute-start(f32[32]{0:T(128)S(1)} %max.53), channel_id=1, source_target_pairs={{0,4},{1,5},{2,6},{3,7},{4,0},{5,1},{6,2},{7,3},{8,12},{9,13},{10,... | collective-permute-start | bytes 392 | tf_op jit(solution)/shard_map/ppermute | solution.py:123
  173.1 5.3 %collective-permute-start.37 = (f32[32]{0:T(128)S(1)}, f32[32]{0:T(128)S(1)}, u32[]{:S(2)}, u32[]{:S(2)}) collective-permute-start(f32[32]{0:T(128)S(1)} %max.57), channel_id=1, source_target_pairs={{0,4},{1,5},{2,6},{3,7},{4,0},{5,1},{6,2},{7,3},{8,12},{9,13},{10,... | collective-permute-start | bytes 392 | tf_op jit(solution)/shard_map/ppermute | solution.py:123
  174.2 6.3 %collective-permute-start.49 = (f32[32]{0:T(128)S(1)}, f32[32]{0:T(128)S(1)}, u32[]{:S(2)}, u32[]{:S(2)}) collective-permute-start(f32[32]{0:T(128)S(1)} %max.61), channel_id=1, source_target_pairs={{0,4},{1,5},{2,6},{3,7},{4,0},{5,1},{6,2},{7,3},{8,12},{9,13},{10,... | collective-permute-start | bytes 392 | tf_op jit(solution)/shard_map/ppermute | solution.py:123
  175.1 6.2 %collective-permute-start.14 = (f32[32]{0:T(128)S(1)}, f32[32]{0:T(128)S(1)}, u32[]{:S(2)}, u32[]{:S(2)}) collective-permute-start(f32[32]{0:T(128)S(1)} %max.50), channel_id=1, source_target_pairs={{0,8},{1,9},{2,10},{3,11},{4,12},{5,13},{6,14},{7,15},{8,0},{9,1},... | collective-permute-start | bytes 392 | tf_op jit(solution)/shard_map/ppermute | solution.py:123
  177.6 4.5 %collective-permute-start.26 = (f32[32]{0:T(128)S(1)}, f32[32]{0:T(128)S(1)}, u32[]{:S(2)}, u32[]{:S(2)}) collective-permute-start(f32[32]{0:T(128)S(1)} %max.54), channel_id=1, source_target_pairs={{0,8},{1,9},{2,10},{3,11},{4,12},{5,13},{6,14},{7,15},{8,0},{9,1},... | collective-permute-start | bytes 392 | tf_op jit(solution)/shard_map/ppermute | solution.py:123
  178.4 4.5 %collective-permute-start.38 = (f32[32]{0:T(128)S(1)}, f32[32]{0:T(128)S(1)}, u32[]{:S(2)}, u32[]{:S(2)}) collective-permute-start(f32[32]{0:T(128)S(1)} %max.58), channel_id=1, source_target_pairs={{0,8},{1,9},{2,10},{3,11},{4,12},{5,13},{6,14},{7,15},{8,0},{9,1},... | collective-permute-start | bytes 392 | tf_op jit(solution)/shard_map/ppermute | solution.py:123
  180.6 4.5 %collective-permute-start.50 = (f32[32]{0:T(128)S(1)}, f32[32]{0:T(128)S(1)}, u32[]{:S(2)}, u32[]{:S(2)}) collective-permute-start(f32[32]{0:T(128)S(1)} %max.62), channel_id=1, source_target_pairs={{0,8},{1,9},{2,10},{3,11},{4,12},{5,13},{6,14},{7,15},{8,0},{9,1},... | collective-permute-start | bytes 392 | tf_op jit(solution)/shard_map/ppermute | solution.py:123

commit v3 on v1

--- a/solution.py
+++ b/solution.py
@@ -3,6 +3,7 @@
 import jax
 import jax.numpy as jnp
 from jax import lax
+from jax.experimental import pallas as pl
 from jax.sharding import PartitionSpec as P
 
 SOURCE = 32
@@ -18,6 +19,57 @@
     return jnp.concatenate([weight * jnp.cos(theta), -weight * jnp.sin(theta)], axis=0).astype(
         jnp.bfloat16
     )
+
+
+ST = 8
+RC = 16
+
+
+def cross_kernel(src_ref, rcv_ref, out_ref):
+    bins = src_ref.shape[-1] // 2
+    windows = src_ref.shape[2]
+    rows = rcv_ref.shape[1]
+
+    def body(s, carry):
+        row = src_ref[0, s].astype(jnp.float32)
+        for c in range(rows // RC):
+            rs = slice(c * RC, (c + 1) * RC)
+            acc_re = jnp.zeros((RC, bins), jnp.float32)
+            acc_im = jnp.zeros((RC, bins), jnp.float32)
+            for w in range(windows):
+                a = jnp.broadcast_to(row[w : w + 1, :bins], (RC, bins))
+                b = jnp.broadcast_to(row[w : w + 1, bins:], (RC, bins))
+                rr = rcv_ref[w, rs, :bins]
+                ri = rcv_ref[w, rs, bins:]
+                acc_re = acc_re + (a * rr + b * ri)
+                acc_im = acc_im + (a * ri - b * rr)
+            out_ref[0, s, rs, :bins] = acc_re.astype(out_ref.dtype)
+            out_ref[0, s, rs, bins:] = acc_im.astype(out_ref.dtype)
+        return carry
+
+    lax.fori_loop(0, src_ref.shape[1], body, 0)
+
+
+def cross_products(src_all, rcv):
+    nb, sources, windows, width = src_all.shape
+    receivers = rcv.shape[0]
+    rcv_t = jnp.transpose(rcv, (1, 0, 2)).astype(jnp.float32)
+    flops = 8 * nb * sources * receivers * windows * (width // 2)
+    return pl.pallas_call(
+        cross_kernel,
+        grid=(nb, sources // ST),
+        in_specs=[
+            pl.BlockSpec((1, ST, windows, width), lambda k, i: (k, i, 0, 0)),
+            pl.BlockSpec((windows, receivers, width), lambda k, i: (0, 0, 0)),
+        ],
+        out_specs=pl.BlockSpec((1, ST, receivers, width), lambda k, i: (k, i, 0, 0)),
+        out_shape=jax.ShapeDtypeStruct((nb, sources, receivers, width), jnp.bfloat16),
+        cost_estimate=pl.CostEstimate(
+            flops=flops,
+            bytes_accessed=src_all.size * 2 + rcv_t.size * 4 + nb * sources * receivers * width * 2,
+            transcendentals=0,
+        ),
+    )(src_all, rcv_t)
 
 
 def plane_size(mesh):
@@ -105,23 +157,12 @@
         lag_table = build_table(bins, LAGS)
         window_mask = window_valid.astype(jnp.bfloat16)[None, None, :, None]
         src_all = src_all * window_mask
-        rr = spectra[..., :bins].astype(jnp.float32)[None, None]
-        ri = spectra[..., bins:].astype(jnp.float32)[None, None]
-        traces_all = []
-        peaks = []
-        for k in range(nb):
-            src = src_all[k]
-            sr = src[..., :bins].astype(jnp.float32)[:, None]
-            si = src[..., bins:].astype(jnp.float32)[:, None]
-            real_part = jnp.sum(sr * rr[0] + si * ri[0], axis=2)
-            imag_part = jnp.sum(sr * ri[0] - si * rr[0], axis=2)
-            cross = jnp.concatenate([real_part, imag_part], axis=2).astype(jnp.bfloat16)
-            flat = cross.reshape(SOURCE * receivers, width)
-            traces = jnp.dot(flat, lag_table, preferred_element_type=jnp.float32).reshape(
-                SOURCE, receivers, LAGS
-            )
-            traces_all.append(traces)
-            peaks.append(jnp.max(jnp.abs(traces), axis=(1, 2)))
+        cross = cross_products(src_all, spectra)
+        traces = jnp.dot(
+            cross.reshape(nb * SOURCE * receivers, width), lag_table, preferred_element_type=jnp.float32
+        ).reshape(nb, SOURCE, receivers, LAGS)
+        traces_all = [traces[k] for k in range(nb)]
+        peaks = [jnp.max(jnp.abs(traces[k]), axis=(1, 2)) for k in range(nb)]
         peak = jnp.stack(peaks)
         d = 1
         while d < n:

time: 163 us -> 143 us (0.88)
  other arithmetic: 63.6 us -> 20.4 us
  Pallas kernels: 0 us -> 25 us
  waiting for transfers between devices: 63 us -> 51.8 us
  starting transfers between devices: 23 us -> 30.7 us
    reduce_sum x1 -> x0, other arithmetic: 49.7 us -> none  [shards(): real_part = jnp.sum(sr * rr[0] + si * ri[0], axis=2)]
    pallas_call x0 -> x1, Pallas kernels: none -> 25 us  [cross_products(): pl.pallas_call(cross_kernel, grid=(nb, sources // ST), in_specs=[pl.Block...]
    ppermute x3, waiting for transfers between devices: 27.6 us -> 3.57 us  [shards(): rec_up = lax.ppermute(cur_up, 'chan', up_pairs)]
    ppermute x3, waiting for transfers between devices: 12.5 us -> 27.9 us  [shards(): rec_down = lax.ppermute(cur_down, 'chan', down_pairs)]
    ppermute x3, starting transfers between devices: 10.4 us -> 15 us  [shards(): rec_up = lax.ppermute(cur_up, 'chan', up_pairs)]
    reduce_max x0 -> x5, other arithmetic: none -> 3.9 us  [shards(): peaks = [jnp.max(jnp.abs(traces[k]), axis=(1, 2)) for k in range(nb)]]
    ppermute x4, starting transfers between devices: 3.85 us -> 7.16 us  [shards(): lax.ppermute(peak, 'chan', pairs_of(n, lambda i, d=d: i ^ d))]
    ppermute x4, waiting for transfers between devices: 9.3 us -> 6.46 us  [shards(): lax.ppermute(peak, 'chan', pairs_of(n, lambda i, d=d: i ^ d))]
  transfers between devices with their start and end apart: 15 -> 15, of which waited for: 13 -> 13; matrix products, arithmetic and copies ran while one was open for 5% -> 6% of each run, Pallas kernels for 0% -> 0%
where the time goes in v3:
time: 143 us
  waiting for transfers between devices  51.8 us (36%)
  starting transfers between devices  30.7 us (21%)
  Pallas kernels  25 us (17%)
  other arithmetic  20.4 us (14%)
  local copies, waits for them, and re-layouts  7.63 us (5%)
  matrix products  6.89 us (5%)
    ppermute x3, waiting for transfers between devices, shards(): rec_down = lax.ppermute(cur_down, 'chan', down_pairs)  27.9 us
    pallas_call x1, Pallas kernels, cross_products(): pl.pallas_call(cross_kernel, grid=(nb, sources // ST), in_specs=[pl.Block...  25 us
    ppermute x3, starting transfers between devices, shards(): rec_up = lax.ppermute(cur_up, 'chan', up_pairs)  15 us
    ppermute x2, waiting for transfers between devices, shards(): lax.ppermute(jnp.stack(held), 'chan', pairs_of(n, lambda i, b=b: i // qc...  9.32 us
    ppermute x4, starting transfers between devices, shards(): lax.ppermute(peak, 'chan', pairs_of(n, lambda i, d=d: i ^ d))  7.16 us
    dot_general x1, matrix products, shards(): jnp.dot(cross.reshape(nb * SOURCE * receivers, width), lag_table, preferr...  6.89 us
    ppermute x4, waiting for transfers between devices, shards(): lax.ppermute(peak, 'chan', pairs_of(n, lambda i, d=d: i ^ d))  6.46 us
    another operation x1, other arithmetic  5.4 us
  transfers between devices with their start and end apart: 15, of which 13 were waited for; matrix products, arithmetic and copies ran while one was open for 6% of the time, Pallas kernels for 0%

profile of v3, /device:TPU:0, one launch (start us, length us, event | category | flops | bytes accessed | tf_op | source)
XLA Modules:
  0.0 142.7 jit_solution(7758303737909210398)
XLA Ops:
  0.0 1.1 constant_dynamic-slice_fusion
  1.1 2.5 %collective-permute-start.2 = (bf16[8,8,1024]{2,1,0:T(8,128)(2,1)S(1)}, bf16[8,8,1024]{2,1,0:T(8,128)(2,1)S(1)}, u32[]{:S(2)}, u32[]{:S(2)}) collective-permute-start(bf16[8,8,1024]{2,1,0:T(8,128)(2,1)S(1)} %get-tuple-element.20), channel_id=1, source_target_pairs={{0,3},{1,2},{2,1},{3,0},{4,7},{5,6},{6,5},{7,4},{8,11},{9,10},{10,... | collective-permute-start | bytes 393224 | tf_op jit(solution)/shard_map/ppermute | solution.py:118
  3.6 0.6 collective-permute-start.1
  4.3 0.0 collective-permute-start
  4.3 0.8 reshape.300
  5.1 0.8 reshape.298
  5.9 1.6 %collective-permute-done.2 = bf16[8,8,1024]{2,1,0:T(8,128)(2,1)S(1)} collective-permute-done((bf16[8,8,1024]{2,1,0:T(8,128)(2,1)S(1)}, bf16[8,8,1024]{2,1,0:T(8,128)(2,1)S(1)}, u32[]{:S(2)}, u32[]{:S(2)}) %collective-permute-start.2) | collective-permute-done | bytes 131104 | tf_op jit(solution)/shard_map/ppermute | solution.py:118
  7.5 3.0 %collective-permute-done.1 = bf16[8,8,1024]{2,1,0:T(8,128)(2,1)S(1)} collective-permute-done((bf16[8,8,1024]{2,1,0:T(8,128)(2,1)S(1)}, bf16[8,8,1024]{2,1,0:T(8,128)(2,1)S(1)}, u32[]{:S(2)}, u32[]{:S(2)}) %collective-permute-start.1) | collective-permute-done | bytes 131104 | tf_op jit(solution)/shard_map/ppermute | solution.py:118
  10.5 0.1 pad_maximum_fusion.3
  10.6 0.6 gather_fusion.1
  11.2 0.1 select_select_fusion
  11.3 1.3 collective-permute-start.6
  12.6 4.9 %collective-permute-start.3 = (bf16[4,8,8,1024]{3,2,1,0:T(8,128)(2,1)S(1)}, bf16[4,8,8,1024]{3,2,1,0:T(8,128)(2,1)S(1)}, u32[]{:S(2)}, u32[]{:S(2)}) collective-permute-start(bf16[4,8,8,1024]{3,2,1,0:T(8,128)(2,1)S(1)} %select_select_fusion), channel_id=1, source_target_pairs={{0,4},{1,5},{2,6},{3,7},{4,8},{5,9},{6,10},{7,11},{8,12},{9,13},{1... | collective-permute-start | bytes 1572872 | tf_op jit(solution)/shard_map/ppermute | solution.py:132
  17.5 10.2 %collective-permute-done.6 = bf16[4,8,8,1024]{3,2,1,0:T(8,128)(2,1)S(1)} collective-permute-done((bf16[4,8,8,1024]{3,2,1,0:T(8,128)(2,1)S(1)}, bf16[4,8,8,1024]{3,2,1,0:T(8,128)(2,1)S(1)}, u32[]{:S(2)}, u32[]{:S(2)}) %collective-permute-start.6) | collective-permute-done | bytes 524320 | tf_op jit(solution)/shard_map/ppermute | solution.py:133
  27.7 1.2 collective-permute-done.3
  28.9 0.2 broadcast_select_fusion.1
  29.0 1.3 collective-permute-start.7
  30.3 0.0 copy-start
  30.4 5.0 %collective-permute-start.4 = (bf16[4,8,8,1024]{3,2,1,0:T(8,128)(2,1)S(1)}, bf16[4,8,8,1024]{3,2,1,0:T(8,128)(2,1)S(1)}, u32[]{:S(2)}, u32[]{:S(2)}) collective-permute-start(bf16[4,8,8,1024]{3,2,1,0:T(8,128)(2,1)S(1)} %get-tuple-element.18), channel_id=1, source_target_pairs={{0,4},{1,5},{2,6},{3,7},{4,8},{5,9},{6,10},{7,11},{8,12},{9,13},{1... | collective-permute-start | bytes 1572872 | tf_op jit(solution)/shard_map/ppermute | solution.py:132
  35.4 9.3 %collective-permute-done.7 = bf16[4,8,8,1024]{3,2,1,0:T(8,128)(2,1)S(1)} collective-permute-done((bf16[4,8,8,1024]{3,2,1,0:T(8,128)(2,1)S(1)}, bf16[4,8,8,1024]{3,2,1,0:T(8,128)(2,1)S(1)}, u32[]{:S(2)}, u32[]{:S(2)}) %collective-permute-start.7) | collective-permute-done | bytes 524320 | tf_op jit(solution)/shard_map/ppermute | solution.py:133
  44.7 1.2 collective-permute-done.4
  45.9 0.2 broadcast_select_fusion
  46.1 1.3 collective-permute-start.8
  47.4 5.0 %collective-permute-start.5 = (bf16[4,8,8,1024]{3,2,1,0:T(8,128)(2,1)S(1)}, bf16[4,8,8,1024]{3,2,1,0:T(8,128)(2,1)S(1)}, u32[]{:S(2)}, u32[]{:S(2)}) collective-permute-start(bf16[4,8,8,1024]{3,2,1,0:T(8,128)(2,1)S(1)} %get-tuple-element.16), channel_id=1, source_target_pairs={{0,4},{1,5},{2,6},{3,7},{4,8},{5,9},{6,10},{7,11},{8,12},{9,13},{1... | collective-permute-start | bytes 1572872 | tf_op jit(solution)/shard_map/ppermute | solution.py:132
  52.4 8.4 %collective-permute-done.8 = bf16[4,8,8,1024]{3,2,1,0:T(8,128)(2,1)S(1)} collective-permute-done((bf16[4,8,8,1024]{3,2,1,0:T(8,128)(2,1)S(1)}, bf16[4,8,8,1024]{3,2,1,0:T(8,128)(2,1)S(1)}, u32[]{:S(2)}, u32[]{:S(2)}) %collective-permute-start.8) | collective-permute-done | bytes 524320 | tf_op jit(solution)/shard_map/ppermute | solution.py:133
  60.9 1.2 collective-permute-done.5
  62.0 0.2 select_bitcast_fusion.1
  62.2 1.4 collective-permute-start.9
  63.6 0.6 gather_fusion
  64.3 9.3 %collective-permute-done.9 = bf16[1,4,8,8,1024]{4,3,2,1,0:T(8,128)(2,1)S(1)} collective-permute-done((bf16[1,4,8,8,1024]{4,3,2,1,0:T(8,128)(2,1)S(1)}, bf16[1,4,8,8,1024]{4,3,2,1,0:T(8,128)(2,1)S(1)}, u32[]{:S(2)}, u32[]{:S(2)}) %collective-permute-start.9) | collective-permute-done | bytes 524320 | tf_op jit(solution)/shard_map/ppermute | solution.py:143
  73.6 0.1 pad_maximum_fusion.2
  73.7 0.1 collective-permute-start.10
  73.8 5.4 %multiply_convert_fusion.1 = (bf16[512,512]{1,0:T(8,128)(2,1)}, bf16[512,512]{1,0:T(8,128)(2,1)}) fusion(s32[512]{0:T(512)S(1)} %iota_add_fusion, f32[512]{0:T(512)S(1)} %get-tuple-element.30, f32[512]{0:T(512)S(1)} %get-tuple-element.31), kind=kLoop, calls=%fused_computation.27 | loop fusion | flops 4718592 | bytes 1054720 | tf_op jit(solution)/shard_map/convert.1
  79.2 1.4 convert_bitcast_fusion.rcv_ref
  80.6 0.2 pad_maximum_fusion.1
  80.8 2.0 %gather_fusion.2 = bf16[4,4,8,8,1024]{4,3,2,1,0:T(8,128)(2,1)} fusion(bf16[4,4,8,8,1024]{4,3,2,1,0:T(8,128)(2,1)S(1)} %pad_maximum_fusion.1, s32[1024]{0:T(1024)S(1)} %pad_clamp_fusion), kind=kCustom, calls=%fused_computation.2 | custom fusion | bytes 4194320 | tf_op jit(solution)/shard_map/jit(_take)/gather | solution.py:154
  82.8 1.9 %select_bitcast_fusion = bf16[4,4,8,8,1024]{4,3,2,0,1:T(8,128)(2,1)S(1)} fusion(bf16[4,4,8,8,1024]{4,3,2,1,0:T(8,128)(2,1)} %gather_fusion.2, pred[4]{0:T(512)(128)(4,1)S(1)} %compare_and_fusion.1), kind=kLoop, calls=%fused_computation.13 | loop fusion | flops 1048576 | bytes 4194308 | tf_op jit(solution)/shard_map/jit(_take)/select_n | solution.py:154
  84.7 0.2 copy.8
  84.9 1.5 %broadcast_multiply_fusion.src_ref = bf16[4,32,8,1024]{3,2,1,0:T(8,128)(2,1)} fusion(bf16[4,32,8,1024]{3,2,1,0:T(8,128)(2,1)S(1)} %bitcast.51, bf16[8]{0:T(256)(128)(2,1)S(1)} %convert_element_type.54), kind=kLoop, calls=%fused_computation.30 | loop fusion | flops 1048576 | bytes 4194320 | tf_op jit(solution)/shard_map/mul | solution.py:159
  86.4 25.0 %shard_map.46 = bf16[4,32,32,1024]{3,2,1,0:T(8,128)(2,1)} custom-call(bf16[4,32,8,1024]{3,2,1,0:T(8,128)(2,1)} %broadcast_multiply_fusion.src_ref, f32[8,32,1024]{2,1,0:T(8,128)} %convert_bitcast_fusion.rcv_ref), custom_call_target="tpu_custom_call" | custom-call | flops 134217728 | bytes 11534336 | tf_op jit(solution)/shard_map/pallas_call | solution.py:58
  111.4 6.9 %fusion.3 = f32[4096,512]{1,0:T(8,128)S(1)} fusion(bf16[4096,1024]{1,0:T(8,128)(2,1)} %bitcast.50, bf16[512,512]{1,0:T(8,128)(2,1)S(1)} %copy-done.5, bf16[512,512]{1,0:T(8,128)(2,1)S(1)} %copy-done.4), kind=kOutput, calls=%fused_computation.21 | convolution fusion | flops 4297064448 | bytes 17825792 | tf_op jit(solution)/shard_map/dot_general | solution.py:161
  118.3 3.4 %abs_reduce_fusion.3 = (f32[1024]{0:T(1024)S(1)}, f32[1024]{0:T(1024)S(1)}, f32[1024]{0:T(1024)S(1)}, f32[1024]{0:T(1024)S(1)}, f32[1024,512]{1,0:T(8,128)S(1)},...) fusion(f32[4096,512]{1,0:T(8,128)S(1)} %fusion.3), kind=kLoop, calls=%fused_computation.12 | loop fusion | flops 4190208 | bytes 16793600 | tf_op jit(solution)/shard_map/reduce_max | solution.py:165
  121.7 0.1 reduce_max.47
  121.8 0.1 reduce_max.53
  121.9 0.1 reduce_max.51
  122.0 0.1 reduce_max.54
  122.1 0.1 reduce_max.59
  122.2 0.1 reduce_max.72
  122.3 0.1 reduce_max.74
  122.4 0.1 reduce_max.75
  122.5 0.6 collective-permute-start.11
  123.1 0.8 collective-permute-done.11
  123.9 1.1 collective-permute-start.12
  125.1 2.5 %collective-permute-done.12 = f32[4,32]{1,0:T(4,128)S(1)} collective-permute-done((f32[4,32]{1,0:T(4,128)S(1)}, f32[4,32]{1,0:T(4,128)S(1)}, u32[]{:S(2)}, u32[]{:S(2)}) %collective-permute-start.12) | collective-permute-done | bytes 544 | tf_op jit(solution)/shard_map/ppermute | solution.py:169
  127.6 2.5 %collective-permute-start.13 = (f32[4,32]{1,0:T(4,128)S(1)}, f32[4,32]{1,0:T(4,128)S(1)}, u32[]{:S(2)}, u32[]{:S(2)}) collective-permute-start(f32[4,32]{1,0:T(4,128)S(1)} %fusion.20), channel_id=1, source_target_pairs={{0,4},{1,5},{2,6},{3,7},{4,0},{5,1},{6,2},{7,3},{8,12},{9,13},{10,... | collective-permute-start | bytes 1544 | tf_op jit(solution)/shard_map/ppermute | solution.py:169
  130.1 1.6 %collective-permute-done.13 = f32[4,32]{1,0:T(4,128)S(1)} collective-permute-done((f32[4,32]{1,0:T(4,128)S(1)}, f32[4,32]{1,0:T(4,128)S(1)}, u32[]{:S(2)}, u32[]{:S(2)}) %collective-permute-start.13) | collective-permute-done | bytes 544 | tf_op jit(solution)/shard_map/ppermute | solution.py:169
  131.7 2.9 %collective-permute-start.14 = (f32[4,32]{1,0:T(4,128)S(1)}, f32[4,32]{1,0:T(4,128)S(1)}, u32[]{:S(2)}, u32[]{:S(2)}) collective-permute-start(f32[4,32]{1,0:T(4,128)S(1)} %max.14), channel_id=1, source_target_pairs={{0,8},{1,9},{2,10},{3,11},{4,12},{5,13},{6,14},{7,15},{8,0},{9,1},... | collective-permute-start | bytes 1544 | tf_op jit(solution)/shard_map/ppermute | solution.py:169
  134.6 1.6 %collective-permute-done.14 = f32[4,32]{1,0:T(4,128)S(1)} collective-permute-done((f32[4,32]{1,0:T(4,128)S(1)}, f32[4,32]{1,0:T(4,128)S(1)}, u32[]{:S(2)}, u32[]{:S(2)}) %collective-permute-start.14) | collective-permute-done | bytes 544 | tf_op jit(solution)/shard_map/ppermute | solution.py:169
  136.2 1.9 %divide_convert_fusion.2 = bf16[1,32,32,512]{3,2,1,0:T(8,128)(2,1)S(1)} fusion(f32[1,32,32,512]{3,2,1,0:T(8,128)} %bitcast.49, f32[32]{0:T(128)S(1)} %get-tuple-element.26), kind=kLoop, calls=%fused_computation.7 | loop fusion | flops 1048576 | bytes 3145856 | tf_op jit(solution)/shard_map/convert_element_type | solution.py:172
  138.1 0.3 divide_convert_fusion.1
  138.5 1.2 copy-done.1
  139.7 0.3 divide_convert_fusion
  140.0 0.3 divide_convert_fusion.3
  140.4 2.3 %pad_maximum_fusion = bf16[4,32,32,512]{3,2,1,0:T(8,128)(2,1)} fusion(bf16[1,32,32,512]{3,2,1,0:T(8,128)(2,1)S(1)} %divide_convert_fusion, bf16[1,32,32,512]{3,2,1,0:T(8,128)(2,1)S(1)} %divide_convert_fusion.1, bf16[1,32,32,512]{3,2,1,0:T(8,128)(2,1)S(1)} %divide_convert_fusion.2, bf16[1,32,32,512]{3,2,1,0:T(8,128)(2,1)S(1)} %divide_convert_fusion.3), kind=kLoop, calls=%fused_computation.3 | loop fusion | flops 6291456 | bytes 8388608 | tf_op jit(solution)/shard_map/stack | solution.py:174
  (32 shorter events, 0.2 us)
Async XLA Ops:
  1.1 6.4 %collective-permute-start.2 = (bf16[8,8,1024]{2,1,0:T(8,128)(2,1)S(1)}, bf16[8,8,1024]{2,1,0:T(8,128)(2,1)S(1)}, u32[]{:S(2)}, u32[]{:S(2)}) collective-permute-start(bf16[8,8,1024]{2,1,0:T(8,128)(2,1)S(1)} %get-tuple-element.20), channel_id=1, source_target_pairs={{0,3},{1,2},{2,1},{3,0},{4,7},{5,6},{6,5},{7,4},{8,11},{9,10},{10,... | collective-permute-start | bytes 393224 | tf_op jit(solution)/shard_map/ppermute | solution.py:118
  3.6 6.9 %collective-permute-start.1 = (bf16[8,8,1024]{2,1,0:T(8,128)(2,1)S(1)}, bf16[8,8,1024]{2,1,0:T(8,128)(2,1)S(1)}, u32[]{:S(2)}, u32[]{:S(2)}) collective-permute-start(bf16[8,8,1024]{2,1,0:T(8,128)(2,1)S(1)} %get-tuple-element.21), channel_id=1, source_target_pairs={{0,2},{1,3},{2,0},{3,1},{4,6},{5,7},{6,4},{7,5},{8,10},{9,11},{10,... | collective-permute-start | bytes 393224 | tf_op jit(solution)/shard_map/ppermute | solution.py:118
  4.3 6.2 %collective-permute-start = (bf16[8,8,1024]{2,1,0:T(8,128)(2,1)S(1)}, bf16[8,8,1024]{2,1,0:T(8,128)(2,1)S(1)}, u32[]{:S(2)}, u32[]{:S(2)}) collective-permute-start(bf16[8,8,1024]{2,1,0:T(8,128)(2,1)S(1)} %get-tuple-element.22), channel_id=1, source_target_pairs={{0,1},{1,0},{2,3},{3,2},{4,5},{5,4},{6,7},{7,6},{8,9},{9,8},{10,11... | collective-permute-start | bytes 393224 | tf_op jit(solution)/shard_map/ppermute | solution.py:118
  11.3 16.4 %collective-permute-start.6 = (bf16[4,8,8,1024]{3,2,1,0:T(8,128)(2,1)S(1)}, bf16[4,8,8,1024]{3,2,1,0:T(8,128)(2,1)S(1)}, u32[]{:S(2)}, u32[]{:S(2)}) collective-permute-start(bf16[4,8,8,1024]{3,2,1,0:T(8,128)(2,1)S(1)} %select_select_fusion), channel_id=1, source_target_pairs={{4,0},{5,1},{6,2},{7,3},{8,4},{9,5},{10,6},{11,7},{12,8},{13,9},{1... | collective-permute-start | bytes 1572872 | tf_op jit(solution)/shard_map/ppermute | solution.py:133
  12.6 16.3 %collective-permute-start.3 = (bf16[4,8,8,1024]{3,2,1,0:T(8,128)(2,1)S(1)}, bf16[4,8,8,1024]{3,2,1,0:T(8,128)(2,1)S(1)}, u32[]{:S(2)}, u32[]{:S(2)}) collective-permute-start(bf16[4,8,8,1024]{3,2,1,0:T(8,128)(2,1)S(1)} %select_select_fusion), channel_id=1, source_target_pairs={{0,4},{1,5},{2,6},{3,7},{4,8},{5,9},{6,10},{7,11},{8,12},{9,13},{1... | collective-permute-start | bytes 1572872 | tf_op jit(solution)/shard_map/ppermute | solution.py:132
  29.0 15.7 %collective-permute-start.7 = (bf16[4,8,8,1024]{3,2,1,0:T(8,128)(2,1)S(1)}, bf16[4,8,8,1024]{3,2,1,0:T(8,128)(2,1)S(1)}, u32[]{:S(2)}, u32[]{:S(2)}) collective-permute-start(bf16[4,8,8,1024]{3,2,1,0:T(8,128)(2,1)S(1)} %get-tuple-element.17), channel_id=1, source_target_pairs={{4,0},{5,1},{6,2},{7,3},{8,4},{9,5},{10,6},{11,7},{12,8},{13,9},{1... | collective-permute-start | bytes 1572872 | tf_op jit(solution)/shard_map/ppermute | solution.py:133
  30.3 33.3 %copy-start.6 = (s32[8]{0:T(128)S(1)}, s32[8]{0:T(128)}, u32[]{:S(2)}) copy-start(s32[8]{0:T(128)} %param.6) | copy-start | bytes 100
  30.3 33.3 %copy-start = (s32[4]{0:T(128)S(1)}, s32[4]{0:T(128)}, u32[]{:S(2)}) copy-start(s32[4]{0:T(128)} %constant.135.clone) | copy-start | bytes 52
  30.4 15.5 %collective-permute-start.4 = (bf16[4,8,8,1024]{3,2,1,0:T(8,128)(2,1)S(1)}, bf16[4,8,8,1024]{3,2,1,0:T(8,128)(2,1)S(1)}, u32[]{:S(2)}, u32[]{:S(2)}) collective-permute-start(bf16[4,8,8,1024]{3,2,1,0:T(8,128)(2,1)S(1)} %get-tuple-element.18), channel_id=1, source_target_pairs={{0,4},{1,5},{2,6},{3,7},{4,8},{5,9},{6,10},{7,11},{8,12},{9,13},{1... | collective-permute-start | bytes 1572872 | tf_op jit(solution)/shard_map/ppermute | solution.py:132
  46.1 14.8 %collective-permute-start.8 = (bf16[4,8,8,1024]{3,2,1,0:T(8,128)(2,1)S(1)}, bf16[4,8,8,1024]{3,2,1,0:T(8,128)(2,1)S(1)}, u32[]{:S(2)}, u32[]{:S(2)}) collective-permute-start(bf16[4,8,8,1024]{3,2,1,0:T(8,128)(2,1)S(1)} %get-tuple-element.15), channel_id=1, source_target_pairs={{4,0},{5,1},{6,2},{7,3},{8,4},{9,5},{10,6},{11,7},{12,8},{13,9},{1... | collective-permute-start | bytes 1572872 | tf_op jit(solution)/shard_map/ppermute | solution.py:133
  47.4 14.7 %collective-permute-start.5 = (bf16[4,8,8,1024]{3,2,1,0:T(8,128)(2,1)S(1)}, bf16[4,8,8,1024]{3,2,1,0:T(8,128)(2,1)S(1)}, u32[]{:S(2)}, u32[]{:S(2)}) collective-permute-start(bf16[4,8,8,1024]{3,2,1,0:T(8,128)(2,1)S(1)} %get-tuple-element.16), channel_id=1, source_target_pairs={{0,4},{1,5},{2,6},{3,7},{4,8},{5,9},{6,10},{7,11},{8,12},{9,13},{1... | collective-permute-start | bytes 1572872 | tf_op jit(solution)/shard_map/ppermute | solution.py:132
  62.2 17.0 %copy-start.3 = (bf16[32,8,1024]{2,1,0:T(8,128)(2,1)S(1)}, bf16[32,8,1024]{2,1,0:T(8,128)(2,1)}, u32[]{:S(2)}) copy-start(bf16[32,8,1024]{2,1,0:T(8,128)(2,1)} %param.4) | copy-start | bytes 1572868
  62.2 11.4 %collective-permute-start.9 = (bf16[1,4,8,8,1024]{4,3,2,1,0:T(8,128)(2,1)S(1)}, bf16[1,4,8,8,1024]{4,3,2,1,0:T(8,128)(2,1)S(1)}, u32[]{:S(2)}, u32[]{:S(2)}) collective-permute-start(bf16[1,4,8,8,1024]{4,3,2,1,0:T(8,128)(2,1)S(1)} %select_bitcast_fusion.1), channel_id=1, source_target_pairs={{0,2},{1,3},{2,0},{3,1},{4,6},{5,7},{6,4},{7,5},{8,10},{9,11},{10,... | collective-permute-start | bytes 1572872 | tf_op jit(solution)/shard_map/ppermute | solution.py:143
  73.7 6.9 %collective-permute-start.10 = (bf16[2,4,8,8,1024]{4,3,2,1,0:T(8,128)(2,1)S(1)}, bf16[2,4,8,8,1024]{4,3,2,1,0:T(8,128)(2,1)S(1)}, u32[]{:S(2)}, u32[]{:S(2)}) collective-permute-start(bf16[2,4,8,8,1024]{4,3,2,1,0:T(8,128)(2,1)S(1)} %pad_maximum_fusion.2), channel_id=1, source_target_pairs={{0,1},{1,0},{2,3},{3,2},{4,5},{5,4},{6,7},{7,6},{8,9},{9,8},{10,11... | collective-permute-start | bytes 3145736 | tf_op jit(solution)/shard_map/ppermute | solution.py:143
  86.4 25.0 %copy-start.4 = (bf16[512,512]{1,0:T(8,128)(2,1)S(1)}, bf16[512,512]{1,0:T(8,128)(2,1)}, u32[]{:S(2)}) copy-start(bf16[512,512]{1,0:T(8,128)(2,1)} %get-tuple-element.27) | copy-start | bytes 1572868
  86.4 25.0 %copy-start.5 = (bf16[512,512]{1,0:T(8,128)(2,1)S(1)}, bf16[512,512]{1,0:T(8,128)(2,1)}, u32[]{:S(2)}) copy-start(bf16[512,512]{1,0:T(8,128)(2,1)} %get-tuple-element.28) | copy-start | bytes 1572868
  122.5 15.6 %copy-start.2 = (f32[1024,512]{1,0:T(8,128)S(1)}, f32[1024,512]{1,0:T(8,128)}, u32[]{:S(2)}) copy-start(f32[1024,512]{1,0:T(8,128)} %get-tuple-element.13) | copy-start | bytes 6291460
  122.5 1.4 collective-permute-start.11
  123.9 3.7 %collective-permute-start.12 = (f32[4,32]{1,0:T(4,128)S(1)}, f32[4,32]{1,0:T(4,128)S(1)}, u32[]{:S(2)}, u32[]{:S(2)}) collective-permute-start(f32[4,32]{1,0:T(4,128)S(1)} %fusion.18), channel_id=1, source_target_pairs={{0,2},{1,3},{2,0},{3,1},{4,6},{5,7},{6,4},{7,5},{8,10},{9,11},{10,... | collective-permute-start | bytes 1544 | tf_op jit(solution)/shard_map/ppermute | solution.py:169
  127.6 4.1 %collective-permute-start.13 = (f32[4,32]{1,0:T(4,128)S(1)}, f32[4,32]{1,0:T(4,128)S(1)}, u32[]{:S(2)}, u32[]{:S(2)}) collective-permute-start(f32[4,32]{1,0:T(4,128)S(1)} %fusion.20), channel_id=1, source_target_pairs={{0,4},{1,5},{2,6},{3,7},{4,0},{5,1},{6,2},{7,3},{8,12},{9,13},{10,... | collective-permute-start | bytes 1544 | tf_op jit(solution)/shard_map/ppermute | solution.py:169
  131.7 4.5 %collective-permute-start.14 = (f32[4,32]{1,0:T(4,128)S(1)}, f32[4,32]{1,0:T(4,128)S(1)}, u32[]{:S(2)}, u32[]{:S(2)}) collective-permute-start(f32[4,32]{1,0:T(4,128)S(1)} %max.14), channel_id=1, source_target_pairs={{0,8},{1,9},{2,10},{3,11},{4,12},{5,13},{6,14},{7,15},{8,0},{9,1},... | collective-permute-start | bytes 1544 | tf_op jit(solution)/shard_map/ppermute | solution.py:169
  138.1 1.6 %copy-start.1 = (f32[1024,512]{1,0:T(8,128)S(1)}, f32[1024,512]{1,0:T(8,128)}, u32[]{:S(2)}) copy-start(f32[1024,512]{1,0:T(8,128)} %get-tuple-element.14) | copy-start | bytes 6291460

commit v4 on v3

--- a/solution.py
+++ b/solution.py
@@ -1,9 +1,12 @@
 import math
 
 import jax
+import ml_dtypes
+import numpy as np
 import jax.numpy as jnp
 from jax import lax
 from jax.experimental import pallas as pl
+from jax.experimental.pallas import tpu as pltpu
 from jax.sharding import PartitionSpec as P
 
 SOURCE = 32
@@ -11,27 +14,27 @@
 
 
 def build_table(bins, lags):
-    freq = jnp.arange(bins, dtype=jnp.int32)[:, None]
-    shifted = jnp.arange(lags, dtype=jnp.int32)[None, :] - lags // 2
-    phase = jnp.remainder(freq * shifted, 2 * bins).astype(jnp.float32)
-    theta = phase * (2.0 * math.pi / (2 * bins))
-    weight = jnp.where(freq == 0, 1.0, 2.0).astype(jnp.float32) / (2 * bins)
-    return jnp.concatenate([weight * jnp.cos(theta), -weight * jnp.sin(theta)], axis=0).astype(
-        jnp.bfloat16
-    )
+    freq = np.arange(bins, dtype=np.int32)[:, None]
+    shifted = np.arange(lags, dtype=np.int32)[None, :] - lags // 2
+    phase = np.remainder(freq * shifted, 2 * bins).astype(np.float32)
+    theta = phase * np.float32(2.0 * math.pi / (2 * bins))
+    weight = (np.where(freq == 0, 1.0, 2.0).astype(np.float32) / np.float32(2 * bins)).astype(np.float32)
+    table = np.concatenate([weight * np.cos(theta), -weight * np.sin(theta)], axis=0).astype(np.float32)
+    return jnp.asarray(table.astype(ml_dtypes.bfloat16))
 
 
 ST = 8
 RC = 16
 
 
-def cross_kernel(src_ref, rcv_ref, out_ref):
+def cross_kernel(order_ref, src_ref, rcv_ref, out_ref):
+    del order_ref
     bins = src_ref.shape[-1] // 2
-    windows = src_ref.shape[2]
+    windows = src_ref.shape[3]
     rows = rcv_ref.shape[1]
 
     def body(s, carry):
-        row = src_ref[0, s].astype(jnp.float32)
+        row = src_ref[0, 0, s].astype(jnp.float32)
         for c in range(rows // RC):
             rs = slice(c * RC, (c + 1) * RC)
             acc_re = jnp.zeros((RC, bins), jnp.float32)
@@ -47,30 +50,32 @@
             out_ref[0, s, rs, bins:] = acc_im.astype(out_ref.dtype)
         return carry
 
-    lax.fori_loop(0, src_ref.shape[1], body, 0)
-
-
-def cross_products(src_all, rcv):
-    nb, sources, windows, width = src_all.shape
-    receivers = rcv.shape[0]
-    rcv_t = jnp.transpose(rcv, (1, 0, 2)).astype(jnp.float32)
+    lax.fori_loop(0, src_ref.shape[2], body, 0)
+
+
+def cross_products(stack, order, rcv_t):
+    qc, nb, piece, windows, width = stack.shape
+    receivers = rcv_t.shape[1]
+    sources = qc * piece
     flops = 8 * nb * sources * receivers * windows * (width // 2)
     return pl.pallas_call(
         cross_kernel,
-        grid=(nb, sources // ST),
-        in_specs=[
-            pl.BlockSpec((1, ST, windows, width), lambda k, i: (k, i, 0, 0)),
-            pl.BlockSpec((windows, receivers, width), lambda k, i: (0, 0, 0)),
-        ],
-        out_specs=pl.BlockSpec((1, ST, receivers, width), lambda k, i: (k, i, 0, 0)),
+        grid_spec=pltpu.PrefetchScalarGridSpec(
+            num_scalar_prefetch=1,
+            grid=(nb, qc),
+            in_specs=[
+                pl.BlockSpec((1, 1, piece, windows, width), lambda k, i, o: (o[i], k, 0, 0, 0)),
+                pl.BlockSpec((windows, receivers, width), lambda k, i, o: (0, 0, 0)),
+            ],
+            out_specs=pl.BlockSpec((1, piece, receivers, width), lambda k, i, o: (k, i, 0, 0)),
+        ),
         out_shape=jax.ShapeDtypeStruct((nb, sources, receivers, width), jnp.bfloat16),
         cost_estimate=pl.CostEstimate(
             flops=flops,
-            bytes_accessed=src_all.size * 2 + rcv_t.size * 4 + nb * sources * receivers * width * 2,
+            bytes_accessed=stack.size * 2 + rcv_t.size * 4 + nb * sources * receivers * width * 2,
             transcendentals=0,
         ),
-    )(src_all, rcv_t)
-
+    )(order, stack, rcv_t)
 
 def plane_size(mesh):
     devs = list(mesh.devices[0])
@@ -149,25 +154,30 @@
         inv = [0] * qc
         for e, o in enumerate(offs):
             inv[o] = e
-        inv = jnp.array(inv, jnp.int32)
-        order = jnp.take(inv, jnp.arange(qc, dtype=jnp.int32) ^ q)
-        full = jnp.take(stack, order, axis=0)
-        src_all = jnp.transpose(full, (1, 0, 2, 3, 4)).reshape(nb, SOURCE, windows, width)
+        order = jnp.take(jnp.array(inv, jnp.int32), jnp.arange(qc, dtype=jnp.int32) ^ q)
 
         lag_table = build_table(bins, LAGS)
-        window_mask = window_valid.astype(jnp.bfloat16)[None, None, :, None]
-        src_all = src_all * window_mask
-        cross = cross_products(src_all, spectra)
+        window_mask = window_valid.astype(jnp.float32)[:, None, None]
+        rcv_t = jnp.transpose(spectra, (1, 0, 2)).astype(jnp.float32) * window_mask
+        cross = cross_products(stack, order, rcv_t)
         traces = jnp.dot(
             cross.reshape(nb * SOURCE * receivers, width), lag_table, preferred_element_type=jnp.float32
         ).reshape(nb, SOURCE, receivers, LAGS)
         traces_all = [traces[k] for k in range(nb)]
         peaks = [jnp.max(jnp.abs(traces[k]), axis=(1, 2)) for k in range(nb)]
         peak = jnp.stack(peaks)
-        d = 1
-        while d < n:
-            peak = jnp.maximum(peak, lax.ppermute(peak, "chan", pairs_of(n, lambda i, d=d: i ^ d)))
-            d *= 2
+        got = [
+            lax.ppermute(peak, "chan", pairs_of(n, lambda i, d=d: (i // qc) * qc + ((i % qc) ^ d)))
+            for d in range(1, qc)
+        ]
+        for g in got:
+            peak = jnp.maximum(peak, g)
+        got = [
+            lax.ppermute(peak, "chan", pairs_of(n, lambda i, d=d: ((i // qc + d) % zc) * qc + i % qc))
+            for d in range(1, zc)
+        ]
+        for g in got:
+            peak = jnp.maximum(peak, g)
         out = [
             (traces_all[k] / (peak[k][:, None, None] + 1e-06)).astype(jnp.bfloat16) for k in range(nb)
         ]

time: 143 us -> 136 us (0.951)
  other arithmetic: 20.4 us -> 15.5 us
  local copies, waits for them, and re-layouts: 7.63 us -> 4.17 us
    another operation x1 -> x0, other arithmetic: 5.4 us -> none
    another operation x2, other arithmetic: 0.37 us -> 2.9 us  [shards(): stack = jnp.stack(held)]
    gather x2 -> x1, local copies, waits for them, and re-layouts: 2.64 us -> 0.64 us  [shards(): jnp.take(jnp.array(inv, jnp.int32), jnp.arange(qc, dtype=jnp.int32) ^ q)]
    convert_element_type x4 -> x2, other arithmetic: 2.92 us -> 3.71 us  [shards(): (traces_all[k] / (peak[k][:, None, None] + 1e-06)).astype(jnp.bfloat16)]
    ppermute x4 -> x6, waiting for transfers between devices: 6.46 us -> 5.95 us  [the longest x3 4 us: shards(): lax.ppermute(peak, 'chan', pairs_of(n, lambda i, d=d: (i // qc + d) % zc...]
    ppermute x4 -> x6, starting transfers between devices: 7.16 us -> 7.65 us  [the longest x3 5.44 us: shards(): lax.ppermute(peak, 'chan', pairs_of(n, lambda i, d=d: (i // qc + d) % zc...]
  transfers between devices with their start and end apart: 15 -> 17, of which waited for: 13 -> 14; matrix products, arithmetic and copies ran while one was open for 6% -> 3% of each run, Pallas kernels for 0% -> 0%
where the time goes in v4:
time: 136 us
  waiting for transfers between devices  52.1 us (38%)
  starting transfers between devices  31.2 us (23%)
  Pallas kernels  25.8 us (19%)
  other arithmetic  15.5 us (11%)
  matrix products  6.89 us (5%)
  local copies, waits for them, and re-layouts  4.17 us (3%)
    ppermute x3, waiting for transfers between devices, shards(): rec_down = lax.ppermute(cur_down, 'chan', down_pairs)  27.9 us
    pallas_call x1, Pallas kernels, cross_products(): pl.pallas_call(cross_kernel, grid_spec=pltpu.PrefetchScalarGridSpec(num_s...  25.8 us
    ppermute x3, starting transfers between devices, shards(): rec_up = lax.ppermute(cur_up, 'chan', up_pairs)  15 us
    ppermute x2, waiting for transfers between devices, shards(): lax.ppermute(jnp.stack(held), 'chan', pairs_of(n, lambda i, b=b: i // qc...  10.1 us
    dot_general x1, matrix products, shards(): jnp.dot(cross.reshape(nb * SOURCE * receivers, width), lag_table, preferr...  6.89 us
    ppermute x3, starting transfers between devices, shards(): lax.ppermute(peak, 'chan', pairs_of(n, lambda i, d=d: (i // qc + d) % zc...  5.44 us
    ppermute x3, waiting for transfers between devices, shards(): lax.ppermute(send, 'chan', pairs_of(n, lambda i, d=d: i // qc * qc + (i %...  4.6 us
    ppermute x3, waiting for transfers between devices, shards(): lax.ppermute(peak, 'chan', pairs_of(n, lambda i, d=d: (i // qc + d) % zc...  4 us
  transfers between devices with their start and end apart: 17, of which 14 were waited for; matrix products, arithmetic and copies ran while one was open for 3% of the time, Pallas kernels for 0%

profile of v4, /device:TPU:0, one launch (start us, length us, event | category | flops | bytes accessed | tf_op | source)
XLA Modules:
  0.0 135.9 jit_solution(14903867465491597432)
XLA Ops:
  0.0 1.1 constant_dynamic-slice_fusion
  1.1 2.5 %collective-permute-start.2 = (bf16[8,8,1024]{2,1,0:T(8,128)(2,1)S(1)}, bf16[8,8,1024]{2,1,0:T(8,128)(2,1)S(1)}, u32[]{:S(2)}, u32[]{:S(2)}) collective-permute-start(bf16[8,8,1024]{2,1,0:T(8,128)(2,1)S(1)} %get-tuple-element.20), channel_id=1, source_target_pairs={{0,3},{1,2},{2,1},{3,0},{4,7},{5,6},{6,5},{7,4},{8,11},{9,10},{10,... | collective-permute-start | bytes 393224 | tf_op jit(solution)/shard_map/ppermute | solution.py:123
  3.6 0.6 collective-permute-start.1
  4.3 0.0 collective-permute-start
  4.3 0.8 reshape.248
  5.1 0.8 reshape.246
  5.9 1.6 %collective-permute-done.2 = bf16[8,8,1024]{2,1,0:T(8,128)(2,1)S(1)} collective-permute-done((bf16[8,8,1024]{2,1,0:T(8,128)(2,1)S(1)}, bf16[8,8,1024]{2,1,0:T(8,128)(2,1)S(1)}, u32[]{:S(2)}, u32[]{:S(2)}) %collective-permute-start.2) | collective-permute-done | bytes 131104 | tf_op jit(solution)/shard_map/ppermute | solution.py:123
  7.5 3.0 %collective-permute-done.1 = bf16[8,8,1024]{2,1,0:T(8,128)(2,1)S(1)} collective-permute-done((bf16[8,8,1024]{2,1,0:T(8,128)(2,1)S(1)}, bf16[8,8,1024]{2,1,0:T(8,128)(2,1)S(1)}, u32[]{:S(2)}, u32[]{:S(2)}) %collective-permute-start.1) | collective-permute-done | bytes 131104 | tf_op jit(solution)/shard_map/ppermute | solution.py:123
  10.5 0.0 collective-permute-done
  10.5 0.1 pad_maximum_fusion.3
  10.6 0.6 gather_fusion.1
  11.2 0.1 select_select_fusion
  11.3 1.3 collective-permute-start.6
  12.6 4.9 %collective-permute-start.3 = (bf16[4,8,8,1024]{3,2,1,0:T(8,128)(2,1)S(1)}, bf16[4,8,8,1024]{3,2,1,0:T(8,128)(2,1)S(1)}, u32[]{:S(2)}, u32[]{:S(2)}) collective-permute-start(bf16[4,8,8,1024]{3,2,1,0:T(8,128)(2,1)S(1)} %select_select_fusion), channel_id=1, source_target_pairs={{0,4},{1,5},{2,6},{3,7},{4,8},{5,9},{6,10},{7,11},{8,12},{9,13},{1... | collective-permute-start | bytes 1572872 | tf_op jit(solution)/shard_map/ppermute | solution.py:137
  17.5 10.2 %collective-permute-done.6 = bf16[4,8,8,1024]{3,2,1,0:T(8,128)(2,1)S(1)} collective-permute-done((bf16[4,8,8,1024]{3,2,1,0:T(8,128)(2,1)S(1)}, bf16[4,8,8,1024]{3,2,1,0:T(8,128)(2,1)S(1)}, u32[]{:S(2)}, u32[]{:S(2)}) %collective-permute-start.6) | collective-permute-done | bytes 524320 | tf_op jit(solution)/shard_map/ppermute | solution.py:138
  27.7 1.2 collective-permute-done.3
  28.9 0.2 broadcast_select_fusion.1
  29.0 1.3 collective-permute-start.7
  30.3 5.0 %collective-permute-start.4 = (bf16[4,8,8,1024]{3,2,1,0:T(8,128)(2,1)S(1)}, bf16[4,8,8,1024]{3,2,1,0:T(8,128)(2,1)S(1)}, u32[]{:S(2)}, u32[]{:S(2)}) collective-permute-start(bf16[4,8,8,1024]{3,2,1,0:T(8,128)(2,1)S(1)} %get-tuple-element.18), channel_id=1, source_target_pairs={{0,4},{1,5},{2,6},{3,7},{4,8},{5,9},{6,10},{7,11},{8,12},{9,13},{1... | collective-permute-start | bytes 1572872 | tf_op jit(solution)/shard_map/ppermute | solution.py:137
  35.4 9.3 %collective-permute-done.7 = bf16[4,8,8,1024]{3,2,1,0:T(8,128)(2,1)S(1)} collective-permute-done((bf16[4,8,8,1024]{3,2,1,0:T(8,128)(2,1)S(1)}, bf16[4,8,8,1024]{3,2,1,0:T(8,128)(2,1)S(1)}, u32[]{:S(2)}, u32[]{:S(2)}) %collective-permute-start.7) | collective-permute-done | bytes 524320 | tf_op jit(solution)/shard_map/ppermute | solution.py:138
  44.7 1.2 collective-permute-done.4
  45.9 0.2 broadcast_select_fusion
  46.0 1.3 collective-permute-start.8
  47.3 5.0 %collective-permute-start.5 = (bf16[4,8,8,1024]{3,2,1,0:T(8,128)(2,1)S(1)}, bf16[4,8,8,1024]{3,2,1,0:T(8,128)(2,1)S(1)}, u32[]{:S(2)}, u32[]{:S(2)}) collective-permute-start(bf16[4,8,8,1024]{3,2,1,0:T(8,128)(2,1)S(1)} %get-tuple-element.16), channel_id=1, source_target_pairs={{0,4},{1,5},{2,6},{3,7},{4,8},{5,9},{6,10},{7,11},{8,12},{9,13},{1... | collective-permute-start | bytes 1572872 | tf_op jit(solution)/shard_map/ppermute | solution.py:137
  52.4 8.4 %collective-permute-done.8 = bf16[4,8,8,1024]{3,2,1,0:T(8,128)(2,1)S(1)} collective-permute-done((bf16[4,8,8,1024]{3,2,1,0:T(8,128)(2,1)S(1)}, bf16[4,8,8,1024]{3,2,1,0:T(8,128)(2,1)S(1)}, u32[]{:S(2)}, u32[]{:S(2)}) %collective-permute-start.8) | collective-permute-done | bytes 524320 | tf_op jit(solution)/shard_map/ppermute | solution.py:138
  60.8 1.2 collective-permute-done.5
  62.0 0.2 select_bitcast_fusion
  62.2 1.4 %collective-permute-start.9 = (bf16[1,4,8,8,1024]{4,3,2,1,0:T(8,128)(2,1)S(1)}, bf16[1,4,8,8,1024]{4,3,2,1,0:T(8,128)(2,1)S(1)}, u32[]{:S(2)}, u32[]{:S(2)}) collective-permute-start(bf16[1,4,8,8,1024]{4,3,2,1,0:T(8,128)(2,1)S(1)} %select_bitcast_fusion), channel_id=1, source_target_pairs={{0,2},{1,3},{2,0},{3,1},{4,6},{5,7},{6,4},{7,5},{8,10},{9,11},{10,... | collective-permute-start | bytes 1572872 | tf_op jit(solution)/shard_map/ppermute | solution.py:148
  63.5 10.0 %collective-permute-done.9 = bf16[1,4,8,8,1024]{4,3,2,1,0:T(8,128)(2,1)S(1)} collective-permute-done((bf16[1,4,8,8,1024]{4,3,2,1,0:T(8,128)(2,1)S(1)}, bf16[1,4,8,8,1024]{4,3,2,1,0:T(8,128)(2,1)S(1)}, u32[]{:S(2)}, u32[]{:S(2)}) %collective-permute-start.9) | collective-permute-done | bytes 524320 | tf_op jit(solution)/shard_map/ppermute | solution.py:148
  73.5 0.1 pad_maximum_fusion.2
  73.7 0.1 collective-permute-start.10
  73.8 0.6 gather_fusion
  74.4 0.6 and_select_fusion.3.order_ref
  75.0 1.4 %multiply_bitcast_fusion.rcv_ref = f32[8,32,1024]{2,1,0:T(8,128)} fusion(bf16[32,8,1024]{2,1,0:T(8,128)(2,1)S(1)} %copy-done.2, f32[8]{0:T(128)S(1)} %convert_element_type.48), kind=kLoop, calls=%fused_computation.13 | loop fusion | flops 524288 | bytes 1572896 | tf_op jit(solution)/shard_map/mul | solution.py:161
  76.4 0.1 collective-permute-done.10
  76.5 2.7 %pad_maximum_fusion.1.src_ref = bf16[4,4,8,8,1024]{4,3,2,1,0:T(8,128)(2,1)} fusion(bf16[2,4,8,8,1024]{4,3,2,1,0:T(8,128)(2,1)} %collective-permute-done.10, bf16[1,4,8,8,1024]{4,3,2,1,0:T(8,128)(2,1)S(1)} %collective-permute-done.9, bf16[1,4,8,8,1024]{4,3,2,1,0:T(8,128)(2,1)S(1)} %select_bitcast_fusion), kind=kLoop, calls=%fused_computation.3 | loop fusion | flops 2097152 | bytes 4194304 | tf_op jit(solution)/shard_map/stack | solution.py:153
  79.3 25.8 %shard_map.55 = bf16[4,32,32,1024]{3,2,1,0:T(8,128)(2,1)} custom-call(s32[4]{0:T(128)} %and_select_fusion.3.order_ref, bf16[4,4,8,8,1024]{4,3,2,1,0:T(8,128)(2,1)} %pad_maximum_fusion.1.src_ref, f32[8,32,1024]{2,1,0:T(8,128)} %multiply_bitcast_fusion.rcv_ref), custom_call_target="tpu_custom_call" | custom-call | flops 134217728 | bytes 11534336 | tf_op jit(solution)/shard_map/pallas_call | solution.py:61
  105.1 0.0 copy-done.4
  105.1 6.9 %fusion.5 = f32[4096,512]{1,0:T(8,128)S(1)} fusion(bf16[4096,1024]{1,0:T(8,128)(2,1)} %bitcast.42, bf16[1024,512]{1,0:T(8,128)(2,1)S(1)} %copy-done.4), kind=kOutput, calls=%fused_computation.55 | convolution fusion | flops 4294967296 | bytes 17825792 | tf_op jit(solution)/shard_map/dot_general | solution.py:163
  112.0 3.4 %abs_reduce_fusion.3 = (f32[1024]{0:T(1024)S(1)}, f32[1024]{0:T(1024)S(1)}, f32[1024]{0:T(1024)S(1)}, f32[1024]{0:T(1024)S(1)}, f32[1024,512]{1,0:T(8,128)S(1)},...) fusion(f32[4096,512]{1,0:T(8,128)S(1)} %fusion.5), kind=kLoop, calls=%fused_computation.11 | loop fusion | flops 4190208 | bytes 16793600 | tf_op jit(solution)/shard_map/reduce_max | solution.py:167
  115.4 0.1 reduce_max.47
  115.5 0.1 reduce_max.53
  115.6 0.1 reduce_max.51
  115.7 0.1 reduce_max.54
  115.8 0.1 reduce_max.59
  115.9 0.1 reduce_max.72
  116.0 0.1 reduce_max.74
  116.1 0.1 reduce_max.75
  116.2 1.1 collective-permute-start.12
  117.4 0.6 collective-permute-start.13
  118.0 0.4 collective-permute-start.11
  118.4 1.4 %collective-permute-done.12 = f32[4,32]{1,0:T(4,128)S(1)} collective-permute-done((f32[4,32]{1,0:T(4,128)S(1)}, f32[4,32]{1,0:T(4,128)S(1)}, u32[]{:S(2)}, u32[]{:S(2)}) %collective-permute-start.12) | collective-permute-done | bytes 544 | tf_op jit(solution)/shard_map/ppermute | solution.py:170
  119.9 0.5 collective-permute-done.13
  120.4 0.0 collective-permute-done.11
  120.4 4.1 %collective-permute-start.16 = (f32[4,32]{1,0:T(4,128)S(1)}, f32[4,32]{1,0:T(4,128)S(1)}, u32[]{:S(2)}, u32[]{:S(2)}) collective-permute-start(f32[4,32]{1,0:T(4,128)S(1)} %maximum_maximum_fusion.1), channel_id=1, source_target_pairs={{0,12},{1,13},{2,14},{3,15},{4,0},{5,1},{6,2},{7,3},{8,4},{9,5},{1... | collective-permute-start | bytes 1544 | tf_op jit(solution)/shard_map/ppermute | solution.py:176
  124.5 0.0 collective-permute-start.15
  124.5 1.4 %collective-permute-start.14 = (f32[4,32]{1,0:T(4,128)S(1)}, f32[4,32]{1,0:T(4,128)S(1)}, u32[]{:S(2)}, u32[]{:S(2)}) collective-permute-start(f32[4,32]{1,0:T(4,128)S(1)} %maximum_maximum_fusion.1), channel_id=1, source_target_pairs={{0,4},{1,5},{2,6},{3,7},{4,8},{5,9},{6,10},{7,11},{8,12},{9,13},{1... | collective-permute-start | bytes 1544 | tf_op jit(solution)/shard_map/ppermute | solution.py:176
  125.8 0.0 collective-permute-done.16
  125.8 3.1 %collective-permute-done.15 = f32[4,32]{1,0:T(4,128)S(1)} collective-permute-done((f32[4,32]{1,0:T(4,128)S(1)}, f32[4,32]{1,0:T(4,128)S(1)}, u32[]{:S(2)}, u32[]{:S(2)}) %collective-permute-start.15) | collective-permute-done | bytes 544 | tf_op jit(solution)/shard_map/ppermute | solution.py:176
  128.9 0.9 collective-permute-done.14
  129.9 0.0 copy-start.1
  129.9 3.0 %divide_convert_fusion = (bf16[1,32,32,512]{3,2,1,0:T(8,128)(2,1)S(1)}, bf16[1,32,32,512]{3,2,1,0:T(8,128)(2,1)S(1)}) fusion(f32[1,32,32,512]{3,2,1,0:T(8,128)} %bitcast.41, f32[32]{0:T(128)S(1)} %get-tuple-element.24, f32[1,32,32,512]{3,2,1,0:T(8,128)} %bitcast.40, f32[32]{0:T(128)S(1)} %get-tuple-element.25), kind=kLoop, calls=%fused_computation.4 | loop fusion | flops 2097152 | bytes 6291712 | tf_op jit(solution)/shard_map/convert_element_type | solution.py:182
  132.9 0.7 divide_convert_fusion.2
  133.6 2.3 %pad_maximum_fusion = bf16[4,32,32,512]{3,2,1,0:T(8,128)(2,1)} fusion(bf16[1,32,32,512]{3,2,1,0:T(8,128)(2,1)S(1)} %get-tuple-element.28, bf16[1,32,32,512]{3,2,1,0:T(8,128)(2,1)S(1)} %get-tuple-element.29, bf16[1,32,32,512]{3,2,1,0:T(8,128)(2,1)S(1)} %get-tuple-element.30, bf16[1,32,32,512]{3,2,1,0:T(8,128)(2,1)S(1)} %get-tuple-element.31), kind=kLoop, calls=%fused_computation.2 | loop fusion | flops 6291456 | bytes 8388608 | tf_op jit(solution)/shard_map/stack | solution.py:184
  (19 shorter events, 0.1 us)
Async XLA Ops:
  1.1 6.4 %collective-permute-start.2 = (bf16[8,8,1024]{2,1,0:T(8,128)(2,1)S(1)}, bf16[8,8,1024]{2,1,0:T(8,128)(2,1)S(1)}, u32[]{:S(2)}, u32[]{:S(2)}) collective-permute-start(bf16[8,8,1024]{2,1,0:T(8,128)(2,1)S(1)} %get-tuple-element.20), channel_id=1, source_target_pairs={{0,3},{1,2},{2,1},{3,0},{4,7},{5,6},{6,5},{7,4},{8,11},{9,10},{10,... | collective-permute-start | bytes 393224 | tf_op jit(solution)/shard_map/ppermute | solution.py:123
  3.6 6.9 %collective-permute-start.1 = (bf16[8,8,1024]{2,1,0:T(8,128)(2,1)S(1)}, bf16[8,8,1024]{2,1,0:T(8,128)(2,1)S(1)}, u32[]{:S(2)}, u32[]{:S(2)}) collective-permute-start(bf16[8,8,1024]{2,1,0:T(8,128)(2,1)S(1)} %get-tuple-element.21), channel_id=1, source_target_pairs={{0,2},{1,3},{2,0},{3,1},{4,6},{5,7},{6,4},{7,5},{8,10},{9,11},{10,... | collective-permute-start | bytes 393224 | tf_op jit(solution)/shard_map/ppermute | solution.py:123
  4.3 6.2 %collective-permute-start = (bf16[8,8,1024]{2,1,0:T(8,128)(2,1)S(1)}, bf16[8,8,1024]{2,1,0:T(8,128)(2,1)S(1)}, u32[]{:S(2)}, u32[]{:S(2)}) collective-permute-start(bf16[8,8,1024]{2,1,0:T(8,128)(2,1)S(1)} %get-tuple-element.22), channel_id=1, source_target_pairs={{0,1},{1,0},{2,3},{3,2},{4,5},{5,4},{6,7},{7,6},{8,9},{9,8},{10,11... | collective-permute-start | bytes 393224 | tf_op jit(solution)/shard_map/ppermute | solution.py:123
  11.3 16.4 %collective-permute-start.6 = (bf16[4,8,8,1024]{3,2,1,0:T(8,128)(2,1)S(1)}, bf16[4,8,8,1024]{3,2,1,0:T(8,128)(2,1)S(1)}, u32[]{:S(2)}, u32[]{:S(2)}) collective-permute-start(bf16[4,8,8,1024]{3,2,1,0:T(8,128)(2,1)S(1)} %select_select_fusion), channel_id=1, source_target_pairs={{4,0},{5,1},{6,2},{7,3},{8,4},{9,5},{10,6},{11,7},{12,8},{13,9},{1... | collective-permute-start | bytes 1572872 | tf_op jit(solution)/shard_map/ppermute | solution.py:138
  12.6 16.3 %collective-permute-start.3 = (bf16[4,8,8,1024]{3,2,1,0:T(8,128)(2,1)S(1)}, bf16[4,8,8,1024]{3,2,1,0:T(8,128)(2,1)S(1)}, u32[]{:S(2)}, u32[]{:S(2)}) collective-permute-start(bf16[4,8,8,1024]{3,2,1,0:T(8,128)(2,1)S(1)} %select_select_fusion), channel_id=1, source_target_pairs={{0,4},{1,5},{2,6},{3,7},{4,8},{5,9},{6,10},{7,11},{8,12},{9,13},{1... | collective-permute-start | bytes 1572872 | tf_op jit(solution)/shard_map/ppermute | solution.py:137
  29.0 15.7 %collective-permute-start.7 = (bf16[4,8,8,1024]{3,2,1,0:T(8,128)(2,1)S(1)}, bf16[4,8,8,1024]{3,2,1,0:T(8,128)(2,1)S(1)}, u32[]{:S(2)}, u32[]{:S(2)}) collective-permute-start(bf16[4,8,8,1024]{3,2,1,0:T(8,128)(2,1)S(1)} %get-tuple-element.17), channel_id=1, source_target_pairs={{4,0},{5,1},{6,2},{7,3},{8,4},{9,5},{10,6},{11,7},{12,8},{13,9},{1... | collective-permute-start | bytes 1572872 | tf_op jit(solution)/shard_map/ppermute | solution.py:138
  30.3 15.5 %collective-permute-start.4 = (bf16[4,8,8,1024]{3,2,1,0:T(8,128)(2,1)S(1)}, bf16[4,8,8,1024]{3,2,1,0:T(8,128)(2,1)S(1)}, u32[]{:S(2)}, u32[]{:S(2)}) collective-permute-start(bf16[4,8,8,1024]{3,2,1,0:T(8,128)(2,1)S(1)} %get-tuple-element.18), channel_id=1, source_target_pairs={{0,4},{1,5},{2,6},{3,7},{4,8},{5,9},{6,10},{7,11},{8,12},{9,13},{1... | collective-permute-start | bytes 1572872 | tf_op jit(solution)/shard_map/ppermute | solution.py:137
  46.0 14.8 %collective-permute-start.8 = (bf16[4,8,8,1024]{3,2,1,0:T(8,128)(2,1)S(1)}, bf16[4,8,8,1024]{3,2,1,0:T(8,128)(2,1)S(1)}, u32[]{:S(2)}, u32[]{:S(2)}) collective-permute-start(bf16[4,8,8,1024]{3,2,1,0:T(8,128)(2,1)S(1)} %get-tuple-element.15), channel_id=1, source_target_pairs={{4,0},{5,1},{6,2},{7,3},{8,4},{9,5},{10,6},{11,7},{12,8},{13,9},{1... | collective-permute-start | bytes 1572872 | tf_op jit(solution)/shard_map/ppermute | solution.py:138
  47.3 14.7 %collective-permute-start.5 = (bf16[4,8,8,1024]{3,2,1,0:T(8,128)(2,1)S(1)}, bf16[4,8,8,1024]{3,2,1,0:T(8,128)(2,1)S(1)}, u32[]{:S(2)}, u32[]{:S(2)}) collective-permute-start(bf16[4,8,8,1024]{3,2,1,0:T(8,128)(2,1)S(1)} %get-tuple-element.16), channel_id=1, source_target_pairs={{0,4},{1,5},{2,6},{3,7},{4,8},{5,9},{6,10},{7,11},{8,12},{9,13},{1... | collective-permute-start | bytes 1572872 | tf_op jit(solution)/shard_map/ppermute | solution.py:137
  62.0 11.7 %copy-start.3 = (s32[8]{0:T(128)S(1)}, s32[8]{0:T(128)}, u32[]{:S(2)}) copy-start(s32[8]{0:T(128)} %param.7) | copy-start | bytes 100
  62.0 11.8 %copy-start = (s32[4]{0:T(128)S(1)}, s32[4]{0:T(128)}, u32[]{:S(2)}) copy-start(s32[4]{0:T(128)} %constant.98.clone) | copy-start | bytes 52
  62.0 13.0 %copy-start.2 = (bf16[32,8,1024]{2,1,0:T(8,128)(2,1)S(1)}, bf16[32,8,1024]{2,1,0:T(8,128)(2,1)}, u32[]{:S(2)}) copy-start(bf16[32,8,1024]{2,1,0:T(8,128)(2,1)} %param.5) | copy-start | bytes 1572868
  62.2 11.4 %collective-permute-start.9 = (bf16[1,4,8,8,1024]{4,3,2,1,0:T(8,128)(2,1)S(1)}, bf16[1,4,8,8,1024]{4,3,2,1,0:T(8,128)(2,1)S(1)}, u32[]{:S(2)}, u32[]{:S(2)}) collective-permute-start(bf16[1,4,8,8,1024]{4,3,2,1,0:T(8,128)(2,1)S(1)} %select_bitcast_fusion), channel_id=1, source_target_pairs={{0,2},{1,3},{2,0},{3,1},{4,6},{5,7},{6,4},{7,5},{8,10},{9,11},{10,... | collective-permute-start | bytes 1572872 | tf_op jit(solution)/shard_map/ppermute | solution.py:148
  73.7 2.9 %collective-permute-start.10 = (bf16[2,4,8,8,1024]{4,3,2,1,0:T(8,128)(2,1)S(1)}, bf16[2,4,8,8,1024]{4,3,2,1,0:T(8,128)(2,1)}, u32[]{:S(2)}, u32[]{:S(2)}) collective-permute-start(bf16[2,4,8,8,1024]{4,3,2,1,0:T(8,128)(2,1)S(1)} %pad_maximum_fusion.2), channel_id=1, source_target_pairs={{0,1},{1,0},{2,3},{3,2},{4,5},{5,4},{6,7},{7,6},{8,9},{9,8},{10,11... | collective-permute-start | bytes 3145736 | tf_op jit(solution)/shard_map/ppermute | solution.py:148
  79.3 25.8 %copy-start.4 = (bf16[1024,512]{1,0:T(8,128)(2,1)S(1)}, bf16[1024,512]{1,0:T(8,128)(2,1)}, u32[]{:S(2)}) copy-start(bf16[1024,512]{1,0:T(8,128)(2,1)} %constant.99.clone) | copy-start | bytes 3145732
  116.2 3.7 %collective-permute-start.12 = (f32[4,32]{1,0:T(4,128)S(1)}, f32[4,32]{1,0:T(4,128)S(1)}, u32[]{:S(2)}, u32[]{:S(2)}) collective-permute-start(f32[4,32]{1,0:T(4,128)S(1)} %pad_maximum_fusion.4), channel_id=1, source_target_pairs={{0,2},{1,3},{2,0},{3,1},{4,6},{5,7},{6,4},{7,5},{8,10},{9,11},{10,... | collective-permute-start | bytes 1544 | tf_op jit(solution)/shard_map/ppermute | solution.py:170
  117.4 3.0 %collective-permute-start.13 = (f32[4,32]{1,0:T(4,128)S(1)}, f32[4,32]{1,0:T(4,128)S(1)}, u32[]{:S(2)}, u32[]{:S(2)}) collective-permute-start(f32[4,32]{1,0:T(4,128)S(1)} %pad_maximum_fusion.4), channel_id=1, source_target_pairs={{0,3},{1,2},{2,1},{3,0},{4,7},{5,6},{6,5},{7,4},{8,11},{9,10},{10,... | collective-permute-start | bytes 1544 | tf_op jit(solution)/shard_map/ppermute | solution.py:170
  118.0 2.4 %collective-permute-start.11 = (f32[4,32]{1,0:T(4,128)S(1)}, f32[4,32]{1,0:T(4,128)S(1)}, u32[]{:S(2)}, u32[]{:S(2)}) collective-permute-start(f32[4,32]{1,0:T(4,128)S(1)} %pad_maximum_fusion.4), channel_id=1, source_target_pairs={{0,1},{1,0},{2,3},{3,2},{4,5},{5,4},{6,7},{7,6},{8,9},{9,8},{10,11... | collective-permute-start | bytes 1544 | tf_op jit(solution)/shard_map/ppermute | solution.py:170
  120.4 5.4 %collective-permute-start.16 = (f32[4,32]{1,0:T(4,128)S(1)}, f32[4,32]{1,0:T(4,128)S(1)}, u32[]{:S(2)}, u32[]{:S(2)}) collective-permute-start(f32[4,32]{1,0:T(4,128)S(1)} %maximum_maximum_fusion.1), channel_id=1, source_target_pairs={{0,12},{1,13},{2,14},{3,15},{4,0},{5,1},{6,2},{7,3},{8,4},{9,5},{1... | collective-permute-start | bytes 1544 | tf_op jit(solution)/shard_map/ppermute | solution.py:176
  124.5 4.5 %collective-permute-start.15 = (f32[4,32]{1,0:T(4,128)S(1)}, f32[4,32]{1,0:T(4,128)S(1)}, u32[]{:S(2)}, u32[]{:S(2)}) collective-permute-start(f32[4,32]{1,0:T(4,128)S(1)} %maximum_maximum_fusion.1), channel_id=1, source_target_pairs={{0,8},{1,9},{2,10},{3,11},{4,12},{5,13},{6,14},{7,15},{8,0},{9,1},... | collective-permute-start | bytes 1544 | tf_op jit(solution)/shard_map/ppermute | solution.py:176
  124.5 5.4 %collective-permute-start.14 = (f32[4,32]{1,0:T(4,128)S(1)}, f32[4,32]{1,0:T(4,128)S(1)}, u32[]{:S(2)}, u32[]{:S(2)}) collective-permute-start(f32[4,32]{1,0:T(4,128)S(1)} %maximum_maximum_fusion.1), channel_id=1, source_target_pairs={{0,4},{1,5},{2,6},{3,7},{4,8},{5,9},{6,10},{7,11},{8,12},{9,13},{1... | collective-permute-start | bytes 1544 | tf_op jit(solution)/shard_map/ppermute | solution.py:176
  129.9 3.0 %copy-start.1 = (f32[1024,512]{1,0:T(8,128)S(1)}, f32[1024,512]{1,0:T(8,128)}, u32[]{:S(2)}) copy-start(f32[1024,512]{1,0:T(8,128)} %get-tuple-element.12) | copy-start | bytes 6291460

commit v5 on v4

--- a/solution.py
+++ b/solution.py
@@ -128,19 +128,28 @@
         sel = jnp.take(by_off, qk ^ q, axis=0)
         payload = jnp.where(here[:, None, None, None], sel, jnp.zeros_like(sel))
 
-        up_pairs = pairs_of(n, lambda i: i + qc if i // qc < zc - 1 else None)
-        down_pairs = pairs_of(n, lambda i: i - qc if i // qc > 0 else None)
         mask = here[:, None, None, None]
-        cur_up, cur_down = payload, payload
-        rec_up, rec_down = payload, payload
-        for r in range(zc - 1):
-            rec_up = lax.ppermute(cur_up, "chan", up_pairs)
-            rec_down = lax.ppermute(cur_down, "chan", down_pairs)
-            if r < zc - 2:
-                cur_up = jnp.where(mask, payload, rec_up)
-                cur_down = jnp.where(mask, payload, rec_down)
-        below = (z > zk)[:, None, None, None]
-        mine = jnp.where(mask, payload, jnp.where(below, rec_up, rec_down))
+        if zc & (zc - 1) == 0:
+            mine = payload
+            d = 1
+            while d < zc:
+                got = lax.ppermute(mine, "chan", pairs_of(n, lambda i, d=d: (((i // qc) ^ d) * qc) + i % qc))
+                valid = (((zk ^ z) & ~(d - 1)) == 0)[:, None, None, None]
+                mine = jnp.where(valid, mine, got)
+                d *= 2
+        else:
+            up_pairs = pairs_of(n, lambda i: i + qc if i // qc < zc - 1 else None)
+            down_pairs = pairs_of(n, lambda i: i - qc if i // qc > 0 else None)
+            cur_up, cur_down = payload, payload
+            rec_up, rec_down = payload, payload
+            for r in range(zc - 1):
+                rec_up = lax.ppermute(cur_up, "chan", up_pairs)
+                rec_down = lax.ppermute(cur_down, "chan", down_pairs)
+                if r < zc - 2:
+                    cur_up = jnp.where(mask, payload, rec_up)
+                    cur_down = jnp.where(mask, payload, rec_down)
+            below = (z > zk)[:, None, None, None]
+            mine = jnp.where(mask, payload, jnp.where(below, rec_up, rec_down))
 
         offs = [0]
         held = [mine]
@@ -163,9 +172,7 @@
         traces = jnp.dot(
             cross.reshape(nb * SOURCE * receivers, width), lag_table, preferred_element_type=jnp.float32
         ).reshape(nb, SOURCE, receivers, LAGS)
-        traces_all = [traces[k] for k in range(nb)]
-        peaks = [jnp.max(jnp.abs(traces[k]), axis=(1, 2)) for k in range(nb)]
-        peak = jnp.stack(peaks)
+        peak = jnp.max(jnp.abs(traces), axis=(2, 3))
         got = [
             lax.ppermute(peak, "chan", pairs_of(n, lambda i, d=d: (i // qc) * qc + ((i % qc) ^ d)))
             for d in range(1, qc)
@@ -178,11 +185,8 @@
         ]
         for g in got:
             peak = jnp.maximum(peak, g)
-        out = [
-            (traces_all[k] / (peak[k][:, None, None] + 1e-06)).astype(jnp.bfloat16) for k in range(nb)
-        ]
-        stacked = jnp.stack(out, axis=0)
-        return stacked.reshape(source_blocks.shape[0], source_blocks.shape[1], SOURCE, receivers, LAGS)
+        normed = (traces / (peak[:, :, None, None] + 1e-06)).astype(jnp.bfloat16)
+        return normed.reshape(source_blocks.shape[0], source_blocks.shape[1], SOURCE, receivers, LAGS)
 
     return shards
 

time: 136 us -> 122 us (0.90)
  starting transfers between devices: 31.2 us -> 17.3 us
  other arithmetic: 15.5 us -> 8.71 us
  waiting for transfers between devices: 52.1 us -> 58.8 us
    ppermute x6 -> x2, starting transfers between devices: 18.9 us -> 5.24 us  [shards(): lax.ppermute(mine, 'chan', pairs_of(n, lambda i, d=d: (i // qc ^ d) * qc...]
    reduce_max x5 -> x0, other arithmetic: 3.9 us -> none  [shards(): peaks = [jnp.max(jnp.abs(traces[k]), axis=(1, 2)) for k in range(nb)]]
    ppermute x6 -> x2, waiting for transfers between devices: 31.4 us -> 34.8 us  [shards(): lax.ppermute(mine, 'chan', pairs_of(n, lambda i, d=d: (i // qc ^ d) * qc...]
    another operation x2 -> x0, other arithmetic: 2.31 us -> none  [the longest x1 2.29 us: shards(): stacked = jnp.stack(out, axis=0)]
    ppermute x2, waiting for transfers between devices: 10.1 us -> 11.6 us  [shards(): lax.ppermute(jnp.stack(held), 'chan', pairs_of(n, lambda i, b=b: i // qc...]
    convert_element_type x2 -> x1, other arithmetic: 3.71 us -> 3.48 us  [shards(): normed = (traces / (peak[:, :, None, None] + 1e-06)).astype(jnp.bfloat16)]
  transfers between devices with their start and end apart: 17 -> 13, of which waited for: 14 -> 11; matrix products, arithmetic and copies ran while one was open for 3% -> 3% of each run, Pallas kernels for 0% -> 0%
where the time goes in v5:
time: 122 us
  waiting for transfers between devices  58.8 us (48%)
  Pallas kernels  25.7 us (21%)
  starting transfers between devices  17.3 us (14%)
  other arithmetic  8.71 us (7%)
  matrix products  7.55 us (6%)
  local copies, waits for them, and re-layouts  3.95 us (3%)
    ppermute x2, waiting for transfers between devices, shards(): lax.ppermute(mine, 'chan', pairs_of(n, lambda i, d=d: (i // qc ^ d) * qc...  34.8 us
    pallas_call x1, Pallas kernels, cross_products(): pl.pallas_call(cross_kernel, grid_spec=pltpu.PrefetchScalarGridSpec(num_s...  25.7 us
    ppermute x2, waiting for transfers between devices, shards(): lax.ppermute(jnp.stack(held), 'chan', pairs_of(n, lambda i, b=b: i // qc...  11.6 us
    dot_general x1, matrix products, shards(): jnp.dot(cross.reshape(nb * SOURCE * receivers, width), lag_table, preferr...  7.55 us
    ppermute x2, starting transfers between devices, shards(): lax.ppermute(mine, 'chan', pairs_of(n, lambda i, d=d: (i // qc ^ d) * qc...  5.24 us
    ppermute x3, starting transfers between devices, shards(): lax.ppermute(peak, 'chan', pairs_of(n, lambda i, d=d: (i // qc + d) % zc...  5.2 us
    ppermute x3, waiting for transfers between devices, shards(): lax.ppermute(peak, 'chan', pairs_of(n, lambda i, d=d: (i // qc + d) % zc...  4.74 us
    ppermute x3, waiting for transfers between devices, shards(): lax.ppermute(send, 'chan', pairs_of(n, lambda i, d=d: i // qc * qc + (i %...  4.61 us
  transfers between devices with their start and end apart: 13, of which 11 were waited for; matrix products, arithmetic and copies ran while one was open for 3% of the time, Pallas kernels for 0%

profile of v5, /device:TPU:0, one launch (start us, length us, event | category | flops | bytes accessed | tf_op | source)
XLA Modules:
  0.0 122.1 jit_solution(563275304573481489)
XLA Ops:
  0.0 0.0 copy-start
  0.0 0.0 copy-start.1
  0.0 0.0 copy-start.2
  0.0 1.2 constant_dynamic-slice_fusion
  1.2 2.5 %collective-permute-start.2 = (bf16[8,8,1024]{2,1,0:T(8,128)(2,1)S(1)}, bf16[8,8,1024]{2,1,0:T(8,128)(2,1)S(1)}, u32[]{:S(2)}, u32[]{:S(2)}) collective-permute-start(bf16[8,8,1024]{2,1,0:T(8,128)(2,1)S(1)} %get-tuple-element.8), channel_id=1, source_target_pairs={{0,3},{1,2},{2,1},{3,0},{4,7},{5,6},{6,5},{7,4},{8,11},{9,10},{10,... | collective-permute-start | bytes 393224 | tf_op jit(solution)/shard_map/ppermute | solution.py:123
  3.7 0.6 collective-permute-start.1
  4.4 0.0 collective-permute-start
  4.4 0.8 reshape.162
  5.2 0.8 reshape.160
  6.0 1.6 %collective-permute-done.2 = bf16[8,8,1024]{2,1,0:T(8,128)(2,1)S(1)} collective-permute-done((bf16[8,8,1024]{2,1,0:T(8,128)(2,1)S(1)}, bf16[8,8,1024]{2,1,0:T(8,128)(2,1)S(1)}, u32[]{:S(2)}, u32[]{:S(2)}) %collective-permute-start.2) | collective-permute-done | bytes 131104 | tf_op jit(solution)/shard_map/ppermute | solution.py:123
  7.6 3.0 %collective-permute-done.1 = bf16[8,8,1024]{2,1,0:T(8,128)(2,1)S(1)} collective-permute-done((bf16[8,8,1024]{2,1,0:T(8,128)(2,1)S(1)}, bf16[8,8,1024]{2,1,0:T(8,128)(2,1)S(1)}, u32[]{:S(2)}, u32[]{:S(2)}) %collective-permute-start.1) | collective-permute-done | bytes 131104 | tf_op jit(solution)/shard_map/ppermute | solution.py:123
  10.6 0.0 collective-permute-done
  10.6 0.1 pad_maximum_fusion.2
  10.7 0.6 gather_fusion.1
  11.3 0.1 select_select_fusion
  11.4 2.4 %collective-permute-start.3 = (bf16[4,8,8,1024]{3,2,1,0:T(8,128)(2,1)S(1)}, bf16[4,8,8,1024]{3,2,1,0:T(8,128)(2,1)S(1)}, u32[]{:S(2)}, u32[]{:S(2)}) collective-permute-start(bf16[4,8,8,1024]{3,2,1,0:T(8,128)(2,1)S(1)} %select_select_fusion), channel_id=1, source_target_pairs={{0,4},{1,5},{2,6},{3,7},{4,0},{5,1},{6,2},{7,3},{8,12},{9,13},{10,... | collective-permute-start | bytes 1572872 | tf_op jit(solution)/shard_map/ppermute | solution.py:136
  13.8 12.1 %collective-permute-done.3 = bf16[4,8,8,1024]{3,2,1,0:T(8,128)(2,1)S(1)} collective-permute-done((bf16[4,8,8,1024]{3,2,1,0:T(8,128)(2,1)S(1)}, bf16[4,8,8,1024]{3,2,1,0:T(8,128)(2,1)S(1)}, u32[]{:S(2)}, u32[]{:S(2)}) %collective-permute-start.3) | collective-permute-done | bytes 524320 | tf_op jit(solution)/shard_map/ppermute | solution.py:136
  26.0 0.1 broadcast_select_fusion
  26.1 2.8 %collective-permute-start.4 = (bf16[4,8,8,1024]{3,2,1,0:T(8,128)(2,1)S(1)}, bf16[4,8,8,1024]{3,2,1,0:T(8,128)(2,1)S(1)}, u32[]{:S(2)}, u32[]{:S(2)}) collective-permute-start(bf16[4,8,8,1024]{3,2,1,0:T(8,128)(2,1)S(1)} %broadcast_select_fusion), channel_id=1, source_target_pairs={{0,8},{1,9},{2,10},{3,11},{4,12},{5,13},{6,14},{7,15},{8,0},{9,1},... | collective-permute-start | bytes 1572872 | tf_op jit(solution)/shard_map/ppermute | solution.py:136
  28.9 22.7 %collective-permute-done.4 = bf16[4,8,8,1024]{3,2,1,0:T(8,128)(2,1)S(1)} collective-permute-done((bf16[4,8,8,1024]{3,2,1,0:T(8,128)(2,1)S(1)}, bf16[4,8,8,1024]{3,2,1,0:T(8,128)(2,1)S(1)}, u32[]{:S(2)}, u32[]{:S(2)}) %collective-permute-start.4) | collective-permute-done | bytes 524320 | tf_op jit(solution)/shard_map/ppermute | solution.py:136
  51.6 0.1 select_bitcast_fusion
  51.7 1.6 %collective-permute-start.5 = (bf16[1,4,8,8,1024]{4,3,2,1,0:T(8,128)(2,1)S(1)}, bf16[1,4,8,8,1024]{4,3,2,1,0:T(8,128)(2,1)S(1)}, u32[]{:S(2)}, u32[]{:S(2)}) collective-permute-start(bf16[1,4,8,8,1024]{4,3,2,1,0:T(8,128)(2,1)S(1)} %select_bitcast_fusion), channel_id=1, source_target_pairs={{0,2},{1,3},{2,0},{3,1},{4,6},{5,7},{6,4},{7,5},{8,10},{9,11},{10,... | collective-permute-start | bytes 1572872 | tf_op jit(solution)/shard_map/ppermute | solution.py:157
  53.3 11.4 %collective-permute-done.5 = bf16[1,4,8,8,1024]{4,3,2,1,0:T(8,128)(2,1)S(1)} collective-permute-done((bf16[1,4,8,8,1024]{4,3,2,1,0:T(8,128)(2,1)S(1)}, bf16[1,4,8,8,1024]{4,3,2,1,0:T(8,128)(2,1)S(1)}, u32[]{:S(2)}, u32[]{:S(2)}) %collective-permute-start.5) | collective-permute-done | bytes 524320 | tf_op jit(solution)/shard_map/ppermute | solution.py:157
  64.7 0.1 pad_maximum_fusion.1
  64.8 0.1 collective-permute-start.6
  64.9 0.0 copy-done.2
  65.0 0.0 copy-done
  65.0 0.6 gather_fusion
  65.6 0.5 and_select_fusion.3.order_ref
  66.1 0.0 copy-done.1
  66.1 1.4 %multiply_bitcast_fusion.rcv_ref = f32[8,32,1024]{2,1,0:T(8,128)} fusion(bf16[32,8,1024]{2,1,0:T(8,128)(2,1)S(1)} %copy-done.1, f32[8]{0:T(128)S(1)} %convert_element_type.11), kind=kLoop, calls=%fused_computation.6 | loop fusion | flops 524288 | bytes 1572896 | tf_op jit(solution)/shard_map/mul | solution.py:170
  67.5 0.2 collective-permute-done.6
  67.7 2.7 %pad_maximum_fusion.src_ref = bf16[4,4,8,8,1024]{4,3,2,1,0:T(8,128)(2,1)} fusion(bf16[2,4,8,8,1024]{4,3,2,1,0:T(8,128)(2,1)} %collective-permute-done.6, bf16[1,4,8,8,1024]{4,3,2,1,0:T(8,128)(2,1)S(1)} %collective-permute-done.5, bf16[1,4,8,8,1024]{4,3,2,1,0:T(8,128)(2,1)S(1)} %select_bitcast_fusion), kind=kLoop, calls=%fused_computation.4 | loop fusion | flops 2097152 | bytes 4194304 | tf_op jit(solution)/shard_map/stack | solution.py:162
  70.4 25.7 %shard_map.55 = bf16[4,32,32,1024]{3,2,1,0:T(8,128)(2,1)} custom-call(s32[4]{0:T(128)} %and_select_fusion.3.order_ref, bf16[4,4,8,8,1024]{4,3,2,1,0:T(8,128)(2,1)} %pad_maximum_fusion.src_ref, f32[8,32,1024]{2,1,0:T(8,128)} %multiply_bitcast_fusion.rcv_ref), custom_call_target="tpu_custom_call" | custom-call | flops 134217728 | bytes 11534336 | tf_op jit(solution)/shard_map/pallas_call | solution.py:61
  96.1 7.5 %abs_reduce_fusion = (f32[4,32]{1,0:T(4,128)S(1)}, f32[4,32,32,512]{3,2,1,0:T(8,128)S(1)}) fusion(bf16[4,32,32,1024]{3,2,1,0:T(8,128)(2,1)} %shard_map.55, bf16[1024,512,1,1]{1,0,3,2:T(8,128)(2,1)} %constant.103), kind=kOutput, calls=%fused_computation.3 | convolution fusion | flops 4299161600 | bytes 17826304 | tf_op jit(solution)/shard_map/dot_general | solution.py:172
  103.7 1.3 %collective-permute-start.9 = (f32[4,32]{1,0:T(4,128)S(1)}, f32[4,32]{1,0:T(4,128)S(1)}, u32[]{:S(2)}, u32[]{:S(2)}) collective-permute-start(f32[4,32]{1,0:T(4,128)S(1)} %get-tuple-element.14), channel_id=1, source_target_pairs={{0,3},{1,2},{2,1},{3,0},{4,7},{5,6},{6,5},{7,4},{8,11},{9,10},{10,... | collective-permute-start | bytes 1544 | tf_op jit(solution)/shard_map/ppermute | solution.py:177
  105.0 0.6 collective-permute-start.8
  105.7 0.0 collective-permute-start.7
  105.7 1.1 collective-permute-done.9
  106.8 1.8 %collective-permute-done.8 = f32[4,32]{1,0:T(4,128)S(1)} collective-permute-done((f32[4,32]{1,0:T(4,128)S(1)}, f32[4,32]{1,0:T(4,128)S(1)}, u32[]{:S(2)}, u32[]{:S(2)}) %collective-permute-start.8) | collective-permute-done | bytes 544 | tf_op jit(solution)/shard_map/ppermute | solution.py:177
  108.6 0.0 collective-permute-done.7
  108.6 4.6 %collective-permute-start.12 = (f32[4,32]{1,0:T(4,128)S(1)}, f32[4,32]{1,0:T(4,128)S(1)}, u32[]{:S(2)}, u32[]{:S(2)}) collective-permute-start(f32[4,32]{1,0:T(4,128)S(1)} %maximum_maximum_fusion), channel_id=1, source_target_pairs={{0,12},{1,13},{2,14},{3,15},{4,0},{5,1},{6,2},{7,3},{8,4},{9,5},{1... | collective-permute-start | bytes 1544 | tf_op jit(solution)/shard_map/ppermute | solution.py:183
  113.2 0.0 collective-permute-start.11
  113.2 0.6 collective-permute-start.10
  113.8 0.7 collective-permute-done.12
  114.5 3.2 %collective-permute-done.11 = f32[4,32]{1,0:T(4,128)S(1)} collective-permute-done((f32[4,32]{1,0:T(4,128)S(1)}, f32[4,32]{1,0:T(4,128)S(1)}, u32[]{:S(2)}, u32[]{:S(2)}) %collective-permute-start.11) | collective-permute-done | bytes 544 | tf_op jit(solution)/shard_map/ppermute | solution.py:183
  117.7 0.9 collective-permute-done.10
  118.6 3.5 %divide_convert_fusion = bf16[4,32,32,512]{3,2,1,0:T(8,128)(2,1)} fusion(f32[4,32,32,512]{3,2,1,0:T(8,128)S(1)} %get-tuple-element.15, f32[4,32]{1,0:T(4,128)S(1)} %maximum_add_fusion), kind=kLoop, calls=%fused_computation.2 | loop fusion | flops 4194304 | bytes 12583424 | tf_op jit(solution)/shard_map/convert_element_type | solution.py:188
  (9 shorter events, 0.1 us)
Async XLA Ops:
  0.0 65.0 %copy-start = (s32[4]{0:T(128)S(1)}, s32[4]{0:T(128)}, u32[]{:S(2)}) copy-start(s32[4]{0:T(128)} %constant.101.clone) | copy-start | bytes 52
  0.0 66.1 %copy-start.1 = (bf16[32,8,1024]{2,1,0:T(8,128)(2,1)S(1)}, bf16[32,8,1024]{2,1,0:T(8,128)(2,1)}, u32[]{:S(2)}) copy-start(bf16[32,8,1024]{2,1,0:T(8,128)(2,1)} %param.5) | copy-start | bytes 1572868
  0.0 64.9 %copy-start.2 = (s32[8]{0:T(128)S(1)}, s32[8]{0:T(128)}, u32[]{:S(2)}) copy-start(s32[8]{0:T(128)} %param.7) | copy-start | bytes 100
  1.2 6.4 %collective-permute-start.2 = (bf16[8,8,1024]{2,1,0:T(8,128)(2,1)S(1)}, bf16[8,8,1024]{2,1,0:T(8,128)(2,1)S(1)}, u32[]{:S(2)}, u32[]{:S(2)}) collective-permute-start(bf16[8,8,1024]{2,1,0:T(8,128)(2,1)S(1)} %get-tuple-element.8), channel_id=1, source_target_pairs={{0,3},{1,2},{2,1},{3,0},{4,7},{5,6},{6,5},{7,4},{8,11},{9,10},{10,... | collective-permute-start | bytes 393224 | tf_op jit(solution)/shard_map/ppermute | solution.py:123
  3.7 6.9 %collective-permute-start.1 = (bf16[8,8,1024]{2,1,0:T(8,128)(2,1)S(1)}, bf16[8,8,1024]{2,1,0:T(8,128)(2,1)S(1)}, u32[]{:S(2)}, u32[]{:S(2)}) collective-permute-start(bf16[8,8,1024]{2,1,0:T(8,128)(2,1)S(1)} %get-tuple-element.9), channel_id=1, source_target_pairs={{0,2},{1,3},{2,0},{3,1},{4,6},{5,7},{6,4},{7,5},{8,10},{9,11},{10,... | collective-permute-start | bytes 393224 | tf_op jit(solution)/shard_map/ppermute | solution.py:123
  4.4 6.2 %collective-permute-start = (bf16[8,8,1024]{2,1,0:T(8,128)(2,1)S(1)}, bf16[8,8,1024]{2,1,0:T(8,128)(2,1)S(1)}, u32[]{:S(2)}, u32[]{:S(2)}) collective-permute-start(bf16[8,8,1024]{2,1,0:T(8,128)(2,1)S(1)} %get-tuple-element.10), channel_id=1, source_target_pairs={{0,1},{1,0},{2,3},{3,2},{4,5},{5,4},{6,7},{7,6},{8,9},{9,8},{10,11... | collective-permute-start | bytes 393224 | tf_op jit(solution)/shard_map/ppermute | solution.py:123
  11.4 14.6 %collective-permute-start.3 = (bf16[4,8,8,1024]{3,2,1,0:T(8,128)(2,1)S(1)}, bf16[4,8,8,1024]{3,2,1,0:T(8,128)(2,1)S(1)}, u32[]{:S(2)}, u32[]{:S(2)}) collective-permute-start(bf16[4,8,8,1024]{3,2,1,0:T(8,128)(2,1)S(1)} %select_select_fusion), channel_id=1, source_target_pairs={{0,4},{1,5},{2,6},{3,7},{4,0},{5,1},{6,2},{7,3},{8,12},{9,13},{10,... | collective-permute-start | bytes 1572872 | tf_op jit(solution)/shard_map/ppermute | solution.py:136
  26.1 25.5 %collective-permute-start.4 = (bf16[4,8,8,1024]{3,2,1,0:T(8,128)(2,1)S(1)}, bf16[4,8,8,1024]{3,2,1,0:T(8,128)(2,1)S(1)}, u32[]{:S(2)}, u32[]{:S(2)}) collective-permute-start(bf16[4,8,8,1024]{3,2,1,0:T(8,128)(2,1)S(1)} %broadcast_select_fusion), channel_id=1, source_target_pairs={{0,8},{1,9},{2,10},{3,11},{4,12},{5,13},{6,14},{7,15},{8,0},{9,1},... | collective-permute-start | bytes 1572872 | tf_op jit(solution)/shard_map/ppermute | solution.py:136
  51.7 13.0 %collective-permute-start.5 = (bf16[1,4,8,8,1024]{4,3,2,1,0:T(8,128)(2,1)S(1)}, bf16[1,4,8,8,1024]{4,3,2,1,0:T(8,128)(2,1)S(1)}, u32[]{:S(2)}, u32[]{:S(2)}) collective-permute-start(bf16[1,4,8,8,1024]{4,3,2,1,0:T(8,128)(2,1)S(1)} %select_bitcast_fusion), channel_id=1, source_target_pairs={{0,2},{1,3},{2,0},{3,1},{4,6},{5,7},{6,4},{7,5},{8,10},{9,11},{10,... | collective-permute-start | bytes 1572872 | tf_op jit(solution)/shard_map/ppermute | solution.py:157
  64.8 2.9 %collective-permute-start.6 = (bf16[2,4,8,8,1024]{4,3,2,1,0:T(8,128)(2,1)S(1)}, bf16[2,4,8,8,1024]{4,3,2,1,0:T(8,128)(2,1)}, u32[]{:S(2)}, u32[]{:S(2)}) collective-permute-start(bf16[2,4,8,8,1024]{4,3,2,1,0:T(8,128)(2,1)S(1)} %pad_maximum_fusion.1), channel_id=1, source_target_pairs={{0,1},{1,0},{2,3},{3,2},{4,5},{5,4},{6,7},{7,6},{8,9},{9,8},{10,11... | collective-permute-start | bytes 3145736 | tf_op jit(solution)/shard_map/ppermute | solution.py:157
  103.7 3.1 %collective-permute-start.9 = (f32[4,32]{1,0:T(4,128)S(1)}, f32[4,32]{1,0:T(4,128)S(1)}, u32[]{:S(2)}, u32[]{:S(2)}) collective-permute-start(f32[4,32]{1,0:T(4,128)S(1)} %get-tuple-element.14), channel_id=1, source_target_pairs={{0,3},{1,2},{2,1},{3,0},{4,7},{5,6},{6,5},{7,4},{8,11},{9,10},{10,... | collective-permute-start | bytes 1544 | tf_op jit(solution)/shard_map/ppermute | solution.py:177
  105.0 3.6 %collective-permute-start.8 = (f32[4,32]{1,0:T(4,128)S(1)}, f32[4,32]{1,0:T(4,128)S(1)}, u32[]{:S(2)}, u32[]{:S(2)}) collective-permute-start(f32[4,32]{1,0:T(4,128)S(1)} %get-tuple-element.14), channel_id=1, source_target_pairs={{0,2},{1,3},{2,0},{3,1},{4,6},{5,7},{6,4},{7,5},{8,10},{9,11},{10,... | collective-permute-start | bytes 1544 | tf_op jit(solution)/shard_map/ppermute | solution.py:177
  105.7 3.0 %collective-permute-start.7 = (f32[4,32]{1,0:T(4,128)S(1)}, f32[4,32]{1,0:T(4,128)S(1)}, u32[]{:S(2)}, u32[]{:S(2)}) collective-permute-start(f32[4,32]{1,0:T(4,128)S(1)} %get-tuple-element.14), channel_id=1, source_target_pairs={{0,1},{1,0},{2,3},{3,2},{4,5},{5,4},{6,7},{7,6},{8,9},{9,8},{10,11... | collective-permute-start | bytes 1544 | tf_op jit(solution)/shard_map/ppermute | solution.py:177
  108.6 5.9 %collective-permute-start.12 = (f32[4,32]{1,0:T(4,128)S(1)}, f32[4,32]{1,0:T(4,128)S(1)}, u32[]{:S(2)}, u32[]{:S(2)}) collective-permute-start(f32[4,32]{1,0:T(4,128)S(1)} %maximum_maximum_fusion), channel_id=1, source_target_pairs={{0,12},{1,13},{2,14},{3,15},{4,0},{5,1},{6,2},{7,3},{8,4},{9,5},{1... | collective-permute-start | bytes 1544 | tf_op jit(solution)/shard_map/ppermute | solution.py:183
  113.2 4.5 %collective-permute-start.11 = (f32[4,32]{1,0:T(4,128)S(1)}, f32[4,32]{1,0:T(4,128)S(1)}, u32[]{:S(2)}, u32[]{:S(2)}) collective-permute-start(f32[4,32]{1,0:T(4,128)S(1)} %maximum_maximum_fusion), channel_id=1, source_target_pairs={{0,8},{1,9},{2,10},{3,11},{4,12},{5,13},{6,14},{7,15},{8,0},{9,1},... | collective-permute-start | bytes 1544 | tf_op jit(solution)/shard_map/ppermute | solution.py:183
  113.2 5.4 %collective-permute-start.10 = (f32[4,32]{1,0:T(4,128)S(1)}, f32[4,32]{1,0:T(4,128)S(1)}, u32[]{:S(2)}, u32[]{:S(2)}) collective-permute-start(f32[4,32]{1,0:T(4,128)S(1)} %maximum_maximum_fusion), channel_id=1, source_target_pairs={{0,4},{1,5},{2,6},{3,7},{4,8},{5,9},{6,10},{7,11},{8,12},{9,13},{1... | collective-permute-start | bytes 1544 | tf_op jit(solution)/shard_map/ppermute | solution.py:183

commit v6 on v5

--- a/solution.py
+++ b/solution.py
@@ -9,6 +9,7 @@
 from jax.experimental.pallas import tpu as pltpu
 from jax.sharding import PartitionSpec as P
 
+
 SOURCE = 32
 LAGS = 512
 
@@ -23,12 +24,12 @@
     return jnp.asarray(table.astype(ml_dtypes.bfloat16))
 
 
-ST = 8
 RC = 16
 
 
-def cross_kernel(order_ref, src_ref, rcv_ref, out_ref):
-    del order_ref
+def cross_kernel(pos_ref, src_ref, rcv_ref, *rest):
+    del pos_ref
+    out_ref = rest[-1]
     bins = src_ref.shape[-1] // 2
     windows = src_ref.shape[3]
     rows = rcv_ref.shape[1]
@@ -53,29 +54,38 @@
     lax.fori_loop(0, src_ref.shape[2], body, 0)
 
 
-def cross_products(stack, order, rcv_t):
-    qc, nb, piece, windows, width = stack.shape
+def cross_part(entries, pos, rcv_t, buf=None):
+    m, nb, piece, windows, width = entries.shape
     receivers = rcv_t.shape[1]
-    sources = qc * piece
-    flops = 8 * nb * sources * receivers * windows * (width // 2)
+    qc = SOURCE // piece
+    flops = 8 * nb * m * piece * receivers * windows * (width // 2)
+    in_specs = [
+        pl.BlockSpec((1, 1, piece, windows, width), lambda k, i, o: (i, k, 0, 0, 0)),
+        pl.BlockSpec((windows, receivers, width), lambda k, i, o: (0, 0, 0)),
+    ]
+    args = [pos, entries, rcv_t]
+    aliases = {}
+    if buf is not None:
+        in_specs.append(pl.BlockSpec(memory_space=pl.ANY))
+        args.append(buf)
+        aliases = {3: 0}
     return pl.pallas_call(
         cross_kernel,
         grid_spec=pltpu.PrefetchScalarGridSpec(
             num_scalar_prefetch=1,
-            grid=(nb, qc),
-            in_specs=[
-                pl.BlockSpec((1, 1, piece, windows, width), lambda k, i, o: (o[i], k, 0, 0, 0)),
-                pl.BlockSpec((windows, receivers, width), lambda k, i, o: (0, 0, 0)),
-            ],
-            out_specs=pl.BlockSpec((1, piece, receivers, width), lambda k, i, o: (k, i, 0, 0)),
+            grid=(nb, m),
+            in_specs=in_specs,
+            out_specs=pl.BlockSpec((1, piece, receivers, width), lambda k, i, o: (k, o[i], 0, 0)),
         ),
-        out_shape=jax.ShapeDtypeStruct((nb, sources, receivers, width), jnp.bfloat16),
+        out_shape=jax.ShapeDtypeStruct((nb, qc * piece, receivers, width), jnp.bfloat16),
+        input_output_aliases=aliases,
         cost_estimate=pl.CostEstimate(
             flops=flops,
-            bytes_accessed=stack.size * 2 + rcv_t.size * 4 + nb * sources * receivers * width * 2,
+            bytes_accessed=entries.size * 2 + rcv_t.size * 4 + nb * m * piece * receivers * width * 2,
             transcendentals=0,
         ),
-    )(order, stack, rcv_t)
+    )(*args)
+
 
 def plane_size(mesh):
     devs = list(mesh.devices[0])
@@ -151,24 +161,22 @@
             below = (z > zk)[:, None, None, None]
             mine = jnp.where(mask, payload, jnp.where(below, rec_up, rec_down))
 
+        lag_table = build_table(bins, LAGS)
+        window_mask = window_valid.astype(jnp.float32)[:, None, None]
+        rcv_t = jnp.transpose(spectra, (1, 0, 2)).astype(jnp.float32) * window_mask
+
+        cross = cross_part(mine[None], q[None].astype(jnp.int32), rcv_t)
         offs = [0]
         held = [mine]
         for b in plane_bits:
             got = lax.ppermute(
                 jnp.stack(held), "chan", pairs_of(n, lambda i, b=b: (i // qc) * qc + ((i % qc) ^ b))
             )
-            offs = offs + [o ^ b for o in offs]
+            new_offs = [o ^ b for o in offs]
+            pos = q ^ jnp.array(new_offs, jnp.int32)
+            cross = cross_part(got, pos, rcv_t, cross)
+            offs = offs + new_offs
             held = held + [got[i] for i in range(got.shape[0])]
-        stack = jnp.stack(held)
-        inv = [0] * qc
-        for e, o in enumerate(offs):
-            inv[o] = e
-        order = jnp.take(jnp.array(inv, jnp.int32), jnp.arange(qc, dtype=jnp.int32) ^ q)
-
-        lag_table = build_table(bins, LAGS)
-        window_mask = window_valid.astype(jnp.float32)[:, None, None]
-        rcv_t = jnp.transpose(spectra, (1, 0, 2)).astype(jnp.float32) * window_mask
-        cross = cross_products(stack, order, rcv_t)
         traces = jnp.dot(
             cross.reshape(nb * SOURCE * receivers, width), lag_table, preferred_element_type=jnp.float32
         ).reshape(nb, SOURCE, receivers, LAGS)
@@ -195,8 +203,10 @@
     n = mesh.shape["chan"]
     qc = plane_size(mesh)
     placed = (P(("parts", "chan"), None, None), P("parts", None), P("parts"))
+    inner = make_shards(n, qc)
+
     return jax.shard_map(
-        make_shards(n, qc),
+        inner,
         mesh=mesh,
         in_specs=placed,
         out_specs=P(None, None, None, ("parts", "chan"), None),

time: 122 us -> 121 us (level)
  Pallas kernels: 25.7 us -> 30 us
  other arithmetic: 8.71 us -> 5.93 us
    pallas_call x1 -> x3, Pallas kernels: 25.7 us -> 30 us  [cross_part(): pl.pallas_call(cross_kernel, grid_spec=pltpu.PrefetchScalarGridSpec(num_s...]
    another operation x2 -> x0, other arithmetic: 2.87 us -> none  [shards(): stack = jnp.stack(held)]
  transfers between devices with their start and end apart: 13 -> 13, of which waited for: 11 -> 10; matrix products, arithmetic and copies ran while one was open for 3% -> 3% of each run, Pallas kernels for 0% -> 13%
where the time goes in v6:
time: 121 us
  waiting for transfers between devices  58.1 us (48%)
  Pallas kernels  30 us (25%)
  starting transfers between devices  16.5 us (14%)
  matrix products  7.24 us (6%)
  other arithmetic  5.93 us (5%)
  local copies, waits for them, and re-layouts  3.32 us (3%)
    ppermute x2, waiting for transfers between devices, shards(): lax.ppermute(mine, 'chan', pairs_of(n, lambda i, d=d: (i // qc ^ d) * qc...  35.3 us
    pallas_call x3, Pallas kernels, cross_part(): pl.pallas_call(cross_kernel, grid_spec=pltpu.PrefetchScalarGridSpec(num_s...  30 us
    ppermute x2, waiting for transfers between devices, shards(): lax.ppermute(jnp.stack(held), 'chan', pairs_of(n, lambda i, b=b: i // qc...  11.2 us
    dot_general x1, matrix products, shards(): jnp.dot(cross.reshape(nb * SOURCE * receivers, width), lag_table, preferr...  7.24 us
    ppermute x3, starting transfers between devices, shards(): lax.ppermute(peak, 'chan', pairs_of(n, lambda i, d=d: (i // qc + d) % zc...  5.07 us
    ppermute x3, waiting for transfers between devices, shards(): lax.ppermute(send, 'chan', pairs_of(n, lambda i, d=d: i // qc * qc + (i %...  5.01 us
    ppermute x2, starting transfers between devices, shards(): lax.ppermute(mine, 'chan', pairs_of(n, lambda i, d=d: (i // qc ^ d) * qc...  4.4 us
    ppermute x3, waiting for transfers between devices, shards(): lax.ppermute(peak, 'chan', pairs_of(n, lambda i, d=d: (i // qc + d) % zc...  3.58 us
  transfers between devices with their start and end apart: 13, of which 10 were waited for; matrix products, arithmetic and copies ran while one was open for 3% of the time, Pallas kernels for 13%

profile of v6, /device:TPU:0, one launch (start us, length us, event | category | flops | bytes accessed | tf_op | source)
XLA Modules:
  0.0 121.2 jit_solution(7154933011590031611)
XLA Ops:
  0.0 0.0 copy-start.5
  0.0 0.0 copy-start.1
  0.0 0.0 copy-start.3
  0.0 1.2 constant_dynamic-slice_fusion
  1.2 0.6 collective-permute-start
  1.8 2.6 %collective-permute-start.1 = (bf16[8,8,1024]{2,1,0:T(8,128)(2,1)S(1)}, bf16[8,8,1024]{2,1,0:T(8,128)(2,1)S(1)}, u32[]{:S(2)}, u32[]{:S(2)}) collective-permute-start(bf16[8,8,1024]{2,1,0:T(8,128)(2,1)S(1)} %get-tuple-element.9), channel_id=1, source_target_pairs={{0,2},{1,3},{2,0},{3,1},{4,6},{5,7},{6,4},{7,5},{8,10},{9,11},{10,... | collective-permute-start | bytes 393224 | tf_op jit(solution)/shard_map/ppermute | solution.py:133
  4.4 0.0 collective-permute-start.2
  4.4 0.8 reshape.141
  5.2 0.8 reshape.139
  6.0 0.0 collective-permute-done
  6.0 2.7 %collective-permute-done.1 = bf16[8,8,1024]{2,1,0:T(8,128)(2,1)S(1)} collective-permute-done((bf16[8,8,1024]{2,1,0:T(8,128)(2,1)S(1)}, bf16[8,8,1024]{2,1,0:T(8,128)(2,1)S(1)}, u32[]{:S(2)}, u32[]{:S(2)}) %collective-permute-start.1) | collective-permute-done | bytes 131104 | tf_op jit(solution)/shard_map/ppermute | solution.py:133
  8.7 2.3 %collective-permute-done.2 = bf16[8,8,1024]{2,1,0:T(8,128)(2,1)S(1)} collective-permute-done((bf16[8,8,1024]{2,1,0:T(8,128)(2,1)S(1)}, bf16[8,8,1024]{2,1,0:T(8,128)(2,1)S(1)}, u32[]{:S(2)}, u32[]{:S(2)}) %collective-permute-start.2) | collective-permute-done | bytes 131104 | tf_op jit(solution)/shard_map/ppermute | solution.py:133
  11.0 0.1 pad_maximum_fusion.1
  11.1 0.6 gather_fusion
  11.7 0.1 select_select_fusion
  11.8 1.6 %collective-permute-start.3 = (bf16[4,8,8,1024]{3,2,1,0:T(8,128)(2,1)S(1)}, bf16[4,8,8,1024]{3,2,1,0:T(8,128)(2,1)S(1)}, u32[]{:S(2)}, u32[]{:S(2)}) collective-permute-start(bf16[4,8,8,1024]{3,2,1,0:T(8,128)(2,1)S(1)} %select_select_fusion), channel_id=1, source_target_pairs={{0,4},{1,5},{2,6},{3,7},{4,0},{5,1},{6,2},{7,3},{8,12},{9,13},{10,... | collective-permute-start | bytes 1572872 | tf_op jit(solution)/shard_map/ppermute | solution.py:146
  13.4 12.5 %collective-permute-done.3 = bf16[4,8,8,1024]{3,2,1,0:T(8,128)(2,1)S(1)} collective-permute-done((bf16[4,8,8,1024]{3,2,1,0:T(8,128)(2,1)S(1)}, bf16[4,8,8,1024]{3,2,1,0:T(8,128)(2,1)S(1)}, u32[]{:S(2)}, u32[]{:S(2)}) %collective-permute-start.3) | collective-permute-done | bytes 524320 | tf_op jit(solution)/shard_map/ppermute | solution.py:146
  25.9 0.1 broadcast_select_fusion
  26.0 2.8 %collective-permute-start.4 = (bf16[4,8,8,1024]{3,2,1,0:T(8,128)(2,1)S(1)}, bf16[4,8,8,1024]{3,2,1,0:T(8,128)(2,1)S(1)}, u32[]{:S(2)}, u32[]{:S(2)}) collective-permute-start(bf16[4,8,8,1024]{3,2,1,0:T(8,128)(2,1)S(1)} %broadcast_select_fusion), channel_id=1, source_target_pairs={{0,8},{1,9},{2,10},{3,11},{4,12},{5,13},{6,14},{7,15},{8,0},{9,1},... | collective-permute-start | bytes 1572872 | tf_op jit(solution)/shard_map/ppermute | solution.py:146
  28.8 22.8 %collective-permute-done.4 = bf16[4,8,8,1024]{3,2,1,0:T(8,128)(2,1)S(1)} collective-permute-done((bf16[4,8,8,1024]{3,2,1,0:T(8,128)(2,1)S(1)}, bf16[4,8,8,1024]{3,2,1,0:T(8,128)(2,1)S(1)}, u32[]{:S(2)}, u32[]{:S(2)}) %collective-permute-start.4) | collective-permute-done | bytes 524320 | tf_op jit(solution)/shard_map/ppermute | solution.py:146
  51.6 0.1 select_bitcast_fusion.src_ref
  51.8 0.0 copy-start
  51.8 1.6 %collective-permute-start.5 = (bf16[1,4,8,8,1024]{4,3,2,1,0:T(8,128)(2,1)S(1)}, bf16[1,4,8,8,1024]{4,3,2,1,0:T(8,128)(2,1)S(1)}, u32[]{:S(2)}, u32[]{:S(2)}) collective-permute-start(bf16[1,4,8,8,1024]{4,3,2,1,0:T(8,128)(2,1)S(1)} %select_bitcast_fusion.src_ref), channel_id=1, source_target_pairs={{0,2},{1,3},{2,0},{3,1},{4,6},{5,7},{6,4},{7,5},{8,10},{9,11},{10,... | collective-permute-start | bytes 1572872 | tf_op jit(solution)/shard_map/ppermute | solution.py:172
  53.4 11.2 %collective-permute-done.5.src_ref = bf16[1,4,8,8,1024]{4,3,2,1,0:T(8,128)(2,1)S(1)} collective-permute-done((bf16[1,4,8,8,1024]{4,3,2,1,0:T(8,128)(2,1)S(1)}, bf16[1,4,8,8,1024]{4,3,2,1,0:T(8,128)(2,1)S(1)}, u32[]{:S(2)}, u32[]{:S(2)}) %collective-permute-start.5) | collective-permute-done | bytes 524320 | tf_op jit(solution)/shard_map/ppermute | solution.py:172
  64.6 0.0 copy-start.2
  64.6 0.1 pad_maximum_fusion
  64.7 0.1 collective-permute-start.6
  64.8 0.0 copy-done.3
  64.8 0.0 copy-done.5
  64.8 0.5 broadcast_xor_fusion.pos_ref
  65.4 0.0 copy-done.1
  65.4 1.3 %multiply_bitcast_fusion.rcv_ref = f32[8,32,1024]{2,1,0:T(8,128)} fusion(bf16[32,8,1024]{2,1,0:T(8,128)(2,1)S(1)} %copy-done.1, f32[8]{0:T(128)S(1)} %convert_element_type.11), kind=kLoop, calls=%fused_computation.4 | loop fusion | flops 524288 | bytes 1572896 | tf_op jit(solution)/shard_map/mul | solution.py:166
  66.7 0.0 copy-done
  66.7 7.8 %shard_map.64.rest_0_ = bf16[4,32,32,1024]{3,2,1,0:T(8,128)(2,1)} custom-call(s32[1]{0:T(128)} %bitcast.10.pos_ref, bf16[1,4,8,8,1024]{4,3,2,1,0:T(8,128)(2,1)} %copy-done, f32[8,32,1024]{2,1,0:T(8,128)} %multiply_bitcast_fusion.rcv_ref), custom_call_target="tpu_custom_call" | custom-call | flops 33554432 | bytes 3670016 | tf_op jit(solution)/shard_map/pallas_call | solution.py:72
  74.4 0.0 copy-done.2
  74.4 7.8 %shard_map.65.rest_0_ = bf16[4,32,32,1024]{3,2,1,0:T(8,128)(2,1)} custom-call(s32[1]{0:T(128)S(6)} %xor.67.pos_ref, bf16[1,4,8,8,1024]{4,3,2,1,0:T(8,128)(2,1)} %copy-done.2, f32[8,32,1024]{2,1,0:T(8,128)} %multiply_bitcast_fusion.rcv_ref, bf16[4,32,32,1024]{3,2,1,0:T(8,128)(2,1)} %shard_map.64.rest_0_), custom_call_target="tpu_custom_call", output_to_operand_aliasing={{}: (3, {})} | custom-call | flops 33554432 | bytes 3670016 | tf_op jit(solution)/shard_map/pallas_call | solution.py:72
  82.2 0.0 copy-start.4
  82.2 0.0 collective-permute-done.6.src_ref
  82.2 14.4 %shard_map.66 = bf16[4,32,32,1024]{3,2,1,0:T(8,128)(2,1)} custom-call(s32[2]{0:T(128)} %broadcast_xor_fusion.pos_ref, bf16[2,4,8,8,1024]{4,3,2,1,0:T(8,128)(2,1)} %collective-permute-done.6.src_ref, f32[8,32,1024]{2,1,0:T(8,128)} %multiply_bitcast_fusion.rcv_ref, bf16[4,32,32,1024]{3,2,1,0:T(8,128)(2,1)} %shard_map.65.rest_0_), custom_call_target="tpu_custom_call", output_to_operand_aliasing={{}: (3, {})} | custom-call | flops 67108864 | bytes 6291456 | tf_op jit(solution)/shard_map/pallas_call | solution.py:72
  96.6 0.0 copy-done.4
  96.6 7.2 %abs_reduce_fusion = (f32[4,32]{1,0:T(4,128)S(1)}, f32[4,32,32,512]{3,2,1,0:T(8,128)S(1)}) fusion(bf16[4,32,32,1024]{3,2,1,0:T(8,128)(2,1)} %shard_map.66, bf16[1024,512,1,1]{1,0,3,2:T(8,128)(2,1)S(1)} %copy-done.4), kind=kOutput, calls=%fused_computation.2 | convolution fusion | flops 4299161600 | bytes 17826304 | tf_op jit(solution)/shard_map/dot_general | solution.py:180
  103.9 0.6 collective-permute-start.7
  104.4 1.6 %collective-permute-start.8 = (f32[4,32]{1,0:T(4,128)S(1)}, f32[4,32]{1,0:T(4,128)S(1)}, u32[]{:S(2)}, u32[]{:S(2)}) collective-permute-start(f32[4,32]{1,0:T(4,128)S(1)} %get-tuple-element.14), channel_id=1, source_target_pairs={{0,2},{1,3},{2,0},{3,1},{4,6},{5,7},{6,4},{7,5},{8,10},{9,11},{10,... | collective-permute-start | bytes 1544 | tf_op jit(solution)/shard_map/ppermute | solution.py:185
  106.0 0.0 collective-permute-start.9
  106.0 0.0 collective-permute-done.7
  106.0 2.0 %collective-permute-done.8 = f32[4,32]{1,0:T(4,128)S(1)} collective-permute-done((f32[4,32]{1,0:T(4,128)S(1)}, f32[4,32]{1,0:T(4,128)S(1)}, u32[]{:S(2)}, u32[]{:S(2)}) %collective-permute-start.8) | collective-permute-done | bytes 544 | tf_op jit(solution)/shard_map/ppermute | solution.py:185
  108.0 1.0 collective-permute-done.9
  109.0 1.7 %collective-permute-start.10 = (f32[4,32]{1,0:T(4,128)S(1)}, f32[4,32]{1,0:T(4,128)S(1)}, u32[]{:S(2)}, u32[]{:S(2)}) collective-permute-start(f32[4,32]{1,0:T(4,128)S(1)} %maximum_maximum_fusion), channel_id=1, source_target_pairs={{0,4},{1,5},{2,6},{3,7},{4,8},{5,9},{6,10},{7,11},{8,12},{9,13},{1... | collective-permute-start | bytes 1544 | tf_op jit(solution)/shard_map/ppermute | solution.py:191
  110.7 3.4 %collective-permute-start.11 = (f32[4,32]{1,0:T(4,128)S(1)}, f32[4,32]{1,0:T(4,128)S(1)}, u32[]{:S(2)}, u32[]{:S(2)}) collective-permute-start(f32[4,32]{1,0:T(4,128)S(1)} %maximum_maximum_fusion), channel_id=1, source_target_pairs={{0,8},{1,9},{2,10},{3,11},{4,12},{5,13},{6,14},{7,15},{8,0},{9,1},... | collective-permute-start | bytes 1544 | tf_op jit(solution)/shard_map/ppermute | solution.py:191
  114.1 0.0 collective-permute-start.12
  114.1 1.0 collective-permute-done.10
  115.1 0.6 collective-permute-done.11
  115.7 2.0 %collective-permute-done.12 = f32[4,32]{1,0:T(4,128)S(1)} collective-permute-done((f32[4,32]{1,0:T(4,128)S(1)}, f32[4,32]{1,0:T(4,128)S(1)}, u32[]{:S(2)}, u32[]{:S(2)}) %collective-permute-start.12) | collective-permute-done | bytes 544 | tf_op jit(solution)/shard_map/ppermute | solution.py:191
  117.7 3.5 %divide_convert_fusion = bf16[4,32,32,512]{3,2,1,0:T(8,128)(2,1)} fusion(f32[4,32,32,512]{3,2,1,0:T(8,128)S(1)} %get-tuple-element.15, f32[4,32]{1,0:T(4,128)S(1)} %maximum_add_fusion), kind=kLoop, calls=%fused_computation.1 | loop fusion | flops 4194304 | bytes 12583424 | tf_op jit(solution)/shard_map/convert_element_type | solution.py:196
  (7 shorter events, 0.1 us)
Async XLA Ops:
  0.0 64.8 %copy-start.5 = (s32[2]{0:T(128)S(1)}, s32[2]{0:T(128)}, u32[]{:S(2)}) copy-start(s32[2]{0:T(128)} %constant.92.clone) | copy-start | bytes 28
  0.0 65.4 %copy-start.1 = (bf16[32,8,1024]{2,1,0:T(8,128)(2,1)S(1)}, bf16[32,8,1024]{2,1,0:T(8,128)(2,1)}, u32[]{:S(2)}) copy-start(bf16[32,8,1024]{2,1,0:T(8,128)(2,1)} %param.6) | copy-start | bytes 1572868
  0.0 64.8 %copy-start.3 = (s32[8]{0:T(128)S(1)}, s32[8]{0:T(128)}, u32[]{:S(2)}) copy-start(s32[8]{0:T(128)} %param.8) | copy-start | bytes 100
  1.2 4.8 %collective-permute-start = (bf16[8,8,1024]{2,1,0:T(8,128)(2,1)S(1)}, bf16[8,8,1024]{2,1,0:T(8,128)(2,1)S(1)}, u32[]{:S(2)}, u32[]{:S(2)}) collective-permute-start(bf16[8,8,1024]{2,1,0:T(8,128)(2,1)S(1)} %get-tuple-element.10), channel_id=1, source_target_pairs={{0,1},{1,0},{2,3},{3,2},{4,5},{5,4},{6,7},{7,6},{8,9},{9,8},{10,11... | collective-permute-start | bytes 393224 | tf_op jit(solution)/shard_map/ppermute | solution.py:133
  1.8 6.9 %collective-permute-start.1 = (bf16[8,8,1024]{2,1,0:T(8,128)(2,1)S(1)}, bf16[8,8,1024]{2,1,0:T(8,128)(2,1)S(1)}, u32[]{:S(2)}, u32[]{:S(2)}) collective-permute-start(bf16[8,8,1024]{2,1,0:T(8,128)(2,1)S(1)} %get-tuple-element.9), channel_id=1, source_target_pairs={{0,2},{1,3},{2,0},{3,1},{4,6},{5,7},{6,4},{7,5},{8,10},{9,11},{10,... | collective-permute-start | bytes 393224 | tf_op jit(solution)/shard_map/ppermute | solution.py:133
  4.4 6.6 %collective-permute-start.2 = (bf16[8,8,1024]{2,1,0:T(8,128)(2,1)S(1)}, bf16[8,8,1024]{2,1,0:T(8,128)(2,1)S(1)}, u32[]{:S(2)}, u32[]{:S(2)}) collective-permute-start(bf16[8,8,1024]{2,1,0:T(8,128)(2,1)S(1)} %get-tuple-element.8), channel_id=1, source_target_pairs={{0,3},{1,2},{2,1},{3,0},{4,7},{5,6},{6,5},{7,4},{8,11},{9,10},{10,... | collective-permute-start | bytes 393224 | tf_op jit(solution)/shard_map/ppermute | solution.py:133
  11.8 14.0 %collective-permute-start.3 = (bf16[4,8,8,1024]{3,2,1,0:T(8,128)(2,1)S(1)}, bf16[4,8,8,1024]{3,2,1,0:T(8,128)(2,1)S(1)}, u32[]{:S(2)}, u32[]{:S(2)}) collective-permute-start(bf16[4,8,8,1024]{3,2,1,0:T(8,128)(2,1)S(1)} %select_select_fusion), channel_id=1, source_target_pairs={{0,4},{1,5},{2,6},{3,7},{4,0},{5,1},{6,2},{7,3},{8,12},{9,13},{10,... | collective-permute-start | bytes 1572872 | tf_op jit(solution)/shard_map/ppermute | solution.py:146
  26.0 25.6 %collective-permute-start.4 = (bf16[4,8,8,1024]{3,2,1,0:T(8,128)(2,1)S(1)}, bf16[4,8,8,1024]{3,2,1,0:T(8,128)(2,1)S(1)}, u32[]{:S(2)}, u32[]{:S(2)}) collective-permute-start(bf16[4,8,8,1024]{3,2,1,0:T(8,128)(2,1)S(1)} %broadcast_select_fusion), channel_id=1, source_target_pairs={{0,8},{1,9},{2,10},{3,11},{4,12},{5,13},{6,14},{7,15},{8,0},{9,1},... | collective-permute-start | bytes 1572872 | tf_op jit(solution)/shard_map/ppermute | solution.py:146
  51.8 14.9 %copy-start = (bf16[1,4,8,8,1024]{4,3,2,1,0:T(8,128)(2,1)}, bf16[1,4,8,8,1024]{4,3,2,1,0:T(8,128)(2,1)S(1)}, u32[]{:S(2)}) copy-start(bf16[1,4,8,8,1024]{4,3,2,1,0:T(8,128)(2,1)S(1)} %select_bitcast_fusion.src_ref) | copy-start | bytes 1572868
  51.8 12.8 %collective-permute-start.5 = (bf16[1,4,8,8,1024]{4,3,2,1,0:T(8,128)(2,1)S(1)}, bf16[1,4,8,8,1024]{4,3,2,1,0:T(8,128)(2,1)S(1)}, u32[]{:S(2)}, u32[]{:S(2)}) collective-permute-start(bf16[1,4,8,8,1024]{4,3,2,1,0:T(8,128)(2,1)S(1)} %select_bitcast_fusion.src_ref), channel_id=1, source_target_pairs={{0,2},{1,3},{2,0},{3,1},{4,6},{5,7},{6,4},{7,5},{8,10},{9,11},{10,... | collective-permute-start | bytes 1572872 | tf_op jit(solution)/shard_map/ppermute | solution.py:172
  64.6 9.8 %copy-start.2 = (bf16[1,4,8,8,1024]{4,3,2,1,0:T(8,128)(2,1)}, bf16[1,4,8,8,1024]{4,3,2,1,0:T(8,128)(2,1)S(1)}, u32[]{:S(2)}) copy-start(bf16[1,4,8,8,1024]{4,3,2,1,0:T(8,128)(2,1)S(1)} %collective-permute-done.5.src_ref) | copy-start | bytes 1572868
  64.7 17.5 %collective-permute-start.6 = (bf16[2,4,8,8,1024]{4,3,2,1,0:T(8,128)(2,1)S(1)}, bf16[2,4,8,8,1024]{4,3,2,1,0:T(8,128)(2,1)}, u32[]{:S(2)}, u32[]{:S(2)}) collective-permute-start(bf16[2,4,8,8,1024]{4,3,2,1,0:T(8,128)(2,1)S(1)} %pad_maximum_fusion), channel_id=1, source_target_pairs={{0,1},{1,0},{2,3},{3,2},{4,5},{5,4},{6,7},{7,6},{8,9},{9,8},{10,11... | collective-permute-start | bytes 3145736 | tf_op jit(solution)/shard_map/ppermute | solution.py:172
  82.2 14.4 %copy-start.4 = (bf16[1024,512,1,1]{1,0,3,2:T(8,128)(2,1)S(1)}, bf16[1024,512,1,1]{1,0,3,2:T(8,128)(2,1)}, u32[]{:S(2)}) copy-start(bf16[1024,512,1,1]{1,0,3,2:T(8,128)(2,1)} %constant.93) | copy-start | bytes 3145732
  103.9 2.2 %collective-permute-start.7 = (f32[4,32]{1,0:T(4,128)S(1)}, f32[4,32]{1,0:T(4,128)S(1)}, u32[]{:S(2)}, u32[]{:S(2)}) collective-permute-start(f32[4,32]{1,0:T(4,128)S(1)} %get-tuple-element.14), channel_id=1, source_target_pairs={{0,1},{1,0},{2,3},{3,2},{4,5},{5,4},{6,7},{7,6},{8,9},{9,8},{10,11... | collective-permute-start | bytes 1544 | tf_op jit(solution)/shard_map/ppermute | solution.py:185
  104.4 3.6 %collective-permute-start.8 = (f32[4,32]{1,0:T(4,128)S(1)}, f32[4,32]{1,0:T(4,128)S(1)}, u32[]{:S(2)}, u32[]{:S(2)}) collective-permute-start(f32[4,32]{1,0:T(4,128)S(1)} %get-tuple-element.14), channel_id=1, source_target_pairs={{0,2},{1,3},{2,0},{3,1},{4,6},{5,7},{6,4},{7,5},{8,10},{9,11},{10,... | collective-permute-start | bytes 1544 | tf_op jit(solution)/shard_map/ppermute | solution.py:185
  106.0 3.0 %collective-permute-start.9 = (f32[4,32]{1,0:T(4,128)S(1)}, f32[4,32]{1,0:T(4,128)S(1)}, u32[]{:S(2)}, u32[]{:S(2)}) collective-permute-start(f32[4,32]{1,0:T(4,128)S(1)} %get-tuple-element.14), channel_id=1, source_target_pairs={{0,3},{1,2},{2,1},{3,0},{4,7},{5,6},{6,5},{7,4},{8,11},{9,10},{10,... | collective-permute-start | bytes 1544 | tf_op jit(solution)/shard_map/ppermute | solution.py:185
  109.0 6.1 %collective-permute-start.10 = (f32[4,32]{1,0:T(4,128)S(1)}, f32[4,32]{1,0:T(4,128)S(1)}, u32[]{:S(2)}, u32[]{:S(2)}) collective-permute-start(f32[4,32]{1,0:T(4,128)S(1)} %maximum_maximum_fusion), channel_id=1, source_target_pairs={{0,4},{1,5},{2,6},{3,7},{4,8},{5,9},{6,10},{7,11},{8,12},{9,13},{1... | collective-permute-start | bytes 1544 | tf_op jit(solution)/shard_map/ppermute | solution.py:191
  110.7 4.9 %collective-permute-start.11 = (f32[4,32]{1,0:T(4,128)S(1)}, f32[4,32]{1,0:T(4,128)S(1)}, u32[]{:S(2)}, u32[]{:S(2)}) collective-permute-start(f32[4,32]{1,0:T(4,128)S(1)} %maximum_maximum_fusion), channel_id=1, source_target_pairs={{0,8},{1,9},{2,10},{3,11},{4,12},{5,13},{6,14},{7,15},{8,0},{9,1},... | collective-permute-start | bytes 1544 | tf_op jit(solution)/shard_map/ppermute | solution.py:191
  114.1 3.6 %collective-permute-start.12 = (f32[4,32]{1,0:T(4,128)S(1)}, f32[4,32]{1,0:T(4,128)S(1)}, u32[]{:S(2)}, u32[]{:S(2)}) collective-permute-start(f32[4,32]{1,0:T(4,128)S(1)} %maximum_maximum_fusion), channel_id=1, source_target_pairs={{0,12},{1,13},{2,14},{3,15},{4,0},{5,1},{6,2},{7,3},{8,4},{9,5},{1... | collective-permute-start | bytes 1544 | tf_op jit(solution)/shard_map/ppermute | solution.py:191

commit v7 on v6

--- a/solution.py
+++ b/solution.py
@@ -32,23 +32,26 @@
     out_ref = rest[-1]
     bins = src_ref.shape[-1] // 2
     windows = src_ref.shape[3]
-    rows = rcv_ref.shape[1]
+    rows = rcv_ref.shape[2]
 
     def body(s, carry):
         row = src_ref[0, 0, s].astype(jnp.float32)
         for c in range(rows // RC):
             rs = slice(c * RC, (c + 1) * RC)
-            acc_re = jnp.zeros((RC, bins), jnp.float32)
-            acc_im = jnp.zeros((RC, bins), jnp.float32)
+            acc1 = jnp.zeros((RC, bins), jnp.float32)
+            acc2 = jnp.zeros((RC, bins), jnp.float32)
+            acc3 = jnp.zeros((RC, bins), jnp.float32)
             for w in range(windows):
-                a = jnp.broadcast_to(row[w : w + 1, :bins], (RC, bins))
-                b = jnp.broadcast_to(row[w : w + 1, bins:], (RC, bins))
-                rr = rcv_ref[w, rs, :bins]
-                ri = rcv_ref[w, rs, bins:]
-                acc_re = acc_re + (a * rr + b * ri)
-                acc_im = acc_im + (a * ri - b * rr)
-            out_ref[0, s, rs, :bins] = acc_re.astype(out_ref.dtype)
-            out_ref[0, s, rs, bins:] = acc_im.astype(out_ref.dtype)
+                a = row[w : w + 1, :bins]
+                b = row[w : w + 1, bins:]
+                amb = jnp.broadcast_to(a - b, (RC, bins))
+                a = jnp.broadcast_to(a, (RC, bins))
+                b = jnp.broadcast_to(b, (RC, bins))
+                acc1 = acc1 + rcv_ref[0, w, rs, :] * amb
+                acc2 = acc2 + rcv_ref[1, w, rs, :] * a
+                acc3 = acc3 + rcv_ref[2, w, rs, :] * b
+            out_ref[0, s, rs, :bins] = (acc1 + acc3).astype(out_ref.dtype)
+            out_ref[0, s, rs, bins:] = (acc1 + acc2).astype(out_ref.dtype)
         return carry
 
     lax.fori_loop(0, src_ref.shape[2], body, 0)
@@ -56,12 +59,12 @@
 
 def cross_part(entries, pos, rcv_t, buf=None):
     m, nb, piece, windows, width = entries.shape
-    receivers = rcv_t.shape[1]
+    receivers = rcv_t.shape[2]
     qc = SOURCE // piece
-    flops = 8 * nb * m * piece * receivers * windows * (width // 2)
+    flops = 6 * nb * m * piece * receivers * windows * (width // 2)
     in_specs = [
         pl.BlockSpec((1, 1, piece, windows, width), lambda k, i, o: (i, k, 0, 0, 0)),
-        pl.BlockSpec((windows, receivers, width), lambda k, i, o: (0, 0, 0)),
+        pl.BlockSpec((3, windows, receivers, width // 2), lambda k, i, o: (0, 0, 0, 0)),
     ]
     args = [pos, entries, rcv_t]
     aliases = {}
@@ -143,7 +146,9 @@
             mine = payload
             d = 1
             while d < zc:
-                got = lax.ppermute(mine, "chan", pairs_of(n, lambda i, d=d: (((i // qc) ^ d) * qc) + i % qc))
+                got = lax.ppermute(
+                    mine, "chan", pairs_of(n, lambda i, d=d: (((i // qc) ^ d) * qc) + i % qc)
+                )
                 valid = (((zk ^ z) & ~(d - 1)) == 0)[:, None, None, None]
                 mine = jnp.where(valid, mine, got)
                 d *= 2
@@ -164,6 +169,8 @@
         lag_table = build_table(bins, LAGS)
         window_mask = window_valid.astype(jnp.float32)[:, None, None]
         rcv_t = jnp.transpose(spectra, (1, 0, 2)).astype(jnp.float32) * window_mask
+        rc, rd = rcv_t[..., :bins], rcv_t[..., bins:]
+        rcv_t = jnp.stack([rc, rd - rc, rc + rd])
 
         cross = cross_part(mine[None], q[None].astype(jnp.int32), rcv_t)
         offs = [0]

time: 121 us -> 119 us (0.983)
  Pallas kernels: 30 us -> 25.1 us
  other arithmetic: 5.93 us -> 7.64 us
    pallas_call x3, Pallas kernels: 30 us -> 25.1 us  [cross_part(): pl.pallas_call(cross_kernel, grid_spec=pltpu.PrefetchScalarGridSpec(num_s...]
    another operation x0 -> x2, other arithmetic: none -> 1.52 us  [shards(): rcv_t = jnp.stack([rc, rd - rc, rc + rd])]
  transfers between devices with their start and end apart: 13 -> 13, of which waited for: 10 -> 10; matrix products, arithmetic and copies ran while one was open for 3% -> 3% of each run, Pallas kernels for 13% -> 11%
where the time goes in v7:
time: 119 us
  waiting for transfers between devices  58.1 us (49%)
  Pallas kernels  25.1 us (21%)
  starting transfers between devices  16.5 us (14%)
  other arithmetic  7.64 us (6%)
  matrix products  7.25 us (6%)
  local copies, waits for them, and re-layouts  4.37 us (4%)
    ppermute x2, waiting for transfers between devices, shards(): lax.ppermute(mine, 'chan', pairs_of(n, lambda i, d=d: (i // qc ^ d) * qc...  35.3 us
    pallas_call x3, Pallas kernels, cross_part(): pl.pallas_call(cross_kernel, grid_spec=pltpu.PrefetchScalarGridSpec(num_s...  25.1 us
    ppermute x2, waiting for transfers between devices, shards(): lax.ppermute(jnp.stack(held), 'chan', pairs_of(n, lambda i, b=b: i // qc...  11.2 us
    dot_general x1, matrix products, shards(): jnp.dot(cross.reshape(nb * SOURCE * receivers, width), lag_table, preferr...  7.25 us
    ppermute x3, starting transfers between devices, shards(): lax.ppermute(peak, 'chan', pairs_of(n, lambda i, d=d: (i // qc + d) % zc...  5.07 us
    ppermute x3, waiting for transfers between devices, shards(): lax.ppermute(send, 'chan', pairs_of(n, lambda i, d=d: i // qc * qc + (i %...  5.01 us
    ppermute x2, starting transfers between devices, shards(): lax.ppermute(mine, 'chan', pairs_of(n, lambda i, d=d: (i // qc ^ d) * qc...  4.4 us
    ppermute x3, waiting for transfers between devices, shards(): lax.ppermute(peak, 'chan', pairs_of(n, lambda i, d=d: (i // qc + d) % zc...  3.58 us
  transfers between devices with their start and end apart: 13, of which 10 were waited for; matrix products, arithmetic and copies ran while one was open for 3% of the time, Pallas kernels for 11%

profile of v7, /device:TPU:0, one launch (start us, length us, event | category | flops | bytes accessed | tf_op | source)
XLA Modules:
  0.0 119.0 jit_solution(15640551922914073820)
XLA Ops:
  0.0 0.0 copy-start.1
  0.0 0.0 copy-start.4
  0.0 0.0 copy-start.6
  0.0 1.2 %constant_dynamic-slice_fusion = (bf16[1,8,8,1024]{3,2,1,0:T(8,128)(2,1)S(1)}, bf16[8,8,1024]{2,1,0:T(8,128)(2,1)S(1)}, bf16[8,8,1024]{2,1,0:T(8,128)(2,1)S(1)}, bf16[8,8,1024]{2,1,0:T(8,128)(2,1)S(1)}) fusion(bf16[4,8,8,1024]{3,2,1,0:T(8,128)(2,1)} %bitcast.29, s32[]{:T(128)S(6)} %select_n.90, s32[]{:T(128)S(6)} %select_n.93, s32[]{:T(128)S(6)} %select_n.92, ...), kind=kLoop, calls=%fused_computation.30 | loop fusion | bytes 1048592 | tf_op jit(solution)/shard_map/jit(dynamic_index_in_dim)/dynamic_slice | solution.py:132
  1.2 0.6 collective-permute-start
  1.8 2.6 %collective-permute-start.1 = (bf16[8,8,1024]{2,1,0:T(8,128)(2,1)S(1)}, bf16[8,8,1024]{2,1,0:T(8,128)(2,1)S(1)}, u32[]{:S(2)}, u32[]{:S(2)}) collective-permute-start(bf16[8,8,1024]{2,1,0:T(8,128)(2,1)S(1)} %get-tuple-element.12), channel_id=1, source_target_pairs={{0,2},{1,3},{2,0},{3,1},{4,6},{5,7},{6,4},{7,5},{8,10},{9,11},{10,... | collective-permute-start | bytes 393224 | tf_op jit(solution)/shard_map/ppermute | solution.py:136
  4.3 0.0 collective-permute-start.2
  4.4 0.8 reshape.141
  5.1 0.8 reshape.139
  6.0 0.0 collective-permute-done
  6.0 2.7 %collective-permute-done.1 = bf16[8,8,1024]{2,1,0:T(8,128)(2,1)S(1)} collective-permute-done((bf16[8,8,1024]{2,1,0:T(8,128)(2,1)S(1)}, bf16[8,8,1024]{2,1,0:T(8,128)(2,1)S(1)}, u32[]{:S(2)}, u32[]{:S(2)}) %collective-permute-start.1) | collective-permute-done | bytes 131104 | tf_op jit(solution)/shard_map/ppermute | solution.py:136
  8.7 2.3 %collective-permute-done.2 = bf16[8,8,1024]{2,1,0:T(8,128)(2,1)S(1)} collective-permute-done((bf16[8,8,1024]{2,1,0:T(8,128)(2,1)S(1)}, bf16[8,8,1024]{2,1,0:T(8,128)(2,1)S(1)}, u32[]{:S(2)}, u32[]{:S(2)}) %collective-permute-start.2) | collective-permute-done | bytes 131104 | tf_op jit(solution)/shard_map/ppermute | solution.py:136
  11.0 0.1 pad_maximum_fusion.2
  11.1 0.6 gather_fusion
  11.6 0.1 select_select_fusion
  11.8 1.6 %collective-permute-start.3 = (bf16[4,8,8,1024]{3,2,1,0:T(8,128)(2,1)S(1)}, bf16[4,8,8,1024]{3,2,1,0:T(8,128)(2,1)S(1)}, u32[]{:S(2)}, u32[]{:S(2)}) collective-permute-start(bf16[4,8,8,1024]{3,2,1,0:T(8,128)(2,1)S(1)} %select_select_fusion), channel_id=1, source_target_pairs={{0,4},{1,5},{2,6},{3,7},{4,0},{5,1},{6,2},{7,3},{8,12},{9,13},{10,... | collective-permute-start | bytes 1572872 | tf_op jit(solution)/shard_map/ppermute | solution.py:149
  13.4 12.5 %collective-permute-done.3 = bf16[4,8,8,1024]{3,2,1,0:T(8,128)(2,1)S(1)} collective-permute-done((bf16[4,8,8,1024]{3,2,1,0:T(8,128)(2,1)S(1)}, bf16[4,8,8,1024]{3,2,1,0:T(8,128)(2,1)S(1)}, u32[]{:S(2)}, u32[]{:S(2)}) %collective-permute-start.3) | collective-permute-done | bytes 524320 | tf_op jit(solution)/shard_map/ppermute | solution.py:149
  25.8 0.1 broadcast_select_fusion
  26.0 2.8 %collective-permute-start.4 = (bf16[4,8,8,1024]{3,2,1,0:T(8,128)(2,1)S(1)}, bf16[4,8,8,1024]{3,2,1,0:T(8,128)(2,1)S(1)}, u32[]{:S(2)}, u32[]{:S(2)}) collective-permute-start(bf16[4,8,8,1024]{3,2,1,0:T(8,128)(2,1)S(1)} %broadcast_select_fusion), channel_id=1, source_target_pairs={{0,8},{1,9},{2,10},{3,11},{4,12},{5,13},{6,14},{7,15},{8,0},{9,1},... | collective-permute-start | bytes 1572872 | tf_op jit(solution)/shard_map/ppermute | solution.py:149
  28.8 22.8 %collective-permute-done.4 = bf16[4,8,8,1024]{3,2,1,0:T(8,128)(2,1)S(1)} collective-permute-done((bf16[4,8,8,1024]{3,2,1,0:T(8,128)(2,1)S(1)}, bf16[4,8,8,1024]{3,2,1,0:T(8,128)(2,1)S(1)}, u32[]{:S(2)}, u32[]{:S(2)}) %collective-permute-start.4) | collective-permute-done | bytes 524320 | tf_op jit(solution)/shard_map/ppermute | solution.py:149
  51.6 0.1 select_bitcast_fusion.src_ref
  51.7 0.0 copy-start
  51.7 1.6 %collective-permute-start.5 = (bf16[1,4,8,8,1024]{4,3,2,1,0:T(8,128)(2,1)S(1)}, bf16[1,4,8,8,1024]{4,3,2,1,0:T(8,128)(2,1)S(1)}, u32[]{:S(2)}, u32[]{:S(2)}) collective-permute-start(bf16[1,4,8,8,1024]{4,3,2,1,0:T(8,128)(2,1)S(1)} %select_bitcast_fusion.src_ref), channel_id=1, source_target_pairs={{0,2},{1,3},{2,0},{3,1},{4,6},{5,7},{6,4},{7,5},{8,10},{9,11},{10,... | collective-permute-start | bytes 1572872 | tf_op jit(solution)/shard_map/ppermute | solution.py:179
  53.4 11.2 %collective-permute-done.5.src_ref = bf16[1,4,8,8,1024]{4,3,2,1,0:T(8,128)(2,1)S(1)} collective-permute-done((bf16[1,4,8,8,1024]{4,3,2,1,0:T(8,128)(2,1)S(1)}, bf16[1,4,8,8,1024]{4,3,2,1,0:T(8,128)(2,1)S(1)}, u32[]{:S(2)}, u32[]{:S(2)}) %collective-permute-start.5) | collective-permute-done | bytes 524320 | tf_op jit(solution)/shard_map/ppermute | solution.py:179
  64.6 0.0 copy-start.2
  64.6 1.2 %pad_maximum_fusion.1 = bf16[2,4,8,8,1024]{4,3,2,1,0:T(8,128)(2,1)} fusion(bf16[1,4,8,8,1024]{4,3,2,1,0:T(8,128)(2,1)S(1)} %collective-permute-done.5.src_ref, bf16[1,4,8,8,1024]{4,3,2,1,0:T(8,128)(2,1)S(1)} %select_bitcast_fusion.src_ref), kind=kLoop, calls=%fused_computation.4 | loop fusion | flops 524288 | bytes 2097152 | tf_op jit(solution)/shard_map/stack | solution.py:180
  65.8 0.0 collective-permute-start.6
  65.8 0.0 copy-done.4
  65.8 0.0 copy-done.1
  65.8 0.3 multiply_bitcast_fusion
  66.2 0.2 slice_bitcast_fusion
  66.4 1.3 %pad_maximum_fusion.rcv_ref = f32[3,8,32,512]{3,2,1,0:T(8,128)} fusion(f32[1,8,32,512]{3,2,1,0:T(8,128)S(1)} %get-tuple-element.8, f32[1,8,32,512]{3,2,1,0:T(8,128)S(1)} %get-tuple-element.9, f32[1,8,32,512]{3,2,1,0:T(8,128)S(1)} %get-tuple-element.7), kind=kLoop, calls=%fused_computation.3 | loop fusion | flops 786432 | bytes 3145728 | tf_op jit(solution)/shard_map/stack | solution.py:173
  67.7 0.0 copy-done.6
  67.7 0.6 broadcast_xor_fusion.pos_ref
  68.3 0.0 copy-done
  68.3 6.6 %shard_map.64.rest_0_ = bf16[4,32,32,1024]{3,2,1,0:T(8,128)(2,1)} custom-call(s32[1]{0:T(128)} %bitcast.13.pos_ref, bf16[1,4,8,8,1024]{4,3,2,1,0:T(8,128)(2,1)} %copy-done, f32[3,8,32,512]{3,2,1,0:T(8,128)} %pad_maximum_fusion.rcv_ref), custom_call_target="tpu_custom_call" | custom-call | flops 25165824 | bytes 4194304 | tf_op jit(solution)/shard_map/pallas_call | solution.py:75
  74.9 0.0 copy-done.2
  74.9 6.6 %shard_map.65.rest_0_ = bf16[4,32,32,1024]{3,2,1,0:T(8,128)(2,1)} custom-call(s32[1]{0:T(128)S(6)} %xor.67.pos_ref, bf16[1,4,8,8,1024]{4,3,2,1,0:T(8,128)(2,1)} %copy-done.2, f32[3,8,32,512]{3,2,1,0:T(8,128)} %pad_maximum_fusion.rcv_ref, bf16[4,32,32,1024]{3,2,1,0:T(8,128)(2,1)} %shard_map.64.rest_0_), custom_call_target="tpu_custom_call", output_to_operand_aliasing={{}: (3, {})} | custom-call | flops 25165824 | bytes 4194304 | tf_op jit(solution)/shard_map/pallas_call | solution.py:75
  81.5 0.0 copy-start.5
  81.5 0.0 collective-permute-done.6.src_ref
  81.5 0.0 copy-start.3
  81.5 1.1 copy-done.3
  82.6 11.9 %shard_map.66 = bf16[4,32,32,1024]{3,2,1,0:T(8,128)(2,1)} custom-call(s32[2]{0:T(128)} %broadcast_xor_fusion.pos_ref, bf16[2,4,8,8,1024]{4,3,2,1,0:T(8,128)(2,1)} %copy-done.3, f32[3,8,32,512]{3,2,1,0:T(8,128)} %pad_maximum_fusion.rcv_ref, bf16[4,32,32,1024]{3,2,1,0:T(8,128)(2,1)} %shard_map.65.rest_0_), custom_call_target="tpu_custom_call", output_to_operand_aliasing={{}: (3, {})} | custom-call | flops 50331648 | bytes 6815744 | tf_op jit(solution)/shard_map/pallas_call | solution.py:75
  94.4 0.0 copy-done.5
  94.4 7.2 %abs_reduce_fusion = (f32[4,32]{1,0:T(4,128)S(1)}, f32[4,32,32,512]{3,2,1,0:T(8,128)S(1)}) fusion(bf16[4,32,32,1024]{3,2,1,0:T(8,128)(2,1)} %shard_map.66, bf16[1024,512,1,1]{1,0,3,2:T(8,128)(2,1)S(1)} %copy-done.5), kind=kOutput, calls=%fused_computation.2 | convolution fusion | flops 4299161600 | bytes 17826304 | tf_op jit(solution)/shard_map/dot_general | solution.py:187
  101.7 0.6 collective-permute-start.7
  102.2 1.6 %collective-permute-start.8 = (f32[4,32]{1,0:T(4,128)S(1)}, f32[4,32]{1,0:T(4,128)S(1)}, u32[]{:S(2)}, u32[]{:S(2)}) collective-permute-start(f32[4,32]{1,0:T(4,128)S(1)} %get-tuple-element.17), channel_id=1, source_target_pairs={{0,2},{1,3},{2,0},{3,1},{4,6},{5,7},{6,4},{7,5},{8,10},{9,11},{10,... | collective-permute-start | bytes 1544 | tf_op jit(solution)/shard_map/ppermute | solution.py:192
  103.9 0.0 collective-permute-start.9
  103.9 0.0 collective-permute-done.7
  103.9 1.9 %collective-permute-done.8 = f32[4,32]{1,0:T(4,128)S(1)} collective-permute-done((f32[4,32]{1,0:T(4,128)S(1)}, f32[4,32]{1,0:T(4,128)S(1)}, u32[]{:S(2)}, u32[]{:S(2)}) %collective-permute-start.8) | collective-permute-done | bytes 544 | tf_op jit(solution)/shard_map/ppermute | solution.py:192
  105.8 1.1 collective-permute-done.9
  106.9 1.7 %collective-permute-start.10 = (f32[4,32]{1,0:T(4,128)S(1)}, f32[4,32]{1,0:T(4,128)S(1)}, u32[]{:S(2)}, u32[]{:S(2)}) collective-permute-start(f32[4,32]{1,0:T(4,128)S(1)} %maximum_maximum_fusion), channel_id=1, source_target_pairs={{0,4},{1,5},{2,6},{3,7},{4,8},{5,9},{6,10},{7,11},{8,12},{9,13},{1... | collective-permute-start | bytes 1544 | tf_op jit(solution)/shard_map/ppermute | solution.py:198
  108.6 3.4 %collective-permute-start.11 = (f32[4,32]{1,0:T(4,128)S(1)}, f32[4,32]{1,0:T(4,128)S(1)}, u32[]{:S(2)}, u32[]{:S(2)}) collective-permute-start(f32[4,32]{1,0:T(4,128)S(1)} %maximum_maximum_fusion), channel_id=1, source_target_pairs={{0,8},{1,9},{2,10},{3,11},{4,12},{5,13},{6,14},{7,15},{8,0},{9,1},... | collective-permute-start | bytes 1544 | tf_op jit(solution)/shard_map/ppermute | solution.py:198
  112.0 0.0 collective-permute-start.12
  112.0 1.0 collective-permute-done.10
  113.0 0.6 collective-permute-done.11
  113.5 2.0 %collective-permute-done.12 = f32[4,32]{1,0:T(4,128)S(1)} collective-permute-done((f32[4,32]{1,0:T(4,128)S(1)}, f32[4,32]{1,0:T(4,128)S(1)}, u32[]{:S(2)}, u32[]{:S(2)}) %collective-permute-start.12) | collective-permute-done | bytes 544 | tf_op jit(solution)/shard_map/ppermute | solution.py:198
  115.5 3.5 %divide_convert_fusion = bf16[4,32,32,512]{3,2,1,0:T(8,128)(2,1)} fusion(f32[4,32,32,512]{3,2,1,0:T(8,128)S(1)} %get-tuple-element.18, f32[4,32]{1,0:T(4,128)S(1)} %maximum_add_fusion), kind=kLoop, calls=%fused_computation.1 | loop fusion | flops 4194304 | bytes 12583424 | tf_op jit(solution)/shard_map/convert_element_type | solution.py:203
  (7 shorter events, 0.1 us)
Async XLA Ops:
  0.0 65.8 %copy-start.1 = (bf16[32,8,1024]{2,1,0:T(8,128)(2,1)S(1)}, bf16[32,8,1024]{2,1,0:T(8,128)(2,1)}, u32[]{:S(2)}) copy-start(bf16[32,8,1024]{2,1,0:T(8,128)(2,1)} %param.6) | copy-start | bytes 1572868
  0.0 65.8 %copy-start.4 = (s32[8]{0:T(128)S(1)}, s32[8]{0:T(128)}, u32[]{:S(2)}) copy-start(s32[8]{0:T(128)} %param.8) | copy-start | bytes 100
  0.0 67.7 %copy-start.6 = (s32[2]{0:T(128)S(1)}, s32[2]{0:T(128)}, u32[]{:S(2)}) copy-start(s32[2]{0:T(128)} %constant.92.clone) | copy-start | bytes 28
  1.2 4.8 %collective-permute-start = (bf16[8,8,1024]{2,1,0:T(8,128)(2,1)S(1)}, bf16[8,8,1024]{2,1,0:T(8,128)(2,1)S(1)}, u32[]{:S(2)}, u32[]{:S(2)}) collective-permute-start(bf16[8,8,1024]{2,1,0:T(8,128)(2,1)S(1)} %get-tuple-element.13), channel_id=1, source_target_pairs={{0,1},{1,0},{2,3},{3,2},{4,5},{5,4},{6,7},{7,6},{8,9},{9,8},{10,11... | collective-permute-start | bytes 393224 | tf_op jit(solution)/shard_map/ppermute | solution.py:136
  1.8 6.9 %collective-permute-start.1 = (bf16[8,8,1024]{2,1,0:T(8,128)(2,1)S(1)}, bf16[8,8,1024]{2,1,0:T(8,128)(2,1)S(1)}, u32[]{:S(2)}, u32[]{:S(2)}) collective-permute-start(bf16[8,8,1024]{2,1,0:T(8,128)(2,1)S(1)} %get-tuple-element.12), channel_id=1, source_target_pairs={{0,2},{1,3},{2,0},{3,1},{4,6},{5,7},{6,4},{7,5},{8,10},{9,11},{10,... | collective-permute-start | bytes 393224 | tf_op jit(solution)/shard_map/ppermute | solution.py:136
  4.3 6.6 %collective-permute-start.2 = (bf16[8,8,1024]{2,1,0:T(8,128)(2,1)S(1)}, bf16[8,8,1024]{2,1,0:T(8,128)(2,1)S(1)}, u32[]{:S(2)}, u32[]{:S(2)}) collective-permute-start(bf16[8,8,1024]{2,1,0:T(8,128)(2,1)S(1)} %get-tuple-element.11), channel_id=1, source_target_pairs={{0,3},{1,2},{2,1},{3,0},{4,7},{5,6},{6,5},{7,4},{8,11},{9,10},{10,... | collective-permute-start | bytes 393224 | tf_op jit(solution)/shard_map/ppermute | solution.py:136
  11.8 14.0 %collective-permute-start.3 = (bf16[4,8,8,1024]{3,2,1,0:T(8,128)(2,1)S(1)}, bf16[4,8,8,1024]{3,2,1,0:T(8,128)(2,1)S(1)}, u32[]{:S(2)}, u32[]{:S(2)}) collective-permute-start(bf16[4,8,8,1024]{3,2,1,0:T(8,128)(2,1)S(1)} %select_select_fusion), channel_id=1, source_target_pairs={{0,4},{1,5},{2,6},{3,7},{4,0},{5,1},{6,2},{7,3},{8,12},{9,13},{10,... | collective-permute-start | bytes 1572872 | tf_op jit(solution)/shard_map/ppermute | solution.py:149
  26.0 25.6 %collective-permute-start.4 = (bf16[4,8,8,1024]{3,2,1,0:T(8,128)(2,1)S(1)}, bf16[4,8,8,1024]{3,2,1,0:T(8,128)(2,1)S(1)}, u32[]{:S(2)}, u32[]{:S(2)}) collective-permute-start(bf16[4,8,8,1024]{3,2,1,0:T(8,128)(2,1)S(1)} %broadcast_select_fusion), channel_id=1, source_target_pairs={{0,8},{1,9},{2,10},{3,11},{4,12},{5,13},{6,14},{7,15},{8,0},{9,1},... | collective-permute-start | bytes 1572872 | tf_op jit(solution)/shard_map/ppermute | solution.py:149
  51.7 16.5 %copy-start = (bf16[1,4,8,8,1024]{4,3,2,1,0:T(8,128)(2,1)}, bf16[1,4,8,8,1024]{4,3,2,1,0:T(8,128)(2,1)S(1)}, u32[]{:S(2)}) copy-start(bf16[1,4,8,8,1024]{4,3,2,1,0:T(8,128)(2,1)S(1)} %select_bitcast_fusion.src_ref) | copy-start | bytes 1572868
  51.7 12.8 %collective-permute-start.5 = (bf16[1,4,8,8,1024]{4,3,2,1,0:T(8,128)(2,1)S(1)}, bf16[1,4,8,8,1024]{4,3,2,1,0:T(8,128)(2,1)S(1)}, u32[]{:S(2)}, u32[]{:S(2)}) collective-permute-start(bf16[1,4,8,8,1024]{4,3,2,1,0:T(8,128)(2,1)S(1)} %select_bitcast_fusion.src_ref), channel_id=1, source_target_pairs={{0,2},{1,3},{2,0},{3,1},{4,6},{5,7},{6,4},{7,5},{8,10},{9,11},{10,... | collective-permute-start | bytes 1572872 | tf_op jit(solution)/shard_map/ppermute | solution.py:179
  64.6 10.3 %copy-start.2 = (bf16[1,4,8,8,1024]{4,3,2,1,0:T(8,128)(2,1)}, bf16[1,4,8,8,1024]{4,3,2,1,0:T(8,128)(2,1)S(1)}, u32[]{:S(2)}) copy-start(bf16[1,4,8,8,1024]{4,3,2,1,0:T(8,128)(2,1)S(1)} %collective-permute-done.5.src_ref) | copy-start | bytes 1572868
  65.8 15.7 %collective-permute-start.6 = (bf16[2,4,8,8,1024]{4,3,2,1,0:T(8,128)(2,1)}, bf16[2,4,8,8,1024]{4,3,2,1,0:T(8,128)(2,1)S(1)}, u32[]{:S(2)}, u32[]{:S(2)}) collective-permute-start(bf16[2,4,8,8,1024]{4,3,2,1,0:T(8,128)(2,1)} %pad_maximum_fusion.1), channel_id=1, source_target_pairs={{0,1},{1,0},{2,3},{3,2},{4,5},{5,4},{6,7},{7,6},{8,9},{9,8},{10,11... | collective-permute-start | bytes 3145736 | tf_op jit(solution)/shard_map/ppermute | solution.py:179
  81.5 12.9 %copy-start.5 = (bf16[1024,512,1,1]{1,0,3,2:T(8,128)(2,1)S(1)}, bf16[1024,512,1,1]{1,0,3,2:T(8,128)(2,1)}, u32[]{:S(2)}) copy-start(bf16[1024,512,1,1]{1,0,3,2:T(8,128)(2,1)} %constant.93) | copy-start | bytes 3145732
  81.5 1.1 copy-start.3
  101.7 2.2 %collective-permute-start.7 = (f32[4,32]{1,0:T(4,128)S(1)}, f32[4,32]{1,0:T(4,128)S(1)}, u32[]{:S(2)}, u32[]{:S(2)}) collective-permute-start(f32[4,32]{1,0:T(4,128)S(1)} %get-tuple-element.17), channel_id=1, source_target_pairs={{0,1},{1,0},{2,3},{3,2},{4,5},{5,4},{6,7},{7,6},{8,9},{9,8},{10,11... | collective-permute-start | bytes 1544 | tf_op jit(solution)/shard_map/ppermute | solution.py:192
  102.2 3.6 %collective-permute-start.8 = (f32[4,32]{1,0:T(4,128)S(1)}, f32[4,32]{1,0:T(4,128)S(1)}, u32[]{:S(2)}, u32[]{:S(2)}) collective-permute-start(f32[4,32]{1,0:T(4,128)S(1)} %get-tuple-element.17), channel_id=1, source_target_pairs={{0,2},{1,3},{2,0},{3,1},{4,6},{5,7},{6,4},{7,5},{8,10},{9,11},{10,... | collective-permute-start | bytes 1544 | tf_op jit(solution)/shard_map/ppermute | solution.py:192
  103.9 3.0 %collective-permute-start.9 = (f32[4,32]{1,0:T(4,128)S(1)}, f32[4,32]{1,0:T(4,128)S(1)}, u32[]{:S(2)}, u32[]{:S(2)}) collective-permute-start(f32[4,32]{1,0:T(4,128)S(1)} %get-tuple-element.17), channel_id=1, source_target_pairs={{0,3},{1,2},{2,1},{3,0},{4,7},{5,6},{6,5},{7,4},{8,11},{9,10},{10,... | collective-permute-start | bytes 1544 | tf_op jit(solution)/shard_map/ppermute | solution.py:192
  106.9 6.1 %collective-permute-start.10 = (f32[4,32]{1,0:T(4,128)S(1)}, f32[4,32]{1,0:T(4,128)S(1)}, u32[]{:S(2)}, u32[]{:S(2)}) collective-permute-start(f32[4,32]{1,0:T(4,128)S(1)} %maximum_maximum_fusion), channel_id=1, source_target_pairs={{0,4},{1,5},{2,6},{3,7},{4,8},{5,9},{6,10},{7,11},{8,12},{9,13},{1... | collective-permute-start | bytes 1544 | tf_op jit(solution)/shard_map/ppermute | solution.py:198
  108.6 4.9 %collective-permute-start.11 = (f32[4,32]{1,0:T(4,128)S(1)}, f32[4,32]{1,0:T(4,128)S(1)}, u32[]{:S(2)}, u32[]{:S(2)}) collective-permute-start(f32[4,32]{1,0:T(4,128)S(1)} %maximum_maximum_fusion), channel_id=1, source_target_pairs={{0,8},{1,9},{2,10},{3,11},{4,12},{5,13},{6,14},{7,15},{8,0},{9,1},... | collective-permute-start | bytes 1544 | tf_op jit(solution)/shard_map/ppermute | solution.py:198
  112.0 3.6 %collective-permute-start.12 = (f32[4,32]{1,0:T(4,128)S(1)}, f32[4,32]{1,0:T(4,128)S(1)}, u32[]{:S(2)}, u32[]{:S(2)}) collective-permute-start(f32[4,32]{1,0:T(4,128)S(1)} %maximum_maximum_fusion), channel_id=1, source_target_pairs={{0,12},{1,13},{2,14},{3,15},{4,0},{5,1},{6,2},{7,3},{8,4},{9,5},{1... | collective-permute-start | bytes 1544 | tf_op jit(solution)/shard_map/ppermute | solution.py:198

commit v8 on v7

--- a/solution.py
+++ b/solution.py
@@ -172,18 +172,28 @@
         rc, rd = rcv_t[..., :bins], rcv_t[..., bins:]
         rcv_t = jnp.stack([rc, rd - rc, rc + rd])
 
-        cross = cross_part(mine[None], q[None].astype(jnp.int32), rcv_t)
-        offs = [0]
-        held = [mine]
-        for b in plane_bits:
-            got = lax.ppermute(
-                jnp.stack(held), "chan", pairs_of(n, lambda i, b=b: (i // qc) * qc + ((i % qc) ^ b))
-            )
-            new_offs = [o ^ b for o in offs]
-            pos = q ^ jnp.array(new_offs, jnp.int32)
-            cross = cross_part(got, pos, rcv_t, cross)
-            offs = offs + new_offs
-            held = held + [got[i] for i in range(got.shape[0])]
+        def xor_pairs(b):
+            return pairs_of(n, lambda i: (i // qc) * qc + ((i % qc) ^ b))
+
+        if qc == 4:
+            from_y = lax.ppermute(mine, "chan", xor_pairs(2))
+            from_c = lax.ppermute(mine, "chan", xor_pairs(1))
+            cross = cross_part(mine[None], q[None].astype(jnp.int32), rcv_t)
+            cross = cross_part(from_c[None], (q ^ 1)[None].astype(jnp.int32), rcv_t, cross)
+            from_yc = lax.ppermute(from_y, "chan", xor_pairs(1))
+            cross = cross_part(from_y[None], (q ^ 2)[None].astype(jnp.int32), rcv_t, cross)
+            cross = cross_part(from_yc[None], (q ^ 3)[None].astype(jnp.int32), rcv_t, cross)
+        else:
+            cross = cross_part(mine[None], q[None].astype(jnp.int32), rcv_t)
+            offs = [0]
+            held = [mine]
+            for b in plane_bits:
+                got = lax.ppermute(jnp.stack(held), "chan", pairs_of(n, lambda i, b=b: (i // qc) * qc + ((i % qc) ^ b)))
+                new_offs = [o ^ b for o in offs]
+                pos = q ^ jnp.array(new_offs, jnp.int32)
+                cross = cross_part(got, pos, rcv_t, cross)
+                offs = offs + new_offs
+                held = held + [got[i] for i in range(got.shape[0])]
         traces = jnp.dot(
             cross.reshape(nb * SOURCE * receivers, width), lag_table, preferred_element_type=jnp.float32
         ).reshape(nb, SOURCE, receivers, LAGS)

time: 119 us -> 121 us (1.017)
  Pallas kernels: 25.1 us -> 26.6 us
    pallas_call x3 -> x4, Pallas kernels: 25.1 us -> 26.6 us  [cross_part(): pl.pallas_call(cross_kernel, grid_spec=pltpu.PrefetchScalarGridSpec(num_s...]
    another operation x2 -> x0, other arithmetic: 1.34 us -> none  [shards(): jnp.stack(held)]
    mul x1, other arithmetic: 0.32 us -> 1.55 us  [shards(): rcv_t = jnp.transpose(spectra, (1, 0, 2)).astype(jnp.float32) * window_mask]
    ppermute x2 -> x3, waiting for transfers between devices: 11.2 us -> 10.6 us  [the longest x1 10.6 us: shards(): from_y = lax.ppermute(mine, 'chan', xor_pairs(2))]
  transfers between devices with their start and end apart: 13 -> 14, of which waited for: 10 -> 10; matrix products, arithmetic and copies ran while one was open for 3% -> 4% of each run, Pallas kernels for 11% -> 16%
where the time goes in v8:
time: 121 us
  waiting for transfers between devices  57.6 us (48%)
  Pallas kernels  26.6 us (22%)
  starting transfers between devices  16.5 us (14%)
  other arithmetic  7.73 us (6%)
  matrix products  7.24 us (6%)
  local copies, waits for them, and re-layouts  4.91 us (4%)
    ppermute x2, waiting for transfers between devices, shards(): lax.ppermute(mine, 'chan', pairs_of(n, lambda i, d=d: (i // qc ^ d) * qc...  35.3 us
    pallas_call x4, Pallas kernels, cross_part(): pl.pallas_call(cross_kernel, grid_spec=pltpu.PrefetchScalarGridSpec(num_s...  26.6 us
    ppermute x1, waiting for transfers between devices, shards(): from_y = lax.ppermute(mine, 'chan', xor_pairs(2))  10.6 us
    dot_general x1, matrix products, shards(): jnp.dot(cross.reshape(nb * SOURCE * receivers, width), lag_table, preferr...  7.24 us
    ppermute x3, starting transfers between devices, shards(): lax.ppermute(peak, 'chan', pairs_of(n, lambda i, d=d: (i // qc + d) % zc...  5.07 us
    ppermute x3, waiting for transfers between devices, shards(): lax.ppermute(send, 'chan', pairs_of(n, lambda i, d=d: i // qc * qc + (i %...  5.01 us
    ppermute x2, starting transfers between devices, shards(): lax.ppermute(mine, 'chan', pairs_of(n, lambda i, d=d: (i // qc ^ d) * qc...  4.4 us
    ppermute x3, waiting for transfers between devices, shards(): lax.ppermute(peak, 'chan', pairs_of(n, lambda i, d=d: (i // qc + d) % zc...  3.58 us
  transfers between devices with their start and end apart: 14, of which 10 were waited for; matrix products, arithmetic and copies ran while one was open for 4% of the time, Pallas kernels for 16%

profile of v8, /device:TPU:0, one launch (start us, length us, event | category | flops | bytes accessed | tf_op | source)
XLA Modules:
  0.0 120.7 jit_solution(11862005564249025128)
XLA Ops:
  0.0 1.1 constant_dynamic-slice_fusion
  1.1 0.6 collective-permute-start
  1.7 2.6 %collective-permute-start.1 = (bf16[8,8,1024]{2,1,0:T(8,128)(2,1)S(1)}, bf16[8,8,1024]{2,1,0:T(8,128)(2,1)S(1)}, u32[]{:S(2)}, u32[]{:S(2)}) collective-permute-start(bf16[8,8,1024]{2,1,0:T(8,128)(2,1)S(1)} %get-tuple-element.12), channel_id=1, source_target_pairs={{0,2},{1,3},{2,0},{3,1},{4,6},{5,7},{6,4},{7,5},{8,10},{9,11},{10,... | collective-permute-start | bytes 393224 | tf_op jit(solution)/shard_map/ppermute | solution.py:136
  4.3 0.0 collective-permute-start.2
  4.3 0.8 reshape.141
  5.1 0.8 reshape.139
  5.9 0.0 collective-permute-done
  5.9 2.7 %collective-permute-done.1 = bf16[8,8,1024]{2,1,0:T(8,128)(2,1)S(1)} collective-permute-done((bf16[8,8,1024]{2,1,0:T(8,128)(2,1)S(1)}, bf16[8,8,1024]{2,1,0:T(8,128)(2,1)S(1)}, u32[]{:S(2)}, u32[]{:S(2)}) %collective-permute-start.1) | collective-permute-done | bytes 131104 | tf_op jit(solution)/shard_map/ppermute | solution.py:136
  8.6 2.3 %collective-permute-done.2 = bf16[8,8,1024]{2,1,0:T(8,128)(2,1)S(1)} collective-permute-done((bf16[8,8,1024]{2,1,0:T(8,128)(2,1)S(1)}, bf16[8,8,1024]{2,1,0:T(8,128)(2,1)S(1)}, u32[]{:S(2)}, u32[]{:S(2)}) %collective-permute-start.2) | collective-permute-done | bytes 131104 | tf_op jit(solution)/shard_map/ppermute | solution.py:136
  10.9 0.1 pad_maximum_fusion.1
  11.0 0.6 gather_fusion
  11.6 0.1 select_select_fusion
  11.7 1.6 %collective-permute-start.3 = (bf16[4,8,8,1024]{3,2,1,0:T(8,128)(2,1)S(1)}, bf16[4,8,8,1024]{3,2,1,0:T(8,128)(2,1)S(1)}, u32[]{:S(2)}, u32[]{:S(2)}) collective-permute-start(bf16[4,8,8,1024]{3,2,1,0:T(8,128)(2,1)S(1)} %select_select_fusion), channel_id=1, source_target_pairs={{0,4},{1,5},{2,6},{3,7},{4,0},{5,1},{6,2},{7,3},{8,12},{9,13},{10,... | collective-permute-start | bytes 1572872 | tf_op jit(solution)/shard_map/ppermute | solution.py:149
  13.3 12.5 %collective-permute-done.3 = bf16[4,8,8,1024]{3,2,1,0:T(8,128)(2,1)S(1)} collective-permute-done((bf16[4,8,8,1024]{3,2,1,0:T(8,128)(2,1)S(1)}, bf16[4,8,8,1024]{3,2,1,0:T(8,128)(2,1)S(1)}, u32[]{:S(2)}, u32[]{:S(2)}) %collective-permute-start.3) | collective-permute-done | bytes 524320 | tf_op jit(solution)/shard_map/ppermute | solution.py:149
  25.7 0.1 broadcast_select_fusion
  25.9 2.8 %collective-permute-start.4 = (bf16[4,8,8,1024]{3,2,1,0:T(8,128)(2,1)S(1)}, bf16[4,8,8,1024]{3,2,1,0:T(8,128)(2,1)S(1)}, u32[]{:S(2)}, u32[]{:S(2)}) collective-permute-start(bf16[4,8,8,1024]{3,2,1,0:T(8,128)(2,1)S(1)} %broadcast_select_fusion), channel_id=1, source_target_pairs={{0,8},{1,9},{2,10},{3,11},{4,12},{5,13},{6,14},{7,15},{8,0},{9,1},... | collective-permute-start | bytes 1572872 | tf_op jit(solution)/shard_map/ppermute | solution.py:149
  28.7 22.8 %collective-permute-done.4 = bf16[4,8,8,1024]{3,2,1,0:T(8,128)(2,1)S(1)} collective-permute-done((bf16[4,8,8,1024]{3,2,1,0:T(8,128)(2,1)S(1)}, bf16[4,8,8,1024]{3,2,1,0:T(8,128)(2,1)S(1)}, u32[]{:S(2)}, u32[]{:S(2)}) %collective-permute-start.4) | collective-permute-done | bytes 524320 | tf_op jit(solution)/shard_map/ppermute | solution.py:149
  51.5 0.1 broadcast_select_fusion.1
  51.7 0.0 copy-start
  51.7 1.6 %collective-permute-start.5 = (bf16[4,8,8,1024]{3,2,1,0:T(8,128)(2,1)S(1)}, bf16[4,8,8,1024]{3,2,1,0:T(8,128)(2,1)S(1)}, u32[]{:S(2)}, u32[]{:S(2)}) collective-permute-start(bf16[4,8,8,1024]{3,2,1,0:T(8,128)(2,1)S(1)} %broadcast_select_fusion.1), channel_id=1, source_target_pairs={{0,2},{1,3},{2,0},{3,1},{4,6},{5,7},{6,4},{7,5},{8,10},{9,11},{10,... | collective-permute-start | bytes 1572872 | tf_op jit(solution)/shard_map/ppermute | solution.py:179
  53.3 0.7 convert_element_type.11
  54.0 0.0 collective-permute-start.7
  54.0 10.6 %collective-permute-done.5 = bf16[4,8,8,1024]{3,2,1,0:T(8,128)(2,1)S(1)} collective-permute-done((bf16[4,8,8,1024]{3,2,1,0:T(8,128)(2,1)S(1)}, bf16[4,8,8,1024]{3,2,1,0:T(8,128)(2,1)S(1)}, u32[]{:S(2)}, u32[]{:S(2)}) %collective-permute-start.5) | collective-permute-done | bytes 524320 | tf_op jit(solution)/shard_map/ppermute | solution.py:179
  64.5 0.0 copy-start.1
  64.5 0.0 collective-permute-start.6
  64.5 1.5 %multiply_bitcast_fusion = f32[8,32,1024]{2,1,0:T(8,128)S(1)} fusion(bf16[32,8,1024]{2,1,0:T(8,128)(2,1)} %param.4, f32[8]{0:T(128)S(1)} %convert_element_type.11), kind=kLoop, calls=%fused_computation.4 | loop fusion | flops 524288 | bytes 1572896 | tf_op jit(solution)/shard_map/mul | solution.py:171
  66.1 0.2 slice_bitcast_fusion
  66.3 1.3 %pad_maximum_fusion.rcv_ref = f32[3,8,32,512]{3,2,1,0:T(8,128)} fusion(f32[1,8,32,512]{3,2,1,0:T(8,128)S(1)} %get-tuple-element.8, f32[1,8,32,512]{3,2,1,0:T(8,128)S(1)} %get-tuple-element.9, f32[1,8,32,512]{3,2,1,0:T(8,128)S(1)} %get-tuple-element.7), kind=kLoop, calls=%fused_computation.3 | loop fusion | flops 786432 | bytes 3145728 | tf_op jit(solution)/shard_map/stack | solution.py:173
  67.6 0.0 copy-done
  67.6 6.6 %shard_map.46.rest_0_ = bf16[4,32,32,1024]{3,2,1,0:T(8,128)(2,1)} custom-call(s32[1]{0:T(128)} %bitcast.18.pos_ref, bf16[1,4,8,8,1024]{4,3,2,1,0:T(8,128)(2,1)} %bitcast.35, f32[3,8,32,512]{3,2,1,0:T(8,128)} %pad_maximum_fusion.rcv_ref), custom_call_target="tpu_custom_call" | custom-call | flops 25165824 | bytes 4194304 | tf_op jit(solution)/shard_map/pallas_call | solution.py:75
  74.2 0.0 copy-done.1
  74.2 0.0 collective-permute-done.7
  74.2 0.0 copy-start.3
  74.2 0.8 copy-done.3
  75.1 6.6 %shard_map.47.rest_0_ = bf16[4,32,32,1024]{3,2,1,0:T(8,128)(2,1)} custom-call(s32[1]{0:T(128)} %bitcast.16.pos_ref, bf16[1,4,8,8,1024]{4,3,2,1,0:T(8,128)(2,1)} %bitcast.38, f32[3,8,32,512]{3,2,1,0:T(8,128)} %pad_maximum_fusion.rcv_ref, bf16[4,32,32,1024]{3,2,1,0:T(8,128)(2,1)} %shard_map.46.rest_0_), custom_call_target="tpu_custom_call", output_to_operand_aliasing={{}: (3, {})} | custom-call | flops 25165824 | bytes 4194304 | tf_op jit(solution)/shard_map/pallas_call | solution.py:75
  81.7 6.6 %shard_map.48.rest_0_ = bf16[4,32,32,1024]{3,2,1,0:T(8,128)(2,1)} custom-call(s32[1]{0:T(128)} %bitcast.14.pos_ref, bf16[1,4,8,8,1024]{4,3,2,1,0:T(8,128)(2,1)} %bitcast.36, f32[3,8,32,512]{3,2,1,0:T(8,128)} %pad_maximum_fusion.rcv_ref, bf16[4,32,32,1024]{3,2,1,0:T(8,128)(2,1)} %shard_map.47.rest_0_), custom_call_target="tpu_custom_call", output_to_operand_aliasing={{}: (3, {})} | custom-call | flops 25165824 | bytes 4194304 | tf_op jit(solution)/shard_map/pallas_call | solution.py:75
  88.3 0.0 collective-permute-done.6
  88.3 0.0 copy-start.2
  88.3 0.8 copy-done.2
  89.2 0.0 copy-start.4
  89.2 6.7 %shard_map.49 = bf16[4,32,32,1024]{3,2,1,0:T(8,128)(2,1)} custom-call(s32[1]{0:T(128)} %bitcast.pos_ref, bf16[1,4,8,8,1024]{4,3,2,1,0:T(8,128)(2,1)} %bitcast.37, f32[3,8,32,512]{3,2,1,0:T(8,128)} %pad_maximum_fusion.rcv_ref, bf16[4,32,32,1024]{3,2,1,0:T(8,128)(2,1)} %shard_map.48.rest_0_), custom_call_target="tpu_custom_call", output_to_operand_aliasing={{}: (3, {})} | custom-call | flops 25165824 | bytes 4194304 | tf_op jit(solution)/shard_map/pallas_call | solution.py:75
  95.9 0.0 copy-done.4
  95.9 7.2 %abs_reduce_fusion = (f32[4,32]{1,0:T(4,128)S(1)}, f32[4,32,32,512]{3,2,1,0:T(8,128)S(1)}) fusion(bf16[4,32,32,1024]{3,2,1,0:T(8,128)(2,1)} %shard_map.49, bf16[1024,512,1,1]{1,0,3,2:T(8,128)(2,1)S(1)} %copy-done.4), kind=kOutput, calls=%fused_computation.2 | convolution fusion | flops 4299161600 | bytes 17826304 | tf_op jit(solution)/shard_map/dot_general | solution.py:197
  103.2 1.6 %collective-permute-start.10 = (f32[4,32]{1,0:T(4,128)S(1)}, f32[4,32]{1,0:T(4,128)S(1)}, u32[]{:S(2)}, u32[]{:S(2)}) collective-permute-start(f32[4,32]{1,0:T(4,128)S(1)} %get-tuple-element.17), channel_id=1, source_target_pairs={{0,3},{1,2},{2,1},{3,0},{4,7},{5,6},{6,5},{7,4},{8,11},{9,10},{10,... | collective-permute-start | bytes 1544 | tf_op jit(solution)/shard_map/ppermute | solution.py:202
  104.8 0.2 collective-permute-start.8
  105.0 0.4 collective-permute-start.9
  105.4 0.9 collective-permute-done.10
  106.2 0.0 collective-permute-done.8
  106.2 2.3 %collective-permute-done.9 = f32[4,32]{1,0:T(4,128)S(1)} collective-permute-done((f32[4,32]{1,0:T(4,128)S(1)}, f32[4,32]{1,0:T(4,128)S(1)}, u32[]{:S(2)}, u32[]{:S(2)}) %collective-permute-start.9) | collective-permute-done | bytes 544 | tf_op jit(solution)/shard_map/ppermute | solution.py:202
  108.5 1.7 %collective-permute-start.11 = (f32[4,32]{1,0:T(4,128)S(1)}, f32[4,32]{1,0:T(4,128)S(1)}, u32[]{:S(2)}, u32[]{:S(2)}) collective-permute-start(f32[4,32]{1,0:T(4,128)S(1)} %maximum_maximum_fusion), channel_id=1, source_target_pairs={{0,4},{1,5},{2,6},{3,7},{4,8},{5,9},{6,10},{7,11},{8,12},{9,13},{1... | collective-permute-start | bytes 1544 | tf_op jit(solution)/shard_map/ppermute | solution.py:208
  110.2 3.4 %collective-permute-start.12 = (f32[4,32]{1,0:T(4,128)S(1)}, f32[4,32]{1,0:T(4,128)S(1)}, u32[]{:S(2)}, u32[]{:S(2)}) collective-permute-start(f32[4,32]{1,0:T(4,128)S(1)} %maximum_maximum_fusion), channel_id=1, source_target_pairs={{0,8},{1,9},{2,10},{3,11},{4,12},{5,13},{6,14},{7,15},{8,0},{9,1},... | collective-permute-start | bytes 1544 | tf_op jit(solution)/shard_map/ppermute | solution.py:208
  113.6 0.0 collective-permute-start.13
  113.6 1.0 collective-permute-done.11
  114.6 0.6 collective-permute-done.12
  115.2 2.0 %collective-permute-done.13 = f32[4,32]{1,0:T(4,128)S(1)} collective-permute-done((f32[4,32]{1,0:T(4,128)S(1)}, f32[4,32]{1,0:T(4,128)S(1)}, u32[]{:S(2)}, u32[]{:S(2)}) %collective-permute-start.13) | collective-permute-done | bytes 544 | tf_op jit(solution)/shard_map/ppermute | solution.py:208
  117.2 3.5 %divide_convert_fusion = bf16[4,32,32,512]{3,2,1,0:T(8,128)(2,1)} fusion(f32[4,32,32,512]{3,2,1,0:T(8,128)S(1)} %get-tuple-element.18, f32[4,32]{1,0:T(4,128)S(1)} %maximum_add_fusion), kind=kLoop, calls=%fused_computation.1 | loop fusion | flops 4194304 | bytes 12583424 | tf_op jit(solution)/shard_map/convert_element_type | solution.py:213
  (6 shorter events, 0.1 us)
Async XLA Ops:
  1.1 4.8 %collective-permute-start = (bf16[8,8,1024]{2,1,0:T(8,128)(2,1)S(1)}, bf16[8,8,1024]{2,1,0:T(8,128)(2,1)S(1)}, u32[]{:S(2)}, u32[]{:S(2)}) collective-permute-start(bf16[8,8,1024]{2,1,0:T(8,128)(2,1)S(1)} %get-tuple-element.13), channel_id=1, source_target_pairs={{0,1},{1,0},{2,3},{3,2},{4,5},{5,4},{6,7},{7,6},{8,9},{9,8},{10,11... | collective-permute-start | bytes 393224 | tf_op jit(solution)/shard_map/ppermute | solution.py:136
  1.7 6.9 %collective-permute-start.1 = (bf16[8,8,1024]{2,1,0:T(8,128)(2,1)S(1)}, bf16[8,8,1024]{2,1,0:T(8,128)(2,1)S(1)}, u32[]{:S(2)}, u32[]{:S(2)}) collective-permute-start(bf16[8,8,1024]{2,1,0:T(8,128)(2,1)S(1)} %get-tuple-element.12), channel_id=1, source_target_pairs={{0,2},{1,3},{2,0},{3,1},{4,6},{5,7},{6,4},{7,5},{8,10},{9,11},{10,... | collective-permute-start | bytes 393224 | tf_op jit(solution)/shard_map/ppermute | solution.py:136
  4.3 6.6 %collective-permute-start.2 = (bf16[8,8,1024]{2,1,0:T(8,128)(2,1)S(1)}, bf16[8,8,1024]{2,1,0:T(8,128)(2,1)S(1)}, u32[]{:S(2)}, u32[]{:S(2)}) collective-permute-start(bf16[8,8,1024]{2,1,0:T(8,128)(2,1)S(1)} %get-tuple-element.11), channel_id=1, source_target_pairs={{0,3},{1,2},{2,1},{3,0},{4,7},{5,6},{6,5},{7,4},{8,11},{9,10},{10,... | collective-permute-start | bytes 393224 | tf_op jit(solution)/shard_map/ppermute | solution.py:136
  11.7 14.0 %collective-permute-start.3 = (bf16[4,8,8,1024]{3,2,1,0:T(8,128)(2,1)S(1)}, bf16[4,8,8,1024]{3,2,1,0:T(8,128)(2,1)S(1)}, u32[]{:S(2)}, u32[]{:S(2)}) collective-permute-start(bf16[4,8,8,1024]{3,2,1,0:T(8,128)(2,1)S(1)} %select_select_fusion), channel_id=1, source_target_pairs={{0,4},{1,5},{2,6},{3,7},{4,0},{5,1},{6,2},{7,3},{8,12},{9,13},{10,... | collective-permute-start | bytes 1572872 | tf_op jit(solution)/shard_map/ppermute | solution.py:149
  25.9 25.6 %collective-permute-start.4 = (bf16[4,8,8,1024]{3,2,1,0:T(8,128)(2,1)S(1)}, bf16[4,8,8,1024]{3,2,1,0:T(8,128)(2,1)S(1)}, u32[]{:S(2)}, u32[]{:S(2)}) collective-permute-start(bf16[4,8,8,1024]{3,2,1,0:T(8,128)(2,1)S(1)} %broadcast_select_fusion), channel_id=1, source_target_pairs={{0,8},{1,9},{2,10},{3,11},{4,12},{5,13},{6,14},{7,15},{8,0},{9,1},... | collective-permute-start | bytes 1572872 | tf_op jit(solution)/shard_map/ppermute | solution.py:149
  51.7 16.0 %copy-start = (bf16[4,8,8,1024]{3,2,1,0:T(8,128)(2,1)}, bf16[4,8,8,1024]{3,2,1,0:T(8,128)(2,1)S(1)}, u32[]{:S(2)}) copy-start(bf16[4,8,8,1024]{3,2,1,0:T(8,128)(2,1)S(1)} %broadcast_select_fusion.1) | copy-start | bytes 1572868
  51.7 12.8 %collective-permute-start.5 = (bf16[4,8,8,1024]{3,2,1,0:T(8,128)(2,1)S(1)}, bf16[4,8,8,1024]{3,2,1,0:T(8,128)(2,1)S(1)}, u32[]{:S(2)}, u32[]{:S(2)}) collective-permute-start(bf16[4,8,8,1024]{3,2,1,0:T(8,128)(2,1)S(1)} %broadcast_select_fusion.1), channel_id=1, source_target_pairs={{0,2},{1,3},{2,0},{3,1},{4,6},{5,7},{6,4},{7,5},{8,10},{9,11},{10,... | collective-permute-start | bytes 1572872 | tf_op jit(solution)/shard_map/ppermute | solution.py:179
  54.0 20.3 %collective-permute-start.7 = (bf16[4,8,8,1024]{3,2,1,0:T(8,128)(2,1)S(1)}, bf16[4,8,8,1024]{3,2,1,0:T(8,128)(2,1)S(1)}, u32[]{:S(2)}, u32[]{:S(2)}) collective-permute-start(bf16[4,8,8,1024]{3,2,1,0:T(8,128)(2,1)S(1)} %broadcast_select_fusion.1), channel_id=1, source_target_pairs={{0,1},{1,0},{2,3},{3,2},{4,5},{5,4},{6,7},{7,6},{8,9},{9,8},{10,11... | collective-permute-start | bytes 1572872 | tf_op jit(solution)/shard_map/ppermute | solution.py:180
  64.5 9.7 %copy-start.1 = (bf16[4,8,8,1024]{3,2,1,0:T(8,128)(2,1)}, bf16[4,8,8,1024]{3,2,1,0:T(8,128)(2,1)S(1)}, u32[]{:S(2)}) copy-start(bf16[4,8,8,1024]{3,2,1,0:T(8,128)(2,1)S(1)} %collective-permute-done.5) | copy-start | bytes 1572868
  64.5 23.8 %collective-permute-start.6 = (bf16[4,8,8,1024]{3,2,1,0:T(8,128)(2,1)S(1)}, bf16[4,8,8,1024]{3,2,1,0:T(8,128)(2,1)S(1)}, u32[]{:S(2)}, u32[]{:S(2)}) collective-permute-start(bf16[4,8,8,1024]{3,2,1,0:T(8,128)(2,1)S(1)} %collective-permute-done.5), channel_id=1, source_target_pairs={{0,1},{1,0},{2,3},{3,2},{4,5},{5,4},{6,7},{7,6},{8,9},{9,8},{10,11... | collective-permute-start | bytes 1572872 | tf_op jit(solution)/shard_map/ppermute | solution.py:183
  74.2 0.8 copy-start.3
  88.3 0.9 copy-start.2
  89.2 6.7 %copy-start.4 = (bf16[1024,512,1,1]{1,0,3,2:T(8,128)(2,1)S(1)}, bf16[1024,512,1,1]{1,0,3,2:T(8,128)(2,1)}, u32[]{:S(2)}) copy-start(bf16[1024,512,1,1]{1,0,3,2:T(8,128)(2,1)} %constant.87) | copy-start | bytes 3145732
  103.2 3.1 %collective-permute-start.10 = (f32[4,32]{1,0:T(4,128)S(1)}, f32[4,32]{1,0:T(4,128)S(1)}, u32[]{:S(2)}, u32[]{:S(2)}) collective-permute-start(f32[4,32]{1,0:T(4,128)S(1)} %get-tuple-element.17), channel_id=1, source_target_pairs={{0,3},{1,2},{2,1},{3,0},{4,7},{5,6},{6,5},{7,4},{8,11},{9,10},{10,... | collective-permute-start | bytes 1544 | tf_op jit(solution)/shard_map/ppermute | solution.py:202
  104.8 1.5 %collective-permute-start.8 = (f32[4,32]{1,0:T(4,128)S(1)}, f32[4,32]{1,0:T(4,128)S(1)}, u32[]{:S(2)}, u32[]{:S(2)}) collective-permute-start(f32[4,32]{1,0:T(4,128)S(1)} %get-tuple-element.17), channel_id=1, source_target_pairs={{0,1},{1,0},{2,3},{3,2},{4,5},{5,4},{6,7},{7,6},{8,9},{9,8},{10,11... | collective-permute-start | bytes 1544 | tf_op jit(solution)/shard_map/ppermute | solution.py:202
  105.0 3.6 %collective-permute-start.9 = (f32[4,32]{1,0:T(4,128)S(1)}, f32[4,32]{1,0:T(4,128)S(1)}, u32[]{:S(2)}, u32[]{:S(2)}) collective-permute-start(f32[4,32]{1,0:T(4,128)S(1)} %get-tuple-element.17), channel_id=1, source_target_pairs={{0,2},{1,3},{2,0},{3,1},{4,6},{5,7},{6,4},{7,5},{8,10},{9,11},{10,... | collective-permute-start | bytes 1544 | tf_op jit(solution)/shard_map/ppermute | solution.py:202
  108.5 6.1 %collective-permute-start.11 = (f32[4,32]{1,0:T(4,128)S(1)}, f32[4,32]{1,0:T(4,128)S(1)}, u32[]{:S(2)}, u32[]{:S(2)}) collective-permute-start(f32[4,32]{1,0:T(4,128)S(1)} %maximum_maximum_fusion), channel_id=1, source_target_pairs={{0,4},{1,5},{2,6},{3,7},{4,8},{5,9},{6,10},{7,11},{8,12},{9,13},{1... | collective-permute-start | bytes 1544 | tf_op jit(solution)/shard_map/ppermute | solution.py:208
  110.2 4.9 %collective-permute-start.12 = (f32[4,32]{1,0:T(4,128)S(1)}, f32[4,32]{1,0:T(4,128)S(1)}, u32[]{:S(2)}, u32[]{:S(2)}) collective-permute-start(f32[4,32]{1,0:T(4,128)S(1)} %maximum_maximum_fusion), channel_id=1, source_target_pairs={{0,8},{1,9},{2,10},{3,11},{4,12},{5,13},{6,14},{7,15},{8,0},{9,1},... | collective-permute-start | bytes 1544 | tf_op jit(solution)/shard_map/ppermute | solution.py:208
  113.6 3.6 %collective-permute-start.13 = (f32[4,32]{1,0:T(4,128)S(1)}, f32[4,32]{1,0:T(4,128)S(1)}, u32[]{:S(2)}, u32[]{:S(2)}) collective-permute-start(f32[4,32]{1,0:T(4,128)S(1)} %maximum_maximum_fusion), channel_id=1, source_target_pairs={{0,12},{1,13},{2,14},{3,15},{4,0},{5,1},{6,2},{7,3},{8,4},{9,5},{1... | collective-permute-start | bytes 1544 | tf_op jit(solution)/shard_map/ppermute | solution.py:208
